TPU v7x, 128 devices: a whole 4x4x4 slice. The times are simulated.
128 devices in a mesh: dp: 4 (over y), exp: 32 (over z, x, core).
Axes of the slice: x: 4, y: 4, z: 4, core: 2. Of those that a mesh axis runs over, the one named last changes fastest.
Arguments:
- hidden: bfloat16 [16384, 2048], P(('dp', 'exp')), may hold values from -6 to 6
- queries: bfloat16 [16384, 2048], P(('dp', 'exp')), may hold values from -1000 to 1000
- draft_entries: bfloat16 [2, 16384, 512], P(None, ('dp', 'exp')), may hold values from -6 to 6
- key_pool: bfloat16 [1024, 64, 512], P(('dp', 'exp')), may hold values from -8 to 8
- value_pool: bfloat16 [1024, 64, 512], P(('dp', 'exp')), may hold values from -6 to 6
- page_table: int32 [256, 4], P(('dp', 'exp')), may hold values from 0 to 31, as said below
- cache_len: int32 [256], P(('dp', 'exp')), may hold values from 2 to 256, as said below
- parents: int32 [256, 64], P(('dp', 'exp')), may hold values from -1 to 62, as said below
- out_proj: bfloat16 [2048, 2048], replicated, may hold values from -0.125 to 0.125
- norm_gain: bfloat16 [2048], replicated, may hold values from 0.099609375 to 1.8984375
- expert_gate: bfloat16 [64, 1408, 2048], P('exp', 'dp'), may hold values from -0.125 to 0.125
- expert_up: bfloat16 [64, 1408, 2048], P('exp', 'dp'), may hold values from -0.125 to 0.125
- expert_down: bfloat16 [64, 1408, 2048], P('exp', 'dp'), may hold values from -0.15625 to 0.15625
- shared_gate: bfloat16 [1408, 2048], P('dp'), may hold values from -0.125 to 0.125
- shared_up: bfloat16 [1408, 2048], P('dp'), may hold values from -0.125 to 0.125
- shared_down: bfloat16 [1408, 2048], P('dp'), may hold values from -0.15625 to 0.15625
- expert_ids: int32 [16384, 6], P(('dp', 'exp')), may hold values from 0 to 63, all different within a row; in each aligned block of 128 rows (0 to 127, 128 to 255, ...) at most 16 rows name the same one
- expert_weights: float32 [16384, 6], P(('dp', 'exp')), may hold values from 0.05 to 0.5
Outputs:
- verified: bfloat16 [16384, 2048], P(('dp', 'exp'))
Inputs may be any that keep to these rules, and one draw needn't show every extreme that they name: `page_table`: page ids count within the 4 devices that share the request's index of exp: page q lies on the one of dp index q // 8, as its page q % 8; the requests of those devices together use each of their 32 pages exactly once. `cache_len`: some request has exactly 256 cached positions. parents[r, i] is -1 or an earlier node i' < i of the same request; parents[r, 0] = -1. `expert_ids`: each row names 6 different experts; the 128 rows of one device name one expert at most 16 times, a bound that some block reaches.
All inputs are finite; a program needn't handle non-finite values.
Results may differ from a plain program's by a relative error of at most 0.015.
Values may be sent and summed in bfloat16 or wider, within the bound.
No kernel may reach another device: no remote copies, remote signals or barrier semaphores. Data moves between devices by JAX's collectives and lax.ppermute only.
A program may use at most 192 MiB of HBM per device.

v0:
```python
import jax
import jax.numpy as jnp
from jax import lax
from jax.sharding import PartitionSpec as P

HEADS = 16
KVH = 4
HD = 128
CAP = 16


NEG_FILL = -1e30
NORM_EPSILON = 1e-06
HIGHEST_PRECISION = lax.Precision.HIGHEST


def tree_reach(parents):
    node_count = parents.shape[-1]
    node_index = jnp.arange(node_count, dtype=jnp.int32)
    linked = (parents[:, :, None] == node_index[None, None, :]).astype(jnp.float32)
    reached = jnp.minimum(linked + jnp.eye(node_count, dtype=jnp.float32)[None], 1.0)
    for rounds in range(max(1, (node_count - 1).bit_length())):
        reached = jnp.minimum(
            jnp.einsum("rij,rjk->rik", reached, reached, precision=HIGHEST_PRECISION), 1.0
        )
    return reached


def score_block(query_heads, key_rows, live_mask):
    raw_scores = jnp.einsum(
        "rtgnd,rcgd->rgntc", query_heads, key_rows, preferred_element_type=jnp.float32
    ) * key_rows.shape[-1] ** (-0.5)
    wide_mask = live_mask[:, None, None]
    return (jnp.where(wide_mask, raw_scores, NEG_FILL), wide_mask)


def fold_keys(carry_state, scores, wide_mask, value_rows):
    running_top, running_total, running_sum = carry_state
    fresh_top = jnp.maximum(running_top, jnp.max(scores, axis=-1))
    rescale = jnp.exp(running_top - fresh_top)
    exponents = jnp.where(wide_mask, jnp.exp(scores - fresh_top[..., None]), 0.0)
    weights = exponents.astype(jnp.bfloat16)
    new_total = running_total * rescale + jnp.sum(exponents, axis=-1)
    mixed = jnp.einsum("rgntc,rcgd->rtgnd", weights, value_rows, preferred_element_type=jnp.float32)
    new_sum = running_sum * jnp.transpose(rescale, (0, 3, 1, 2))[..., None] + mixed
    return (fresh_top, new_total, new_sum)


def pool_state(carry_state, query_heads, table_rows, lengths, pieces):
    piece_keys, piece_values = pieces
    piece_count = piece_keys.shape[0]
    request_count, pages_per = table_rows.shape
    page_size = piece_keys.shape[1]
    key_heads = query_heads.shape[2]
    inside = (table_rows >= 0) & (table_rows < piece_count)
    picked = jnp.clip(table_rows, 0, piece_count - 1)
    cache_keys = piece_keys[picked].reshape(request_count, pages_per * page_size, key_heads, -1)
    cache_values = piece_values[picked].reshape(request_count, pages_per * page_size, key_heads, -1)
    positions = jnp.arange(pages_per * page_size, dtype=jnp.int32)
    usable = jnp.repeat(inside, page_size, axis=1) & (positions[None, :] < lengths[:, None])
    live_mask = jnp.broadcast_to(
        usable[:, None, :], (request_count, query_heads.shape[1], pages_per * page_size)
    )
    scores, wide_mask = score_block(query_heads, cache_keys, live_mask)
    return fold_keys(carry_state, scores, wide_mask, cache_values)


def blank_state(request_count, draft_nodes, key_heads, group_size, head_size):
    return (
        jnp.full((request_count, key_heads, group_size, draft_nodes), NEG_FILL, jnp.float32),
        jnp.zeros((request_count, key_heads, group_size, draft_nodes), jnp.float32),
        jnp.zeros((request_count, draft_nodes, key_heads, group_size, head_size), jnp.float32),
    )


def expert_block(grouped, gate_rows, upper_rows, down_rows):
    gate_values = jnp.einsum(
        "sekd,efd->sekf", grouped, gate_rows, preferred_element_type=jnp.float32
    )
    upper_values = jnp.einsum(
        "sekd,efd->sekf", grouped, upper_rows, preferred_element_type=jnp.float32
    )
    inner = (jax.nn.silu(gate_values) * upper_values).astype(jnp.bfloat16)
    return jnp.einsum("sekf,efd->sekd", inner, down_rows, preferred_element_type=jnp.float32)


def shared_block(tokens, gate_rows, upper_rows, down_rows):
    gate_values = jnp.einsum("td,fd->tf", tokens, gate_rows, preferred_element_type=jnp.float32)
    upper_values = jnp.einsum("td,fd->tf", tokens, upper_rows, preferred_element_type=jnp.float32)
    inner = (jax.nn.silu(gate_values) * upper_values).astype(jnp.bfloat16)
    return jnp.dot(inner, down_rows, preferred_element_type=jnp.float32)


def on_device(
    hidden,
    queries,
    draft_entries,
    key_pool,
    value_pool,
    page_table,
    cache_len,
    parents,
    out_proj,
    norm_gain,
    expert_gate,
    expert_up,
    expert_down,
    shared_gate,
    shared_up,
    shared_down,
    expert_ids,
    expert_weights,
):
    tok_rows, model_width = hidden.shape
    local_requests, draft_nodes = parents.shape
    group_size = HEADS // KVH
    query_heads = queries.reshape(local_requests, draft_nodes, KVH, group_size, HD)
    draft_keys = draft_entries[0].reshape(local_requests, draft_nodes, KVH, HD)
    draft_values = draft_entries[1].reshape(local_requests, draft_nodes, KVH, HD)
    reached = tree_reach(parents)
    tree_scores, tree_mask = score_block(query_heads, draft_keys, reached > 0.5)
    tree_state = fold_keys(
        blank_state(local_requests, draft_nodes, KVH, group_size, HD),
        tree_scores,
        tree_mask,
        draft_values,
    )
    final_top, final_total, final_sum = pool_state(
        tree_state,
        query_heads,
        page_table,
        cache_len,
        (
            lax.all_gather(key_pool, "dp", axis=0, tiled=True),
            lax.all_gather(value_pool, "dp", axis=0, tiled=True),
        ),
    )
    attention = (
        (final_sum / jnp.transpose(final_total, (0, 3, 1, 2))[..., None])
        .reshape(tok_rows, queries.shape[1])
        .astype(jnp.bfloat16)
    )
    residual = (
        hidden.astype(jnp.float32)
        + jnp.dot(attention, out_proj, preferred_element_type=jnp.float32)
    ).astype(jnp.bfloat16)
    residual_wide = residual.astype(jnp.float32)
    scale_rows = lax.rsqrt(
        jnp.mean(residual_wide * residual_wide, axis=-1, keepdims=True) + NORM_EPSILON
    )
    normed = (residual_wide * scale_rows * norm_gain.astype(jnp.float32)).astype(jnp.bfloat16)
    local_experts = expert_gate.shape[0]
    column_count = lax.axis_size("exp")
    expert_count = local_experts * column_count
    pick_count = expert_ids.shape[1]
    flat_experts = expert_ids.reshape(-1)
    onehot = (flat_experts[:, None] == jnp.arange(expert_count, dtype=jnp.int32)[None, :]).astype(
        jnp.int32
    )
    slot_ids = jnp.sum((jnp.cumsum(onehot, axis=0) - 1) * onehot, axis=1)
    destinations = flat_experts * CAP + slot_ids
    token_rows = jnp.arange(tok_rows * pick_count, dtype=jnp.int32) // pick_count
    outgoing = (
        jnp.zeros((expert_count * CAP, model_width), jnp.bfloat16)
        .at[destinations]
        .set(normed[token_rows])
    )
    outgoing = outgoing.reshape(column_count, local_experts, CAP, model_width)
    arrived = lax.all_to_all(outgoing, "exp", split_axis=0, concat_axis=0, tiled=True)
    grouped, group_tokens = (
        lax.all_gather(arrived, "dp", axis=0, tiled=True),
        lax.all_gather(normed, "dp", axis=0, tiled=True),
    )
    routed_terms = expert_block(grouped, expert_gate, expert_up, expert_down)
    shared_terms = shared_block(group_tokens, shared_gate, shared_up, shared_down)
    routed_sum, shared_sum = (
        lax.psum_scatter(
            routed_terms.astype(jnp.bfloat16), "dp", scatter_dimension=0, tiled=True
        ).astype(jnp.float32),
        lax.psum_scatter(
            shared_terms.astype(jnp.bfloat16), "dp", scatter_dimension=0, tiled=True
        ).astype(jnp.float32),
    )
    returned = lax.all_to_all(
        routed_sum.astype(jnp.bfloat16), "exp", split_axis=0, concat_axis=0, tiled=True
    )
    returned_rows = returned.reshape(expert_count * CAP, model_width)
    picked_rows = (
        returned_rows[destinations].astype(jnp.float32).reshape(tok_rows, pick_count, model_width)
    )
    routed_out = jnp.sum(picked_rows * expert_weights[:, :, None], axis=1)
    return (residual.astype(jnp.float32) + routed_out + shared_sum).astype(jnp.bfloat16)


def solution(mesh):
    placed = (
        P(("dp", "exp"), None),
        P(("dp", "exp"), None),
        P(None, ("dp", "exp"), None),
        P(("dp", "exp"), None, None),
        P(("dp", "exp"), None, None),
        P(("dp", "exp"), None),
        P(("dp", "exp")),
        P(("dp", "exp"), None),
        P(),
        P(),
        P("exp", "dp", None),
        P("exp", "dp", None),
        P("exp", "dp", None),
        P("dp", None),
        P("dp", None),
        P("dp", None),
        P(("dp", "exp"), None),
        P(("dp", "exp"), None),
    )
    return jax.shard_map(
        on_device, mesh=mesh, in_specs=placed, out_specs=P(("dp", "exp"), None), check_vma=False
    )
```

profile of v0, /device:TPU:0, one launch (start us, length us, event | category | flops | bytes accessed | tf_op | source)
XLA Modules:
  0.0 618.6 jit_solution(10467240075292490919)
XLA Ops:
  13.0 1.4 reshape.147
  16.6 1.6 fusion.76
  18.2 1.6 reshape_squeeze.6
  21.2 1.4 fusion.52
  22.6 4.4 reduce-window.6
  32.2 2.5 fusion.77
  34.7 7.6 %all-gather.5.cloned.1.call-done = bf16[32,64,512]{2,1,0:T(8,128)(2,1)} async-done(((bf16[8,64,512]{2,1,0:T(8,128)(2,1)}), bf16[32,64,512]{2,1,0:T(8,128)(2,1)}) %all-gather.5.cloned.1.call-update) | async-done | bytes 2097168 | tf_op jit(solution)/shard_map/all_gather | solution.py:134
  42.3 2.2 gather_fusion
  45.4 29.4 %all-gather.7.cloned.1.call-done = bf16[32,64,512]{2,1,0:T(8,128)(2,1)} async-done(((bf16[8,64,512]{2,1,0:T(8,128)(2,1)}), bf16[32,64,512]{2,1,0:T(8,128)(2,1)}) %all-gather.7.cloned.1.call-update) | async-done | bytes 2097168 | tf_op jit(solution)/shard_map/all_gather | solution.py:135
  74.8 2.2 gather_fusion.1
  77.9 1.8 bitcast_reduce_fusion
  81.8 1.2 fusion.23
  83.1 1.2 copy.50
  84.3 1.4 convert_element_type.79
  85.7 4.8 multiply_reduce_fusion.1
  91.7 23.5 %scatter_custom_fusion = bf16[1024,2048]{1,0:T(8,128)(2,1)} fusion(s32[768]{0:T(1024)S(1)} %fusion.66, bf16[128,2048]{1,0:T(8,128)(2,1)S(1)} %multiply_convert_fusion, s32[1024]{0:T(1024)} %pad_clamp_fusion.1, bf16[]{:T(256)} %constant.12.clone.1), kind=kCustom, calls=%fused_computation.14 | custom fusion | bytes 4194816 | tf_op jit(solution)/shard_map/scatter | solution.py:166
  115.2 58.1 %all_to_all.10 = bf16[32,2,16,2048]{3,2,1,0:T(8,128)(2,1)S(1)} all-to-all(bf16[32,2,16,2048]{3,2,1,0:T(8,128)(2,1)} %bitcast.127), channel_id=1, replica_groups=mesh['dp'=4,'exp'=32] {'exp'}, dimensions={0} | all-to-all | bytes 8388608 | tf_op jit(solution)/shard_map/all_to_all | solution.py:169
  173.3 4.2 copy.55
  178.2 150.0 %all-gather.9.cloned.1.call-done = bf16[128,2,16,2048]{3,0,2,1:T(8,128)(2,1)} async-done(((bf16[32,2,16,2048]{3,0,2,1:T(8,128)(2,1)}), bf16[128,2,16,2048]{3,0,2,1:T(8,128)(2,1)}) %all-gather.9.cloned.1.call-update) | async-done | bytes 16777232 | tf_op jit(solution)/shard_map/all_gather | solution.py:171
  328.2 12.3 %fusion.7 = f32[2,128,16,352]{1,3,2,0:T(8,128)} fusion(bf16[128,2,16,2048]{3,0,2,1:T(8,128)(2,1)} %all-gather.9.cloned.1.call-done, bf16[2,352,2048]{2,1,0:T(8,128)(2,1)} %param.29), kind=kOutput, calls=%fused_computation.18 | convolution fusion | flops 5905580032 | bytes 25427968 | tf_op jit(solution)/shard_map/sekd,efd->sekf/dot_general | solution.py:80
  340.5 12.7 %fusion = bf16[128,2,16,352]{0,3,2,1:T(8,128)(2,1)} fusion(f32[2,128,16,352]{1,3,2,0:T(8,128)} %fusion.7, bf16[128,2,16,2048]{3,0,2,1:T(8,128)(2,1)} %all-gather.9.cloned.1.call-done, bf16[2,352,2048]{2,1,0:T(8,128)(2,1)S(1)} %copy-done.8), kind=kOutput, calls=%fused_computation.8 | convolution fusion | flops 5914230784 | bytes 28311552 | tf_op jit(solution)/shard_map/sekd,efd->sekf/dot_general | solution.py:77
  353.2 14.4 %convert_bitcast_fusion = bf16[128,2,16,2048]{3,0,2,1:T(8,128)(2,1)} fusion(bf16[128,2,16,352]{0,3,2,1:T(8,128)(2,1)} %fusion, bf16[2,352,2048]{2,1,0:T(8,128)(2,1)S(1)} %copy-done), kind=kOutput, calls=%fused_computation.5 | convolution fusion | flops 5913968640 | bytes 22544384 | tf_op jit(solution)/shard_map/sekf,efd->sekd/dot_general | solution.py:84
  367.7 3.8 fusion.78
  371.5 145.3 %reduce-scatter.3.cloned.1.call-done = bf16[32,2,16,2048]{3,0,2,1:T(8,128)(2,1)} async-done(((bf16[128,2,16,2048]{3,0,2,1:T(8,128)(2,1)}), bf16[32,2,16,2048]{3,0,2,1:T(8,128)(2,1)}) %reduce-scatter.3.cloned.1.call-update) | async-done | bytes 4194320 | tf_op jit(solution)/shard_map/reduce_scatter | solution.py:177
  516.8 6.5 %copy.56 = bf16[32,2,16,2048]{3,2,1,0:T(8,128)(2,1)} copy(bf16[32,2,16,2048]{3,0,2,1:T(8,128)(2,1)} %reduce-scatter.3.cloned.1.call-done) | data formatting | bytes 8388608 | tf_op jit(solution)/shard_map/reduce_scatter | solution.py:177
  523.3 7.4 %all-to-all-start.1 = ((bf16[32,2,16,2048]{3,2,1,0:T(8,128)(2,1)}), bf16[32,2,16,2048]{3,2,1,0:T(8,128)(2,1)}, u32[]{:S(2)}, u32[]{:S(2)}) async-start(bf16[32,2,16,2048]{3,2,1,0:T(8,128)(2,1)} %copy.56), calls=%async_computation.2 | async-start | bytes 8388608 | tf_op jit(solution)/shard_map/all_to_all | solution.py:184
  530.7 6.3 %convolution_convert_fusion = bf16[512,2048]{1,0:T(8,128)(2,1)} fusion(bf16[352,2048]{1,0:T(8,128)(2,1)} %param.33, bf16[512,2048]{1,0:T(8,128)(2,1)} %all-gather.11.cloned.1.call-done, bf16[352,2048]{1,0:T(8,128)(2,1)} %param.32, f32[512,352]{0,1:T(8,128)} %fusion.78), kind=kOutput, calls=%fused_computation.16 | convolution fusion | flops 1478524928 | bytes 7798784 | tf_op jit(solution)/shard_map/dot_general | solution.py:91
  537.1 47.5 %all-to-all-done.1 = bf16[32,2,16,2048]{3,2,1,0:T(8,128)(2,1)} async-done(((bf16[32,2,16,2048]{3,2,1,0:T(8,128)(2,1)}), bf16[32,2,16,2048]{3,2,1,0:T(8,128)(2,1)}, u32[]{:S(2)}, u32[]{:S(2)}) %all-to-all-start.1) | async-done | bytes 4194336 | tf_op jit(solution)/shard_map/all_to_all | solution.py:184
  584.6 10.1 %gather_fusion.2 = bf16[768,2048]{1,0:T(8,128)(2,1)} fusion(bf16[1024,2048]{1,0:T(8,128)(2,1)} %bitcast.23, s32[1024]{0:T(1024)S(1)} %pad_clamp_fusion), kind=kCustom, calls=%fused_computation.3 | custom fusion | bytes 6294528 | tf_op jit(solution)/shard_map/gather | solution.py:189
  594.7 6.6 %reshape.154 = f32[128,6,2048]{2,1,0:T(8,128)} reshape(bf16[768,2048]{1,0:T(8,128)(2,1)} %gather_fusion.2) | data formatting | bytes 9437184 | tf_op jit(solution)/shard_map/convert_element_type | solution.py:189
  601.2 7.6 %multiply_reduce_fusion = f32[128,2048]{1,0:T(8,128)} fusion(f32[128,6,2048]{2,1,0:T(8,128)} %reshape.154, f32[128,6]{1,0:T(8,128)S(1)} %copy.57), kind=kLoop, calls=%fused_computation.6 | loop fusion | flops 2883584 | bytes 7343104 | tf_op jit(solution)/shard_map/reduce_sum | solution.py:191
  608.8 2.7 add_convert_fusion
  (72 shorter events, 21.1 us)
Async XLA Ops:
  6.5 346.7 %copy-start = (bf16[2,352,2048]{2,1,0:T(8,128)(2,1)S(1)}, bf16[2,352,2048]{2,1,0:T(8,128)(2,1)}, u32[]{:S(2)}) copy-start(bf16[2,352,2048]{2,1,0:T(8,128)(2,1)} %param.30) | copy-start | bytes 8650756
  6.5 35.8 %all-gather.5.cloned.1.call-start = ((), (), s32[]{:S(2)}) async-start(), calls=%async_computation.4 | async-start | bytes 2621440 | tf_op jit(solution)/shard_map/all_gather | solution.py:134
  7.3 67.5 %all-gather.7.cloned.1.call-start = ((), (), s32[]{:S(2)}) async-start(), calls=%async_computation.5 | async-start | bytes 2621440 | tf_op jit(solution)/shard_map/all_gather | solution.py:135
  8.0 320.2 %all-gather.9.cloned.1.call-start = ((), (), s32[]{:S(2)}) async-start(), calls=%async_computation.6 | async-start | bytes 20971520 | tf_op jit(solution)/shard_map/all_gather | solution.py:171
  14.4 20.3 %copy-start.3 = (bf16[2,64,4,4,128]{4,3,2,1,0:T(4,128)(2,1)}, bf16[2,64,4,4,128]{4,3,2,1,0:T(4,128)(2,1)S(1)}, u32[]{:S(2)}) copy-start(bf16[2,64,4,4,128]{4,3,2,1,0:T(4,128)(2,1)S(1)} %reshape.147) | copy-start | bytes 1572868
  77.9 2.8 copy-start.5
  79.8 1.8 copy-start.2
  80.7 1.1 copy-start.6
  90.5 1.0 copy-start.1
  91.7 81.6 %copy-start.4 = (bf16[128,2048]{1,0:T(8,128)(2,1)}, bf16[128,2048]{1,0:T(8,128)(2,1)S(1)}, u32[]{:S(2)}) copy-start(bf16[128,2048]{1,0:T(8,128)(2,1)S(1)} %multiply_convert_fusion) | copy-start | bytes 1572868
  177.5 190.2 %all-gather.11.cloned.1.call-start = ((), (), s32[]{:S(2)}) async-start(), calls=%async_computation.8 | async-start | bytes 2621440 | tf_op jit(solution)/shard_map/all_gather | solution.py:172
  178.1 338.7 %reduce-scatter.3.cloned.1.call-start = ((), (), s32[]{:S(2)}) async-start(), calls=%async_computation.7 | async-start | bytes 20971520 | tf_op jit(solution)/shard_map/reduce_scatter | solution.py:177
  328.2 12.3 %copy-start.8 = (bf16[2,352,2048]{2,1,0:T(8,128)(2,1)S(1)}, bf16[2,352,2048]{2,1,0:T(8,128)(2,1)}, u32[]{:S(2)}) copy-start(bf16[2,352,2048]{2,1,0:T(8,128)(2,1)} %param.28) | copy-start | bytes 8650756
  523.3 61.3 %all-to-all-start.1 = ((bf16[32,2,16,2048]{3,2,1,0:T(8,128)(2,1)}), bf16[32,2,16,2048]{3,2,1,0:T(8,128)(2,1)}, u32[]{:S(2)}, u32[]{:S(2)}) async-start(bf16[32,2,16,2048]{3,2,1,0:T(8,128)(2,1)} %copy.56), calls=%async_computation.2 | async-start | bytes 8388608 | tf_op jit(solution)/shard_map/all_to_all | solution.py:184
  530.6 6.4 %copy-start.7 = (f32[128,6]{0,1:T(8,128)S(1)}, f32[128,6]{0,1:T(8,128)}, u32[]{:S(2)}) copy-start(f32[128,6]{0,1:T(8,128)} %param.35) | copy-start | bytes 9220
  530.6 78.2 %reduce-scatter.5.cloned.1.call-start = ((), (), s32[]{:S(2)}) async-start(), calls=%async_computation.9 | async-start | bytes 2621440 | tf_op jit(solution)/shard_map/reduce_scatter | solution.py:180
Sparse Core Ops, SparseCore 0:
  9.0 33.2 all-gather.4
  44.0 30.7 all-gather.6
  177.7 150.4 all-gather.8
  329.7 31.7 all-gather.10
  367.8 148.9 reduce-scatter.2
  537.1 29.5 reduce-scatter.4
where the time goes:
time: 626 us; the launch traced here: 619 us
  waiting for transfers between devices  382 us (61%)
  local copies, waits for them, and re-layouts  71.2 us (11%)
  matrix products  62.7 us (10%)
  blocking collectives  58.1 us (9%)
  other arithmetic  23.3 us (4%)
  between operations  14 us (2%)
  starting transfers between devices  7.55 us (1%)
    all_gather x1, waiting for transfers between devices, on_device(): lax.all_gather(arrived, 'dp', axis=0, tiled=True)  150 us
    reduce_scatter x1, waiting for transfers between devices, on_device(): lax.psum_scatter(routed_terms.astype(jnp.bfloat16), 'dp', scatter_dimensi...  145 us
    all_to_all x1, blocking collectives, on_device(): lax.all_to_all(outgoing, 'exp', split_axis=0, concat_axis=0, tiled=True)  58.1 us
    all_to_all x1, waiting for transfers between devices, on_device(): lax.all_to_all(routed_sum.astype(jnp.bfloat16), 'exp', split_axis=0, conc...  47.5 us
    all_gather x1, waiting for transfers between devices, on_device(): lax.all_gather(value_pool, 'dp', axis=0, tiled=True)  29.4 us
    scatter x1, local copies, waits for them, and re-layouts, on_device(): outgoing = jnp.zeros((expert_count * CAP, model_width), jnp.bfloat16).at[...  23.5 us
    dot_general x1, matrix products, expert_block(): jnp.einsum('sekf,efd->sekd', inner, down_rows, preferred_element_type=jnp...  14.4 us
    dot_general x1, matrix products, expert_block(): jnp.einsum('sekd,efd->sekf', grouped, gate_rows, preferred_element_type=j...  12.7 us
  transfers between devices with their start and end apart: 7, of which 5 were waited for; matrix products, arithmetic and copies ran while one was open for 17% of the time, Pallas kernels for 0%

commit v1 on v0

--- a/solution.py
+++ b/solution.py
@@ -125,15 +125,13 @@
         tree_mask,
         draft_values,
     )
+    both_pools = lax.all_gather(jnp.stack([key_pool, value_pool]), "dp", axis=1, tiled=True)
     final_top, final_total, final_sum = pool_state(
         tree_state,
         query_heads,
         page_table,
         cache_len,
-        (
-            lax.all_gather(key_pool, "dp", axis=0, tiled=True),
-            lax.all_gather(value_pool, "dp", axis=0, tiled=True),
-        ),
+        (both_pools[0], both_pools[1]),
     )
     attention = (
         (final_sum / jnp.transpose(final_total, (0, 3, 1, 2))[..., None])
@@ -151,44 +149,59 @@
     normed = (residual_wide * scale_rows * norm_gain.astype(jnp.float32)).astype(jnp.bfloat16)
     local_experts = expert_gate.shape[0]
     column_count = lax.axis_size("exp")
+    row_count = lax.axis_size("dp")
     expert_count = local_experts * column_count
-    pick_count = expert_ids.shape[1]
+    slot_total = expert_count * CAP
     flat_experts = expert_ids.reshape(-1)
     onehot = (flat_experts[:, None] == jnp.arange(expert_count, dtype=jnp.int32)[None, :]).astype(
         jnp.int32
     )
     slot_ids = jnp.sum((jnp.cumsum(onehot, axis=0) - 1) * onehot, axis=1)
-    destinations = flat_experts * CAP + slot_ids
-    token_rows = jnp.arange(tok_rows * pick_count, dtype=jnp.int32) // pick_count
-    outgoing = (
-        jnp.zeros((expert_count * CAP, model_width), jnp.bfloat16)
-        .at[destinations]
-        .set(normed[token_rows])
-    )
-    outgoing = outgoing.reshape(column_count, local_experts, CAP, model_width)
+    destinations = (flat_experts * CAP + slot_ids).reshape(expert_ids.shape)
+    slot_hits = destinations[:, :, None] == jnp.arange(slot_total, dtype=jnp.int32)[None, None, :]
+    placement = jnp.sum(slot_hits.astype(jnp.bfloat16), axis=1)
+    outgoing = jnp.einsum(
+        "ts,td->sd", placement, normed, preferred_element_type=jnp.float32
+    ).astype(jnp.bfloat16)
+    outgoing = outgoing.reshape(column_count, local_experts * CAP, model_width)
     arrived = lax.all_to_all(outgoing, "exp", split_axis=0, concat_axis=0, tiled=True)
-    grouped, group_tokens = (
-        lax.all_gather(arrived, "dp", axis=0, tiled=True),
-        lax.all_gather(normed, "dp", axis=0, tiled=True),
-    )
+    arrived = arrived.reshape(column_count * local_experts * CAP, model_width)
+    gathered = lax.all_gather(
+        jnp.concatenate([arrived, normed], axis=0), "dp", axis=0, tiled=False
+    )
+    arrived_rows = column_count * local_experts * CAP
+    grouped = gathered[:, :arrived_rows].reshape(
+        row_count * column_count, local_experts, CAP, model_width
+    )
+    group_tokens = gathered[:, arrived_rows:].reshape(row_count * tok_rows, model_width)
     routed_terms = expert_block(grouped, expert_gate, expert_up, expert_down)
     shared_terms = shared_block(group_tokens, shared_gate, shared_up, shared_down)
-    routed_sum, shared_sum = (
-        lax.psum_scatter(
-            routed_terms.astype(jnp.bfloat16), "dp", scatter_dimension=0, tiled=True
-        ).astype(jnp.float32),
-        lax.psum_scatter(
-            shared_terms.astype(jnp.bfloat16), "dp", scatter_dimension=0, tiled=True
-        ).astype(jnp.float32),
-    )
+    both_terms = jnp.concatenate(
+        [
+            routed_terms.astype(jnp.bfloat16).reshape(row_count, arrived_rows, model_width),
+            shared_terms.astype(jnp.bfloat16).reshape(row_count, tok_rows, model_width),
+        ],
+        axis=1,
+    )
+    both_sums = lax.psum_scatter(both_terms, "dp", scatter_dimension=0, tiled=False)
+    routed_sum = both_sums[:arrived_rows]
+    shared_sum = both_sums[arrived_rows:].astype(jnp.float32)
     returned = lax.all_to_all(
-        routed_sum.astype(jnp.bfloat16), "exp", split_axis=0, concat_axis=0, tiled=True
-    )
-    returned_rows = returned.reshape(expert_count * CAP, model_width)
-    picked_rows = (
-        returned_rows[destinations].astype(jnp.float32).reshape(tok_rows, pick_count, model_width)
-    )
-    routed_out = jnp.sum(picked_rows * expert_weights[:, :, None], axis=1)
+        routed_sum.reshape(column_count, local_experts * CAP, model_width),
+        "exp",
+        split_axis=0,
+        concat_axis=0,
+        tiled=True,
+    )
+    returned_rows = returned.reshape(slot_total, model_width)
+    slot_weights = jnp.sum(
+        jnp.where(slot_hits, expert_weights[:, :, None], 0.0), axis=1
+    )
+    weights_high = slot_weights.astype(jnp.bfloat16)
+    weights_low = (slot_weights - weights_high.astype(jnp.float32)).astype(jnp.bfloat16)
+    routed_out = jnp.dot(
+        weights_high, returned_rows, preferred_element_type=jnp.float32
+    ) + jnp.dot(weights_low, returned_rows, preferred_element_type=jnp.float32)
     return (residual.astype(jnp.float32) + routed_out + shared_sum).astype(jnp.bfloat16)
 
 

time: 626 us -> 667 us (1.065)
  waiting for transfers between devices: 382 us -> 413 us
  other arithmetic: 23.3 us -> 37.8 us
  matrix products: 62.7 us -> 70.6 us
    scatter x1 -> x0, local copies, waits for them, and re-layouts: 23.5 us -> none  [on_device(): outgoing = jnp.zeros((expert_count * CAP, model_width), jnp.bfloat16).at[...]
    concatenate x0 -> x2, other arithmetic: none -> 22.8 us  [the longest x1 20.3 us: on_device(): jnp.concatenate([routed_terms.astype(jnp.bfloat16).reshape(row_count, arr...]
    slice x1 -> x4, local copies, waits for them, and re-layouts: 1.2 us -> 22.9 us  [the longest x1 15.2 us: on_device(): gathered[:, :arrived_rows]]
    reduce_scatter x2 -> x1, waiting for transfers between devices: 145 us -> 165 us  [on_device(): lax.psum_scatter(both_terms, 'dp', scatter_dimension=0, tiled=False)]
    convert_element_type x1, local copies, waits for them, and re-layouts: 6.55 us -> 18.7 us  [on_device(): routed_terms.astype(jnp.bfloat16)]
    gather x1 -> x0, local copies, waits for them, and re-layouts: 10.1 us -> none  [on_device(): returned_rows[destinations].astype(jnp.float32)]
    dot_general x0 -> x3, matrix products: none -> 8.25 us  [the longest x1 3.99 us: on_device(): jnp.dot(weights_low, returned_rows, preferred_element_type=jnp.float32)]
    all_gather x4 -> x2, waiting for transfers between devices: 187 us -> 194 us  [the longest x1 169 us: on_device(): lax.all_gather(jnp.concatenate([arrived, normed], axis=0), 'dp', axis=0,...]
  transfers between devices with their start and end apart: 7 -> 4, of which waited for: 5 -> 4; matrix products, arithmetic and copies ran while one was open for 17% -> 4% of each run, Pallas kernels for 0% -> 0%
where the time goes in v1:
time: 667 us; the launch traced here: 666 us
  waiting for transfers between devices  413 us (62%)
  matrix products  70.6 us (11%)
  local copies, waits for them, and re-layouts  65.5 us (10%)
  blocking collectives  57.9 us (9%)
  other arithmetic  37.8 us (6%)
  between operations  13.4 us (2%)
  starting transfers between devices  7.79 us (1%)
    all_gather x1, waiting for transfers between devices, on_device(): lax.all_gather(jnp.concatenate([arrived, normed], axis=0), 'dp', axis=0,...  169 us
    reduce_scatter x1, waiting for transfers between devices, on_device(): lax.psum_scatter(both_terms, 'dp', scatter_dimension=0, tiled=False)  165 us
    all_to_all x1, blocking collectives, on_device(): lax.all_to_all(outgoing, 'exp', split_axis=0, concat_axis=0, tiled=True)  57.9 us
    all_to_all x1, waiting for transfers between devices, on_device(): lax.all_to_all(routed_sum.reshape(column_count, local_experts * CAP, mode...  53.5 us
    all_gather x1, waiting for transfers between devices, on_device(): lax.all_gather(jnp.stack([key_pool, value_pool]), 'dp', axis=1, tiled=True)  25 us
    concatenate x1, other arithmetic, on_device(): jnp.concatenate([routed_terms.astype(jnp.bfloat16).reshape(row_count, arr...  20.3 us
    convert_element_type x1, local copies, waits for them, and re-layouts, on_device(): routed_terms.astype(jnp.bfloat16)  18.7 us
    slice x1, local copies, waits for them, and re-layouts, on_device(): gathered[:, :arrived_rows]  15.2 us
  transfers between devices with their start and end apart: 4, of which 4 were waited for; matrix products, arithmetic and copies ran while one was open for 4% of the time, Pallas kernels for 0%

profile of v1, /device:TPU:0, one launch (start us, length us, event | category | flops | bytes accessed | tf_op | source)
XLA Modules:
  0.0 665.8 jit_solution(17949467007883011695)
XLA Ops:
  6.6 2.4 pad_maximum_fusion.2
  11.4 1.4 reshape.101
  13.5 1.6 fusion.87
  15.1 1.6 reshape_squeeze.6
  20.8 1.4 fusion.62
  22.2 4.4 reduce-window.6
  32.3 2.6 fusion.88
  34.9 25.0 %all-gather.4.cloned.1.call-done = bf16[2,32,64,512]{3,2,1,0:T(8,128)(2,1)} async-done(((bf16[2,8,64,512]{3,2,1,0:T(8,128)(2,1)}), bf16[2,32,64,512]{3,2,1,0:T(8,128)(2,1)}) %all-gather.4.cloned.1.call-update) | async-done | bytes 4194320 | tf_op jit(solution)/shard_map/all_gather | solution.py:128
  59.9 4.7 slice_bitcast_fusion
  64.6 2.2 gather_fusion
  67.7 2.2 gather_fusion.1
  70.8 1.8 bitcast_reduce_fusion
  77.2 1.4 convert_element_type.90
  78.6 4.9 multiply_reduce_fusion
  85.9 57.9 %all_to_all.10 = bf16[32,32,2048]{2,1,0:T(8,128)(2,1)S(1)} all-to-all(bf16[32,32,2048]{2,1,0:T(8,128)(2,1)S(1)} %bitcast.149), channel_id=1, replica_groups=mesh['dp'=4,'exp'=32] {'exp'}, dimensions={0} | all-to-all | bytes 8388608 | tf_op jit(solution)/shard_map/all_to_all | solution.py:167
  143.9 2.5 pad_maximum_fusion.1
  146.6 169.1 %all-gather.6.cloned.1.call-done = bf16[4608,2048]{1,0:T(8,128)(2,1)} async-done(((bf16[1152,2048]{1,0:T(8,128)(2,1)}), bf16[4608,2048]{1,0:T(8,128)(2,1)}) %all-gather.6.cloned.1.call-update) | async-done | bytes 18874384 | tf_op jit(solution)/shard_map/all_gather | solution.py:169
  315.8 1.8 slice.50
  317.7 15.2 %slice.49 = bf16[4,1024,2048]{2,1,0:T(8,128)(2,1)} slice(bf16[4,1152,2048]{2,1,0:T(8,128)(2,1)} %bitcast.151), slice={[0:4], [0:1024], [0:2048]} | slice | bytes 33554432 | tf_op jit(solution)/shard_map/slice | solution.py:173
  332.8 14.3 %fusion = f32[2,128,16,352]{3,2,1,0:T(8,128)} fusion(bf16[128,2,16,2048]{3,2,1,0:T(8,128)(2,1)} %bitcast.152, bf16[2,352,2048]{2,1,0:T(8,128)(2,1)S(1)} %copy-done.13), kind=kOutput, calls=%fused_computation.4 | convolution fusion | flops 5905580032 | bytes 25427968 | tf_op jit(solution)/shard_map/sekd,efd->sekf/dot_general | solution.py:80
  347.1 14.6 %fusion.4 = bf16[128,2,16,352]{3,2,0,1:T(8,128)(2,1)S(1)} fusion(f32[2,128,16,352]{3,2,1,0:T(8,128)} %fusion, bf16[2,352,2048]{2,1,0:T(8,128)(2,1)} %param.28, bf16[128,2,16,2048]{3,2,1,0:T(8,128)(2,1)} %bitcast.153), kind=kOutput, calls=%fused_computation.9 | convolution fusion | flops 5914230784 | bytes 28311552 | tf_op jit(solution)/shard_map/sekd,efd->sekf/dot_general | solution.py:77
  361.7 12.3 %convert_bitcast_fusion = bf16[128,2,16,2048]{3,0,2,1:T(8,128)(2,1)} fusion(bf16[128,2,16,352]{3,2,0,1:T(8,128)(2,1)S(1)} %fusion.4, bf16[2,352,2048]{2,1,0:T(8,128)(2,1)S(1)} %copy-done), kind=kOutput, calls=%fused_computation.3 | convolution fusion | flops 5913968640 | bytes 22544384 | tf_op jit(solution)/shard_map/sekf,efd->sekd/dot_general | solution.py:84
  374.0 18.7 %copy.80 = bf16[128,2,16,2048]{3,2,1,0:T(8,128)(2,1)} copy(bf16[128,2,16,2048]{3,0,2,1:T(8,128)(2,1)} %convert_bitcast_fusion) | data formatting | bytes 33554432 | tf_op jit(solution)/shard_map/convert_element_type | solution.py:181
  392.8 1.8 fusion.89
  394.6 6.1 convolution_convert_fusion.1
  400.7 20.3 %pad_maximum_fusion = bf16[4,1152,2048]{2,1,0:T(8,128)(2,1)} fusion(bf16[4,128,2048]{2,1,0:T(8,128)(2,1)} %bitcast.156, bf16[4,1024,2048]{2,1,0:T(8,128)(2,1)} %bitcast.148), kind=kLoop, calls=%fused_computation.2 | loop fusion | flops 37748736 | bytes 37748736 | tf_op jit(solution)/shard_map/concatenate | solution.py:179
  421.0 165.0 %reduce-scatter.2.cloned.1.call-done = bf16[1,1152,2048]{2,1,0:T(8,128)(2,1)} async-done(((bf16[4,1152,2048]{2,1,0:T(8,128)(2,1)}), bf16[1,1152,2048]{2,1,0:T(8,128)(2,1)}) %reduce-scatter.2.cloned.1.call-update) | async-done | bytes 4718608 | tf_op jit(solution)/shard_map/reduce_scatter | solution.py:186
  586.0 4.7 slice.51
  590.8 7.5 %all-to-all-start.1 = ((bf16[32,32,2048]{2,1,0:T(8,128)(2,1)}), bf16[32,32,2048]{2,1,0:T(8,128)(2,1)}, u32[]{:S(2)}, u32[]{:S(2)}) async-start(bf16[32,32,2048]{2,1,0:T(8,128)(2,1)} %bitcast.154), calls=%async_computation.2 | async-start | bytes 8388608 | tf_op jit(solution)/shard_map/all_to_all | solution.py:189
  598.7 53.5 %all-to-all-done.1 = bf16[32,32,2048]{2,1,0:T(8,128)(2,1)} async-done(((bf16[32,32,2048]{2,1,0:T(8,128)(2,1)}), bf16[32,32,2048]{2,1,0:T(8,128)(2,1)}, u32[]{:S(2)}, u32[]{:S(2)}) %all-to-all-start.1) | async-done | bytes 4194336 | tf_op jit(solution)/shard_map/all_to_all | solution.py:189
  652.2 3.0 fusion.66
  655.2 4.0 fusion.15
  (76 shorter events, 22.3 us)
Async XLA Ops:
  6.5 355.2 %copy-start = (bf16[2,352,2048]{2,1,0:T(8,128)(2,1)S(1)}, bf16[2,352,2048]{2,1,0:T(8,128)(2,1)}, u32[]{:S(2)}) copy-start(bf16[2,352,2048]{2,1,0:T(8,128)(2,1)} %param.30) | copy-start | bytes 8650756
  6.5 2.5 copy-start.9
  6.5 4.1 copy-start.12
  6.5 10.2 %copy-start.11 = (s32[2,64]{1,0:T(2,128)S(1)}, s32[2,64]{1,0:T(2,128)}, u32[]{:S(2)}) copy-start(s32[2,64]{1,0:T(2,128)} %param.25) | copy-start | bytes 1540
  6.5 53.4 %all-gather.4.cloned.1.call-start = ((), (), s32[]{:S(2)}) async-start(), calls=%async_computation.3 | async-start | bytes 5242880 | tf_op jit(solution)/shard_map/all_gather | solution.py:128
  9.0 306.8 %all-gather.6.cloned.1.call-start = ((), (), s32[]{:S(2)}) async-start(), calls=%async_computation.5 | async-start | bytes 23592960 | tf_op jit(solution)/shard_map/all_gather | solution.py:169
  12.8 51.8 %copy-start.5 = (bf16[2,64,4,4,128]{4,3,2,1,0:T(4,128)(2,1)}, bf16[2,64,4,4,128]{4,3,2,1,0:T(4,128)(2,1)S(1)}, u32[]{:S(2)}) copy-start(bf16[2,64,4,4,128]{4,3,2,1,0:T(4,128)(2,1)S(1)} %reshape.101) | copy-start | bytes 1572868
  70.8 2.8 copy-start.7
  72.7 1.8 copy-start.3
  73.6 1.1 copy-start.8
  78.6 6.0 copy-start.6
  83.5 1.0 copy-start.1
  146.4 439.6 %reduce-scatter.2.cloned.1.call-start = ((), (), s32[]{:S(2)}) async-start(), calls=%async_computation.4 | async-start | bytes 23592960 | tf_op jit(solution)/shard_map/reduce_scatter | solution.py:186
  317.6 75.1 %copy-start.4 = (bf16[4,128,2048]{2,1,0:T(8,128)(2,1)}, bf16[4,128,2048]{2,1,0:T(8,128)(2,1)S(1)}, u32[]{:S(2)}) copy-start(bf16[4,128,2048]{2,1,0:T(8,128)(2,1)S(1)} %slice.50) | copy-start | bytes 6291460
  317.6 15.2 %copy-start.13 = (bf16[2,352,2048]{2,1,0:T(8,128)(2,1)S(1)}, bf16[2,352,2048]{2,1,0:T(8,128)(2,1)}, u32[]{:S(2)}) copy-start(bf16[2,352,2048]{2,1,0:T(8,128)(2,1)} %param.29) | copy-start | bytes 8650756
  374.0 18.7 %copy-start.14 = (bf16[352,2048]{1,0:T(8,128)(2,1)S(1)}, bf16[352,2048]{1,0:T(8,128)(2,1)}, u32[]{:S(2)}) copy-start(bf16[352,2048]{1,0:T(8,128)(2,1)} %param.31) | copy-start | bytes 4325380
  590.8 7.5 %copy-start.10 = (f32[128,6]{0,1:T(8,128)S(1)}, f32[128,6]{0,1:T(8,128)}, u32[]{:S(2)}) copy-start(f32[128,6]{0,1:T(8,128)} %param.35) | copy-start | bytes 9220
  590.8 61.5 %all-to-all-start.1 = ((bf16[32,32,2048]{2,1,0:T(8,128)(2,1)}), bf16[32,32,2048]{2,1,0:T(8,128)(2,1)}, u32[]{:S(2)}, u32[]{:S(2)}) async-start(bf16[32,32,2048]{2,1,0:T(8,128)(2,1)} %bitcast.154), calls=%async_computation.2 | async-start | bytes 8388608 | tf_op jit(solution)/shard_map/all_to_all | solution.py:189
  652.2 3.0 copy-start.2
Sparse Core Ops, SparseCore 0:
  9.2 50.6 all-gather.3
  146.5 169.2 all-gather.5
  421.1 164.8 reduce-scatter.1

commit v2 on v0

--- a/solution.py
+++ b/solution.py
@@ -47,15 +47,15 @@
 
 
 def pool_state(carry_state, query_heads, table_rows, lengths, pieces):
-    piece_keys, piece_values = pieces
-    piece_count = piece_keys.shape[0]
+    piece_count = pieces.shape[1]
     request_count, pages_per = table_rows.shape
-    page_size = piece_keys.shape[1]
+    page_size = pieces.shape[2]
     key_heads = query_heads.shape[2]
     inside = (table_rows >= 0) & (table_rows < piece_count)
     picked = jnp.clip(table_rows, 0, piece_count - 1)
-    cache_keys = piece_keys[picked].reshape(request_count, pages_per * page_size, key_heads, -1)
-    cache_values = piece_values[picked].reshape(request_count, pages_per * page_size, key_heads, -1)
+    picked_pages = pieces[:, picked]
+    cache_keys = picked_pages[0].reshape(request_count, pages_per * page_size, key_heads, -1)
+    cache_values = picked_pages[1].reshape(request_count, pages_per * page_size, key_heads, -1)
     positions = jnp.arange(pages_per * page_size, dtype=jnp.int32)
     usable = jnp.repeat(inside, page_size, axis=1) & (positions[None, :] < lengths[:, None])
     live_mask = jnp.broadcast_to(
@@ -125,15 +125,19 @@
         tree_mask,
         draft_values,
     )
+    both_pools = lax.all_gather(jnp.stack([key_pool, value_pool]), "dp", axis=1, tiled=True)
+    group_picks = lax.all_gather(
+        jnp.concatenate([expert_ids.astype(jnp.float32), expert_weights], axis=1),
+        "dp",
+        axis=0,
+        tiled=True,
+    )
     final_top, final_total, final_sum = pool_state(
         tree_state,
         query_heads,
         page_table,
         cache_len,
-        (
-            lax.all_gather(key_pool, "dp", axis=0, tiled=True),
-            lax.all_gather(value_pool, "dp", axis=0, tiled=True),
-        ),
+        both_pools,
     )
     attention = (
         (final_sum / jnp.transpose(final_total, (0, 3, 1, 2))[..., None])
@@ -149,47 +153,102 @@
         jnp.mean(residual_wide * residual_wide, axis=-1, keepdims=True) + NORM_EPSILON
     )
     normed = (residual_wide * scale_rows * norm_gain.astype(jnp.float32)).astype(jnp.bfloat16)
-    local_experts = expert_gate.shape[0]
     column_count = lax.axis_size("exp")
-    expert_count = local_experts * column_count
+    row_count = lax.axis_size("dp")
     pick_count = expert_ids.shape[1]
-    flat_experts = expert_ids.reshape(-1)
-    onehot = (flat_experts[:, None] == jnp.arange(expert_count, dtype=jnp.int32)[None, :]).astype(
-        jnp.int32
-    )
-    slot_ids = jnp.sum((jnp.cumsum(onehot, axis=0) - 1) * onehot, axis=1)
-    destinations = flat_experts * CAP + slot_ids
-    token_rows = jnp.arange(tok_rows * pick_count, dtype=jnp.int32) // pick_count
-    outgoing = (
-        jnp.zeros((expert_count * CAP, model_width), jnp.bfloat16)
-        .at[destinations]
-        .set(normed[token_rows])
-    )
-    outgoing = outgoing.reshape(column_count, local_experts, CAP, model_width)
-    arrived = lax.all_to_all(outgoing, "exp", split_axis=0, concat_axis=0, tiled=True)
-    grouped, group_tokens = (
-        lax.all_gather(arrived, "dp", axis=0, tiled=True),
-        lax.all_gather(normed, "dp", axis=0, tiled=True),
-    )
-    routed_terms = expert_block(grouped, expert_gate, expert_up, expert_down)
+    near_cap = CAP
+    far_cap = CAP * row_count
+    group_tokens = lax.all_gather(normed, "dp", axis=0, tiled=True)
+    group_ids = group_picks[:, :pick_count].astype(jnp.int32)
+    group_weights = group_picks[:, pick_count:]
+
+    def slot_plan(ids, weights, parity, cap):
+        token_count = ids.shape[0]
+        picks = ((ids // 2)[:, :, None] == jnp.arange(column_count, dtype=jnp.int32)[None, None, :]) & (
+            (ids % 2) == parity
+        )[:, :, None]
+        member = jnp.any(picks, axis=1)
+        token_weight = jnp.sum(jnp.where(picks, weights[:, :, None], 0.0), axis=1)
+        earlier = (
+            jnp.arange(token_count, dtype=jnp.int32)[:, None]
+            > jnp.arange(token_count, dtype=jnp.int32)[None, :]
+        ).astype(jnp.bfloat16)
+        rank = jnp.dot(
+            earlier, member.astype(jnp.bfloat16), preferred_element_type=jnp.float32
+        ).astype(jnp.int32)
+        place = member[:, :, None] & (
+            rank[:, :, None] == jnp.arange(cap, dtype=jnp.int32)[None, None, :]
+        )
+        slot_weights = jnp.where(place, token_weight[:, :, None], 0.0)
+        return (
+            place.reshape(token_count, column_count * cap),
+            slot_weights.reshape(token_count, column_count * cap),
+        )
+
+    near_place, near_weights = slot_plan(expert_ids, expert_weights, 0, near_cap)
+    far_place, far_weights = slot_plan(group_ids, group_weights, 1, far_cap)
+    near_out = jnp.einsum(
+        "ts,td->sd",
+        near_place.astype(jnp.bfloat16),
+        normed,
+        preferred_element_type=jnp.float32,
+    ).astype(jnp.bfloat16)
+    far_out = jnp.einsum(
+        "ts,td->sd",
+        far_place.astype(jnp.bfloat16),
+        group_tokens,
+        preferred_element_type=jnp.float32,
+    ).astype(jnp.bfloat16)
+    near_arrived = lax.all_to_all(
+        near_out.reshape(column_count, near_cap, model_width),
+        "exp",
+        split_axis=0,
+        concat_axis=0,
+        tiled=True,
+    )
+    far_arrived = lax.all_to_all(
+        far_out.reshape(column_count, far_cap, model_width),
+        "exp",
+        split_axis=0,
+        concat_axis=0,
+        tiled=True,
+    )
+    near_rows = lax.all_gather(near_arrived, "dp", axis=0, tiled=True).reshape(-1, model_width)
+    far_rows = far_arrived.reshape(-1, model_width)
+    near_terms = shared_block(near_rows, expert_gate[0], expert_up[0], expert_down[0])
+    far_terms = shared_block(far_rows, expert_gate[1], expert_up[1], expert_down[1])
     shared_terms = shared_block(group_tokens, shared_gate, shared_up, shared_down)
-    routed_sum, shared_sum = (
-        lax.psum_scatter(
-            routed_terms.astype(jnp.bfloat16), "dp", scatter_dimension=0, tiled=True
-        ).astype(jnp.float32),
-        lax.psum_scatter(
-            shared_terms.astype(jnp.bfloat16), "dp", scatter_dimension=0, tiled=True
-        ).astype(jnp.float32),
-    )
-    returned = lax.all_to_all(
-        routed_sum.astype(jnp.bfloat16), "exp", split_axis=0, concat_axis=0, tiled=True
-    )
-    returned_rows = returned.reshape(expert_count * CAP, model_width)
-    picked_rows = (
-        returned_rows[destinations].astype(jnp.float32).reshape(tok_rows, pick_count, model_width)
-    )
-    routed_out = jnp.sum(picked_rows * expert_weights[:, :, None], axis=1)
-    return (residual.astype(jnp.float32) + routed_out + shared_sum).astype(jnp.bfloat16)
+    near_sum = lax.psum_scatter(
+        near_terms.astype(jnp.bfloat16).reshape(row_count, column_count, near_cap, model_width),
+        "dp",
+        scatter_dimension=0,
+        tiled=False,
+    )
+    far_back = lax.all_to_all(
+        far_terms.astype(jnp.bfloat16).reshape(column_count, far_cap, model_width),
+        "exp",
+        split_axis=0,
+        concat_axis=0,
+        tiled=True,
+    ).reshape(-1, model_width)
+    near_back = lax.all_to_all(
+        near_sum, "exp", split_axis=0, concat_axis=0, tiled=True
+    ).reshape(-1, model_width)
+
+    def combine(slot_weights, rows):
+        return jnp.dot(slot_weights.astype(jnp.bfloat16), rows, preferred_element_type=jnp.float32)
+
+    far_part = combine(far_weights, far_back) + shared_terms.astype(
+        jnp.bfloat16
+    ).astype(jnp.float32)
+    far_sum = lax.psum_scatter(
+        far_part.astype(jnp.bfloat16).reshape(row_count, tok_rows, model_width),
+        "dp",
+        scatter_dimension=0,
+        tiled=False,
+    ).astype(jnp.float32)
+    near_part = combine(near_weights, near_back)
+    return (residual.astype(jnp.float32) + near_part + far_sum).astype(jnp.bfloat16)
 
 
 def solution(mesh):

time: 626 us -> 440 us (0.70); the launches traced: 619 us -> 439 us
  waiting for transfers between devices: 382 us -> 260 us
  local copies, waits for them, and re-layouts: 71.2 us -> 13.9 us
  matrix products: 62.7 us -> 80.2 us
  other arithmetic: 23.3 us -> 8.4 us
  blocking collectives: 58.1 us -> 47.7 us
  starting transfers between devices: 7.55 us -> 15.1 us
    reduce_scatter x2, waiting for transfers between devices: 145 us -> 20.5 us  [the longest x1 20.5 us: on_device(): lax.psum_scatter(far_part.astype(jnp.bfloat16).reshape(row_count, tok_row...]
    all_to_all x1 -> x3, waiting for transfers between devices: 47.5 us -> 144 us  [the longest x1 97 us: on_device(): lax.all_to_all(far_terms.astype(jnp.bfloat16).reshape(column_count, far_c...]
    all_gather x4 -> x3, waiting for transfers between devices: 187 us -> 95.3 us  [the longest x1 50.4 us: on_device(): lax.all_gather(near_arrived, 'dp', axis=0, tiled=True)]
    scatter x1 -> x0, local copies, waits for them, and re-layouts: 23.5 us -> none  [on_device(): outgoing = jnp.zeros((expert_count * CAP, model_width), jnp.bfloat16).at[...]
    all_to_all x1, blocking collectives: 58.1 us -> 35.6 us  [on_device(): lax.all_to_all(near_out.reshape(column_count, near_cap, model_width), 'ex...]
    dot_general x1 -> x3, matrix products: 6.27 us -> 19.6 us  [shared_block(): return jnp.dot(inner, down_rows, preferred_element_type=jnp.float32)]
    dot_general x1 -> x3, matrix products: 3.8 us -> 15.9 us  [shared_block(): jnp.einsum('td,fd->tf', tokens, gate_rows, preferred_element_type=jnp.flo...]
    all_gather x0 -> x1, blocking collectives: none -> 12.1 us  [on_device(): lax.all_gather(jnp.concatenate([expert_ids.astype(jnp.float32), expert_we...]
  transfers between devices with their start and end apart: 7 -> 8, of which waited for: 5 -> 6; matrix products, arithmetic and copies ran while one was open for 17% -> 17% of each run, Pallas kernels for 0% -> 0%
where the time goes in v2:
time: 440 us; the launch traced here: 439 us
  waiting for transfers between devices  260 us (59%)
  matrix products  80.2 us (18%)
  blocking collectives  47.7 us (11%)
  starting transfers between devices  15.1 us (3%)
  local copies, waits for them, and re-layouts  13.9 us (3%)
  between operations  13.8 us (3%)
  other arithmetic  8.4 us (2%)
    all_to_all x1, waiting for transfers between devices, on_device(): lax.all_to_all(far_terms.astype(jnp.bfloat16).reshape(column_count, far_c...  97 us
    all_gather x1, waiting for transfers between devices, on_device(): lax.all_gather(near_arrived, 'dp', axis=0, tiled=True)  50.4 us
    all_gather x1, waiting for transfers between devices, on_device(): lax.all_gather(jnp.stack([key_pool, value_pool]), 'dp', axis=1, tiled=True)  44.9 us
    all_to_all x1, waiting for transfers between devices, on_device(): lax.all_to_all(far_out.reshape(column_count, far_cap, model_width), 'exp'...  37.9 us
    all_to_all x1, blocking collectives, on_device(): lax.all_to_all(near_out.reshape(column_count, near_cap, model_width), 'ex...  35.6 us
    reduce_scatter x1, waiting for transfers between devices, on_device(): lax.psum_scatter(far_part.astype(jnp.bfloat16).reshape(row_count, tok_row...  20.5 us
    dot_general x3, matrix products, shared_block(): return jnp.dot(inner, down_rows, preferred_element_type=jnp.float32)  19.6 us
    dot_general x3, matrix products, shared_block(): jnp.einsum('td,fd->tf', tokens, gate_rows, preferred_element_type=jnp.flo...  15.9 us
  transfers between devices with their start and end apart: 8, of which 6 were waited for; matrix products, arithmetic and copies ran while one was open for 17% of the time, Pallas kernels for 0%

profile of v2, /device:TPU:0, one launch (start us, length us, event | category | flops | bytes accessed | tf_op | source)
XLA Modules:
  0.0 439.3 jit_solution(16087155554490792741)
XLA Ops:
  6.6 2.5 pad_maximum_fusion
  13.8 1.3 fusion.109
  15.0 44.9 %all-gather.4.cloned.1.call-done = bf16[2,32,64,512]{3,2,1,0:T(8,128)(2,1)} async-done(((bf16[2,8,64,512]{3,2,1,0:T(8,128)(2,1)}), bf16[2,32,64,512]{3,2,1,0:T(8,128)(2,1)}) %all-gather.4.cloned.1.call-update) | async-done | bytes 4194320 | tf_op jit(solution)/shard_map/all_gather | solution.py:128
  59.9 2.9 gather_fusion
  63.8 2.0 reshape_squeeze.14
  66.8 1.7 bitcast_reduce_fusion
  70.5 1.2 fusion.38
  72.8 4.8 %multiply_reduce_fusion = (f32[128]{0:T(128)S(1)}, f32[128,2048]{1,0:T(8,128)S(1)}) fusion(bf16[128,2048]{1,0:T(8,128)(2,1)S(1)} %convert_element_type.109, bf16[2048,2048]{1,0:T(8,128)(2,1)} %param.26, bf16[128,2048]{1,0:T(8,128)(2,1)S(1)} %copy-done.3), kind=kOutput, calls=%fused_computation.74 | convolution fusion | flops 1075314560 | bytes 10486272 | tf_op jit(solution)/shard_map/dot_general | solution.py:149
  77.6 1.0 multiply_convert_fusion
  80.7 1.7 convolution_convert_fusion.4
  82.5 35.6 %all_to_all.20 = bf16[32,16,2048]{2,1,0:T(8,128)(2,1)} all-to-all(bf16[32,16,2048]{2,1,0:T(8,128)(2,1)S(1)} %bitcast.152), channel_id=1, replica_groups=mesh['dp'=4,'exp'=32] {'exp'}, dimensions={0} | all-to-all | bytes 4194304 | tf_op jit(solution)/shard_map/all_to_all | solution.py:202
  118.8 12.1 %all_gather.14 = f32[512,12]{0,1:T(8,128)S(1)} all-gather(f32[128,12]{0,1:T(8,128)S(1)} %pad_maximum_fusion.1), channel_id=1, replica_groups=mesh['dp'=4,'exp'=32] {'dp'}, dimensions={0}, use_global_device_ids=true | all-gather | bytes 30720 | tf_op jit(solution)/shard_map/all_gather | solution.py:129
  132.7 1.6 fusion.2
  134.3 8.3 %convolution_convert_fusion.1 = bf16[2048,2048]{1,0:T(8,128)(2,1)} fusion(pred[512,2048]{0,1:T(32,128)(4,1)S(1)} %fusion.2, bf16[512,2048]{1,0:T(8,128)(2,1)} %all-gather.8.cloned.1.call-done), kind=kOutput, calls=%fused_computation.2 | convolution fusion | flops 4299161600 | bytes 11534336 | tf_op jit(solution)/shard_map/ts,td->sd/dot_general | solution.py:196
  142.6 5.0 %all-to-all-start.2 = ((bf16[32,64,2048]{2,1,0:T(8,128)(2,1)}), bf16[32,64,2048]{2,1,0:T(8,128)(2,1)}, u32[]{:S(2)}, u32[]{:S(2)}) async-start(bf16[32,64,2048]{2,1,0:T(8,128)(2,1)} %bitcast.150), calls=%async_computation.3 | async-start | bytes 16777216 | tf_op jit(solution)/shard_map/all_to_all | solution.py:209
  147.7 50.4 %all-gather.6.cloned.1.call-done = bf16[128,16,2048]{2,1,0:T(8,128)(2,1)} async-done(((bf16[32,16,2048]{2,1,0:T(8,128)(2,1)}), bf16[128,16,2048]{2,1,0:T(8,128)(2,1)}) %all-gather.6.cloned.1.call-update) | async-done | bytes 8388624 | tf_op jit(solution)/shard_map/all_gather | solution.py:216
  198.1 6.5 %fusion.24 = f32[2048,352]{0,1:T(8,128)S(1)} fusion(bf16[2048,2048]{1,0:T(8,128)(2,1)} %bitcast.163, bf16[2,352,2048]{2,1,0:T(8,128)(2,1)} %param.28), kind=kOutput, calls=%fused_computation.41 | convolution fusion | flops 2952790016 | bytes 12713984 | tf_op jit(solution)/shard_map/td,fd->tf/dot_general | solution.py:88
  205.2 3.5 fusion.3
  208.7 6.9 %convolution_convert_fusion.2 = bf16[2048,2048]{1,0:T(8,128)(2,1)} fusion(bf16[2048,352]{0,1:T(8,128)(2,1)S(1)} %fusion.3, bf16[2,352,2048]{2,1,0:T(8,128)(2,1)S(1)} %copy-done.37), kind=kOutput, calls=%fused_computation.3 | convolution fusion | flops 2956984320 | bytes 11272192 | tf_op jit(solution)/shard_map/dot_general | solution.py:91
  215.6 37.9 %all-to-all-done.2 = bf16[32,64,2048]{2,1,0:T(8,128)(2,1)} async-done(((bf16[32,64,2048]{2,1,0:T(8,128)(2,1)}), bf16[32,64,2048]{2,1,0:T(8,128)(2,1)}, u32[]{:S(2)}, u32[]{:S(2)}) %all-to-all-start.2) | async-done | bytes 8388640 | tf_op jit(solution)/shard_map/all_to_all | solution.py:209
  253.5 6.4 %fusion.20 = f32[2048,352]{0,1:T(8,128)S(1)} fusion(bf16[2048,2048]{1,0:T(8,128)(2,1)} %bitcast.29, bf16[2,352,2048]{2,1,0:T(8,128)(2,1)} %param.28), kind=kOutput, calls=%fused_computation.37 | convolution fusion | flops 2952790016 | bytes 12713984 | tf_op jit(solution)/shard_map/td,fd->tf/dot_general | solution.py:88
  260.0 7.2 %fusion.4 = bf16[2048,352]{0,1:T(8,128)(2,1)S(1)} fusion(bf16[2048,2048]{1,0:T(8,128)(2,1)} %bitcast.29, f32[2048,352]{0,1:T(8,128)S(1)} %fusion.20, bf16[2,352,2048]{2,1,0:T(8,128)(2,1)S(1)} %copy-done.36), kind=kOutput, calls=%fused_computation.16 | convolution fusion | flops 2957115392 | bytes 14155776 | tf_op jit(solution)/shard_map/td,fd->tf/dot_general | solution.py:89
  267.2 7.1 %convolution_convert_fusion = bf16[2048,2048]{1,0:T(8,128)(2,1)} fusion(bf16[2048,352]{0,1:T(8,128)(2,1)S(1)} %fusion.4, bf16[2,352,2048]{2,1,0:T(8,128)(2,1)S(1)} %copy-done.38), kind=kOutput, calls=%fused_computation.1 | convolution fusion | flops 2956984320 | bytes 11272192 | tf_op jit(solution)/shard_map/dot_general | solution.py:91
  274.3 5.1 %all-to-all-start.3 = ((bf16[32,64,2048]{2,1,0:T(8,128)(2,1)}), bf16[32,64,2048]{2,1,0:T(8,128)(2,1)}, u32[]{:S(2)}, u32[]{:S(2)}) async-start(bf16[32,64,2048]{2,1,0:T(8,128)(2,1)} %bitcast.151), calls=%async_computation.4 | async-start | bytes 16777216 | tf_op jit(solution)/shard_map/all_to_all | solution.py:227
  279.6 3.0 fusion.110
  282.7 5.6 %convolution_convert_fusion.3 = bf16[512,2048]{1,0:T(8,128)(2,1)} fusion(bf16[352,2048]{1,0:T(8,128)(2,1)S(1)} %copy-done, bf16[512,2048]{1,0:T(8,128)(2,1)} %all-gather.8.cloned.1.call-done, bf16[352,2048]{1,0:T(8,128)(2,1)} %param.32, f32[512,352]{0,1:T(8,128)S(1)} %fusion.110), kind=kOutput, calls=%fused_computation.11 | convolution fusion | flops 1478524928 | bytes 7798784 | tf_op jit(solution)/shard_map/dot_general | solution.py:91
  288.3 97.0 %all-to-all-done.3 = bf16[32,64,2048]{2,1,0:T(8,128)(2,1)} async-done(((bf16[32,64,2048]{2,1,0:T(8,128)(2,1)}), bf16[32,64,2048]{2,1,0:T(8,128)(2,1)}, u32[]{:S(2)}, u32[]{:S(2)}) %all-to-all-start.3) | async-done | bytes 8388640 | tf_op jit(solution)/shard_map/all_to_all | solution.py:227
  385.3 9.5 %fusion = bf16[512,2048]{1,0:T(8,128)(2,1)} fusion(bf16[512,2048]{1,0:T(8,128)(2,1)} %convolution_convert_fusion.3, bf16[32,64,2048]{2,1,0:T(8,128)(2,1)} %all-to-all-done.3, bf16[512,32]{0,1:T(8,128)(2,1)S(1)} %select_reduce_fusion, s32[512,32]{0,1:T(8,128)S(1)} %copy-done.16, pred[512,32]{0,1:T(8,128)(4,1)S(1)} %copy-done.12), kind=kOutput, calls=%fused_computation.5 | convolution fusion | flops 4301258752 | bytes 12697600 | tf_op jit(solution)/shard_map/dot_general | solution.py:239
  395.0 4.8 %all-to-all-start.1 = ((bf16[32,16,2048]{2,1,0:T(8,128)(2,1)}), bf16[32,16,2048]{2,1,0:T(8,128)(2,1)}, u32[]{:S(2)}, u32[]{:S(2)}) async-start(bf16[32,16,2048]{2,1,0:T(8,128)(2,1)} %bitcast.155), calls=%async_computation.2 | async-start | bytes 4194304 | tf_op jit(solution)/shard_map/all_to_all | solution.py:234
  399.8 20.5 %reduce-scatter.5.cloned.1.call-done = bf16[1,128,2048]{2,1,0:T(8,128)(2,1)} async-done(((bf16[4,128,2048]{2,1,0:T(8,128)(2,1)}), bf16[1,128,2048]{2,1,0:T(8,128)(2,1)}) %reduce-scatter.5.cloned.1.call-update) | async-done | bytes 524304 | tf_op jit(solution)/shard_map/reduce_scatter | solution.py:244
  420.3 9.5 %all-to-all-done.1 = bf16[32,16,2048]{2,1,0:T(8,128)(2,1)} async-done(((bf16[32,16,2048]{2,1,0:T(8,128)(2,1)}), bf16[32,16,2048]{2,1,0:T(8,128)(2,1)}, u32[]{:S(2)}, u32[]{:S(2)}) %all-to-all-start.1) | async-done | bytes 2097184 | tf_op jit(solution)/shard_map/all_to_all | solution.py:234
  429.8 3.0 fusion.9
  (138 shorter events, 15.1 us)
Async XLA Ops:
  6.5 276.1 %copy-start = (bf16[352,2048]{1,0:T(8,128)(2,1)S(1)}, bf16[352,2048]{1,0:T(8,128)(2,1)}, u32[]{:S(2)}) copy-start(bf16[352,2048]{1,0:T(8,128)(2,1)} %param.33) | copy-start | bytes 4325380
  6.5 2.6 copy-start.32
  6.5 2.8 copy-start.4
  6.5 53.4 %all-gather.4.cloned.1.call-start = ((), (), s32[]{:S(2)}) async-start(), calls=%async_computation.6 | async-start | bytes 5242880 | tf_op jit(solution)/shard_map/all_gather | solution.py:128
  6.5 3.2 copy-start.31
  9.0 3.0 copy-start.30
  9.0 4.1 copy-start.33
  9.1 125.3 %all-gather.8.cloned.1.call-start = ((), (), s32[]{:S(2)}) async-start(), calls=%async_computation.9 | async-start | bytes 2621440 | tf_op jit(solution)/shard_map/all_gather | solution.py:161
  9.8 5.3 %copy-start.1 = (bf16[2,64,4,4,128]{4,3,2,1,0:T(4,128)(2,1)}, bf16[2,64,4,4,128]{4,3,2,1,0:T(4,128)(2,1)S(1)}, u32[]{:S(2)}) copy-start(bf16[2,64,4,4,128]{4,3,2,1,0:T(4,128)(2,1)S(1)} %reshape.106) | copy-start | bytes 1572868
  62.9 3.8 copy-start.2
  66.8 2.7 copy-start.5
  72.8 4.8 %copy-start.23 = (f32[2048]{0:T(1024)S(1)}, f32[2048]{0:T(1024)}, u32[]{:S(2)}) copy-start(f32[2048]{0:T(1024)} %convert_element_type.114) | copy-start | bytes 24580
  78.6 119.5 %all-gather.6.cloned.1.call-start = ((), (), s32[]{:S(2)}) async-start(), calls=%async_computation.7 | async-start | bytes 10485760 | tf_op jit(solution)/shard_map/all_gather | solution.py:216
  142.6 110.9 %all-to-all-start.2 = ((bf16[32,64,2048]{2,1,0:T(8,128)(2,1)}), bf16[32,64,2048]{2,1,0:T(8,128)(2,1)}, u32[]{:S(2)}, u32[]{:S(2)}) async-start(bf16[32,64,2048]{2,1,0:T(8,128)(2,1)} %bitcast.150), calls=%async_computation.3 | async-start | bytes 16777216 | tf_op jit(solution)/shard_map/all_to_all | solution.py:209
  147.6 247.3 %reduce-scatter.3.cloned.1.call-start = ((), (), s32[]{:S(2)}) async-start(), calls=%async_computation.8 | async-start | bytes 10485760 | tf_op jit(solution)/shard_map/reduce_scatter | solution.py:221
  198.1 6.5 %copy-start.34 = (bf16[128,16,2048]{2,1,0:T(8,128)(2,1)S(1)}, bf16[128,16,2048]{2,1,0:T(8,128)(2,1)}, u32[]{:S(2)}) copy-start(bf16[128,16,2048]{2,1,0:T(8,128)(2,1)} %all-gather.6.cloned.1.call-done) | copy-start | bytes 25165828
  198.1 7.1 %copy-start.35 = (bf16[2,352,2048]{2,1,0:T(8,128)(2,1)S(1)}, bf16[2,352,2048]{2,1,0:T(8,128)(2,1)}, u32[]{:S(2)}) copy-start(bf16[2,352,2048]{2,1,0:T(8,128)(2,1)} %param.29) | copy-start | bytes 8650756
  205.2 3.5 copy-start.37
  253.5 6.4 %copy-start.36 = (bf16[2,352,2048]{2,1,0:T(8,128)(2,1)S(1)}, bf16[2,352,2048]{2,1,0:T(8,128)(2,1)}, u32[]{:S(2)}) copy-start(bf16[2,352,2048]{2,1,0:T(8,128)(2,1)} %param.29) | copy-start | bytes 8650756
  260.0 7.3 %copy-start.38 = (bf16[2,352,2048]{2,1,0:T(8,128)(2,1)S(1)}, bf16[2,352,2048]{2,1,0:T(8,128)(2,1)}, u32[]{:S(2)}) copy-start(bf16[2,352,2048]{2,1,0:T(8,128)(2,1)} %param.30) | copy-start | bytes 8650756
  274.3 5.2 %copy-start.8 = (f32[512,12]{0,1:T(8,128)S(1)}, f32[512,12]{0,1:T(8,128)}, u32[]{:S(2)}) copy-start(f32[512,12]{0,1:T(8,128)} %copy-done.7) | copy-start | bytes 73732
  274.3 5.2 %copy-start.22 = (pred[512,6]{0,1:T(8,128)(4,1)S(1)}, pred[512,6]{0,1:T(8,128)(4,1)}, u32[]{:S(2)}) copy-start(pred[512,6]{0,1:T(8,128)(4,1)} %copy-done.21) | copy-start | bytes 9220
  274.3 111.0 %all-to-all-start.3 = ((bf16[32,64,2048]{2,1,0:T(8,128)(2,1)}), bf16[32,64,2048]{2,1,0:T(8,128)(2,1)}, u32[]{:S(2)}, u32[]{:S(2)}) async-start(bf16[32,64,2048]{2,1,0:T(8,128)(2,1)} %bitcast.151), calls=%async_computation.4 | async-start | bytes 16777216 | tf_op jit(solution)/shard_map/all_to_all | solution.py:227
  279.4 140.8 %reduce-scatter.5.cloned.1.call-start = ((), (), s32[]{:S(2)}) async-start(), calls=%async_computation.10 | async-start | bytes 2621440 | tf_op jit(solution)/shard_map/reduce_scatter | solution.py:244
  282.7 102.7 %copy-start.12 = (pred[512,32]{0,1:T(8,128)(4,1)S(1)}, pred[512,32]{0,1:T(8,128)(4,1)}, u32[]{:S(2)}) copy-start(pred[512,32]{0,1:T(8,128)(4,1)} %copy-done.11) | copy-start | bytes 49156
  282.7 102.7 %copy-start.16 = (s32[512,32]{0,1:T(8,128)S(1)}, s32[512,32]{0,1:T(8,128)}, u32[]{:S(2)}) copy-start(s32[512,32]{0,1:T(8,128)} %copy-done.15) | copy-start | bytes 196612
  394.9 4.8 %copy-start.20 = (s32[128,6]{0,1:T(8,128)S(1)}, s32[128,6]{0,1:T(8,128)}, u32[]{:S(2)}) copy-start(s32[128,6]{0,1:T(8,128)} %copy-done.19) | copy-start | bytes 9220
  394.9 4.8 %copy-start.26 = (f32[128,6]{0,1:T(8,128)S(1)}, f32[128,6]{0,1:T(8,128)}, u32[]{:S(2)}) copy-start(f32[128,6]{0,1:T(8,128)} %param.35) | copy-start | bytes 9220
  394.9 4.8 %copy-start.29 = (pred[128,6]{0,1:T(8,128)(4,1)S(1)}, pred[128,6]{0,1:T(8,128)(4,1)}, u32[]{:S(2)}) copy-start(pred[128,6]{0,1:T(8,128)(4,1)} %copy-done.28) | copy-start | bytes 2308
  394.9 34.9 %copy-start.14 = (s32[128,32]{0,1:T(8,128)S(1)}, s32[128,32]{0,1:T(8,128)}, u32[]{:S(2)}) copy-start(s32[128,32]{0,1:T(8,128)} %copy-done.13) | copy-start | bytes 49156
  394.9 34.9 %copy-start.18 = (pred[128,32]{0,1:T(8,128)(4,1)S(1)}, pred[128,32]{0,1:T(8,128)(4,1)}, u32[]{:S(2)}) copy-start(pred[128,32]{0,1:T(8,128)(4,1)} %copy-done.17) | copy-start | bytes 12292
  395.0 34.9 %all-to-all-start.1 = ((bf16[32,16,2048]{2,1,0:T(8,128)(2,1)}), bf16[32,16,2048]{2,1,0:T(8,128)(2,1)}, u32[]{:S(2)}, u32[]{:S(2)}) async-start(bf16[32,16,2048]{2,1,0:T(8,128)(2,1)} %bitcast.155), calls=%async_computation.2 | async-start | bytes 4194304 | tf_op jit(solution)/shard_map/all_to_all | solution.py:234
  (15 other events, 14.4 us)
Sparse Core Ops, SparseCore 0:
  9.2 50.6 all-gather.3
  78.7 31.2 all-gather.7
  118.2 79.8 all-gather.5
  215.7 81.4 reduce-scatter.2
  395.0 25.2 reduce-scatter.4

commit v3 on v2

--- a/solution.py
+++ b/solution.py
@@ -112,6 +112,15 @@
     expert_weights,
 ):
     tok_rows, model_width = hidden.shape
+    group_picks = lax.all_gather(
+        jnp.concatenate([expert_ids.astype(jnp.float32), expert_weights], axis=1),
+        "dp",
+        axis=0,
+        tiled=True,
+    )
+    group_picks, queries, draft_entries = lax.optimization_barrier(
+        (group_picks, queries, draft_entries)
+    )
     local_requests, draft_nodes = parents.shape
     group_size = HEADS // KVH
     query_heads = queries.reshape(local_requests, draft_nodes, KVH, group_size, HD)
@@ -126,12 +135,6 @@
         draft_values,
     )
     both_pools = lax.all_gather(jnp.stack([key_pool, value_pool]), "dp", axis=1, tiled=True)
-    group_picks = lax.all_gather(
-        jnp.concatenate([expert_ids.astype(jnp.float32), expert_weights], axis=1),
-        "dp",
-        axis=0,
-        tiled=True,
-    )
     final_top, final_total, final_sum = pool_state(
         tree_state,
         query_heads,

time: 440 us -> 428 us (0.973)
  waiting for transfers between devices: 260 us -> 247 us
    all_gather x1, waiting for transfers between devices: 44.9 us -> 31 us  [on_device(): lax.all_gather(jnp.stack([key_pool, value_pool]), 'dp', axis=1, tiled=True)]
    all_to_all x1, waiting for transfers between devices: 37.9 us -> 25.9 us  [on_device(): lax.all_to_all(far_out.reshape(column_count, far_cap, model_width), 'exp'...]
    all_gather x1, waiting for transfers between devices: 50.4 us -> 62.4 us  [on_device(): lax.all_gather(near_arrived, 'dp', axis=0, tiled=True)]
  transfers between devices with their start and end apart: 8 -> 8, of which waited for: 6 -> 6; matrix products, arithmetic and copies ran while one was open for 17% -> 18% of each run, Pallas kernels for 0% -> 0%
where the time goes in v3:
time: 428 us; the launch traced here: 427 us
  waiting for transfers between devices  247 us (58%)
  matrix products  79.9 us (19%)
  blocking collectives  48.8 us (11%)
  starting transfers between devices  15.1 us (4%)
  local copies, waits for them, and re-layouts  13.8 us (3%)
  between operations  13.8 us (3%)
  other arithmetic  9.05 us (2%)
    all_to_all x1, waiting for transfers between devices, on_device(): lax.all_to_all(far_terms.astype(jnp.bfloat16).reshape(column_count, far_c...  97.2 us
    all_gather x1, waiting for transfers between devices, on_device(): lax.all_gather(near_arrived, 'dp', axis=0, tiled=True)  62.4 us
    all_to_all x1, blocking collectives, on_device(): lax.all_to_all(near_out.reshape(column_count, near_cap, model_width), 'ex...  35.6 us
    all_gather x1, waiting for transfers between devices, on_device(): lax.all_gather(jnp.stack([key_pool, value_pool]), 'dp', axis=1, tiled=True)  31 us
    all_to_all x1, waiting for transfers between devices, on_device(): lax.all_to_all(far_out.reshape(column_count, far_cap, model_width), 'exp'...  25.9 us
    reduce_scatter x1, waiting for transfers between devices, on_device(): lax.psum_scatter(far_part.astype(jnp.bfloat16).reshape(row_count, tok_row...  20.9 us
    dot_general x3, matrix products, shared_block(): return jnp.dot(inner, down_rows, preferred_element_type=jnp.float32)  19.6 us
    dot_general x3, matrix products, shared_block(): jnp.einsum('td,fd->tf', tokens, gate_rows, preferred_element_type=jnp.flo...  15.6 us
  transfers between devices with their start and end apart: 8, of which 6 were waited for; matrix products, arithmetic and copies ran while one was open for 18% of the time, Pallas kernels for 0%

profile of v3, /device:TPU:0, one launch (start us, length us, event | category | flops | bytes accessed | tf_op | source)
XLA Modules:
  0.0 427.0 jit_solution(6823115987195912476)
XLA Ops:
  6.6 2.5 pad_maximum_fusion
  9.8 13.2 %all_gather.12 = f32[512,12]{0,1:T(8,128)} all-gather(f32[128,12]{0,1:T(8,128)S(1)} %pad_maximum_fusion.1), channel_id=1, replica_groups=mesh['dp'=4,'exp'=32] {'dp'}, dimensions={0}, use_global_device_ids=true | all-gather | bytes 30720 | tf_op jit(solution)/shard_map/all_gather | solution.py:115
  27.7 1.3 fusion.107
  28.9 31.0 %all-gather.4.cloned.1.call-done = bf16[2,32,64,512]{3,2,1,0:T(8,128)(2,1)} async-done(((bf16[2,8,64,512]{3,2,1,0:T(8,128)(2,1)}), bf16[2,32,64,512]{3,2,1,0:T(8,128)(2,1)}) %all-gather.4.cloned.1.call-update) | async-done | bytes 4194320 | tf_op jit(solution)/shard_map/all_gather | solution.py:137
  60.0 2.9 gather_fusion
  63.9 2.0 reshape_squeeze.14
  66.8 1.7 bitcast_reduce_fusion
  70.5 1.2 fusion.38
  72.8 4.8 %multiply_reduce_fusion = (f32[128]{0:T(128)S(1)}, f32[128,2048]{1,0:T(8,128)S(1)}) fusion(bf16[128,2048]{1,0:T(8,128)(2,1)S(1)} %convert_element_type.110, bf16[2048,2048]{1,0:T(8,128)(2,1)} %param.26, bf16[128,2048]{1,0:T(8,128)(2,1)S(1)} %copy-done.3), kind=kOutput, calls=%fused_computation.74 | convolution fusion | flops 1075314560 | bytes 10486272 | tf_op jit(solution)/shard_map/dot_general | solution.py:152
  77.6 1.0 multiply_convert_fusion
  80.7 1.7 convolution_convert_fusion.4
  82.4 35.6 %all_to_all.20 = bf16[32,16,2048]{2,1,0:T(8,128)(2,1)} all-to-all(bf16[32,16,2048]{2,1,0:T(8,128)(2,1)S(1)} %bitcast.152), channel_id=1, replica_groups=mesh['dp'=4,'exp'=32] {'exp'}, dimensions={0} | all-to-all | bytes 4194304 | tf_op jit(solution)/shard_map/all_to_all | solution.py:205
  120.6 1.6 fusion.2
  122.2 8.4 %convolution_convert_fusion.1 = bf16[2048,2048]{1,0:T(8,128)(2,1)} fusion(pred[512,2048]{0,1:T(32,128)(4,1)S(1)} %fusion.2, bf16[512,2048]{1,0:T(8,128)(2,1)} %all-gather.8.cloned.1.call-done), kind=kOutput, calls=%fused_computation.2 | convolution fusion | flops 4299161600 | bytes 11534336 | tf_op jit(solution)/shard_map/ts,td->sd/dot_general | solution.py:199
  130.6 5.0 %all-to-all-start.2 = ((bf16[32,64,2048]{2,1,0:T(8,128)(2,1)}), bf16[32,64,2048]{2,1,0:T(8,128)(2,1)}, u32[]{:S(2)}, u32[]{:S(2)}) async-start(bf16[32,64,2048]{2,1,0:T(8,128)(2,1)} %bitcast.150), calls=%async_computation.3 | async-start | bytes 16777216 | tf_op jit(solution)/shard_map/all_to_all | solution.py:212
  135.7 62.4 %all-gather.6.cloned.1.call-done = bf16[128,16,2048]{2,1,0:T(8,128)(2,1)} async-done(((bf16[32,16,2048]{2,1,0:T(8,128)(2,1)}), bf16[128,16,2048]{2,1,0:T(8,128)(2,1)}) %all-gather.6.cloned.1.call-update) | async-done | bytes 8388624 | tf_op jit(solution)/shard_map/all_gather | solution.py:219
  198.1 6.5 %fusion.24 = f32[2048,352]{0,1:T(8,128)S(1)} fusion(bf16[2048,2048]{1,0:T(8,128)(2,1)} %bitcast.163, bf16[2,352,2048]{2,1,0:T(8,128)(2,1)} %param.28), kind=kOutput, calls=%fused_computation.41 | convolution fusion | flops 2952790016 | bytes 12713984 | tf_op jit(solution)/shard_map/td,fd->tf/dot_general | solution.py:88
  205.1 3.5 fusion.3
  208.7 6.9 %convolution_convert_fusion.2 = bf16[2048,2048]{1,0:T(8,128)(2,1)} fusion(bf16[2048,352]{0,1:T(8,128)(2,1)S(1)} %fusion.3, bf16[2,352,2048]{2,1,0:T(8,128)(2,1)S(1)} %copy-done.38), kind=kOutput, calls=%fused_computation.3 | convolution fusion | flops 2956984320 | bytes 11272192 | tf_op jit(solution)/shard_map/dot_general | solution.py:91
  215.6 25.9 %all-to-all-done.2 = bf16[32,64,2048]{2,1,0:T(8,128)(2,1)} async-done(((bf16[32,64,2048]{2,1,0:T(8,128)(2,1)}), bf16[32,64,2048]{2,1,0:T(8,128)(2,1)}, u32[]{:S(2)}, u32[]{:S(2)}) %all-to-all-start.2) | async-done | bytes 8388640 | tf_op jit(solution)/shard_map/all_to_all | solution.py:212
  241.5 6.2 %fusion.20 = f32[2048,352]{0,1:T(8,128)S(1)} fusion(bf16[2048,2048]{1,0:T(8,128)(2,1)} %bitcast.29, bf16[2,352,2048]{2,1,0:T(8,128)(2,1)} %param.28), kind=kOutput, calls=%fused_computation.37 | convolution fusion | flops 2952790016 | bytes 12713984 | tf_op jit(solution)/shard_map/td,fd->tf/dot_general | solution.py:88
  247.7 7.1 %fusion.4 = bf16[2048,352]{0,1:T(8,128)(2,1)S(1)} fusion(bf16[2048,2048]{1,0:T(8,128)(2,1)} %bitcast.29, f32[2048,352]{0,1:T(8,128)S(1)} %fusion.20, bf16[2,352,2048]{2,1,0:T(8,128)(2,1)S(1)} %copy-done.37), kind=kOutput, calls=%fused_computation.16 | convolution fusion | flops 2957115392 | bytes 14155776 | tf_op jit(solution)/shard_map/td,fd->tf/dot_general | solution.py:89
  254.8 7.1 %convolution_convert_fusion = bf16[2048,2048]{1,0:T(8,128)(2,1)} fusion(bf16[2048,352]{0,1:T(8,128)(2,1)S(1)} %fusion.4, bf16[2,352,2048]{2,1,0:T(8,128)(2,1)S(1)} %copy-done.39), kind=kOutput, calls=%fused_computation.1 | convolution fusion | flops 2956984320 | bytes 11272192 | tf_op jit(solution)/shard_map/dot_general | solution.py:91
  262.0 5.1 %all-to-all-start.3 = ((bf16[32,64,2048]{2,1,0:T(8,128)(2,1)}), bf16[32,64,2048]{2,1,0:T(8,128)(2,1)}, u32[]{:S(2)}, u32[]{:S(2)}) async-start(bf16[32,64,2048]{2,1,0:T(8,128)(2,1)} %bitcast.151), calls=%async_computation.4 | async-start | bytes 16777216 | tf_op jit(solution)/shard_map/all_to_all | solution.py:230
  267.3 2.9 fusion.108
  270.2 5.5 %convolution_convert_fusion.3 = bf16[512,2048]{1,0:T(8,128)(2,1)} fusion(bf16[352,2048]{1,0:T(8,128)(2,1)S(1)} %copy-done, bf16[512,2048]{1,0:T(8,128)(2,1)} %all-gather.8.cloned.1.call-done, bf16[352,2048]{1,0:T(8,128)(2,1)} %param.32, f32[512,352]{0,1:T(8,128)S(1)} %fusion.108), kind=kOutput, calls=%fused_computation.11 | convolution fusion | flops 1478524928 | bytes 7798784 | tf_op jit(solution)/shard_map/dot_general | solution.py:91
  275.8 97.2 %all-to-all-done.3 = bf16[32,64,2048]{2,1,0:T(8,128)(2,1)} async-done(((bf16[32,64,2048]{2,1,0:T(8,128)(2,1)}), bf16[32,64,2048]{2,1,0:T(8,128)(2,1)}, u32[]{:S(2)}, u32[]{:S(2)}) %all-to-all-start.3) | async-done | bytes 8388640 | tf_op jit(solution)/shard_map/all_to_all | solution.py:230
  373.0 9.5 %fusion = bf16[512,2048]{1,0:T(8,128)(2,1)} fusion(bf16[512,2048]{1,0:T(8,128)(2,1)} %convolution_convert_fusion.3, bf16[32,64,2048]{2,1,0:T(8,128)(2,1)} %all-to-all-done.3, bf16[512,32]{0,1:T(8,128)(2,1)S(1)} %select_reduce_fusion, s32[512,32]{0,1:T(8,128)S(1)} %copy-done.16, pred[512,32]{0,1:T(8,128)(4,1)S(1)} %copy-done.12), kind=kOutput, calls=%fused_computation.5 | convolution fusion | flops 4301258752 | bytes 12697600 | tf_op jit(solution)/shard_map/dot_general | solution.py:242
  382.6 4.8 %all-to-all-start.1 = ((bf16[32,16,2048]{2,1,0:T(8,128)(2,1)}), bf16[32,16,2048]{2,1,0:T(8,128)(2,1)}, u32[]{:S(2)}, u32[]{:S(2)}) async-start(bf16[32,16,2048]{2,1,0:T(8,128)(2,1)} %bitcast.155), calls=%async_computation.2 | async-start | bytes 4194304 | tf_op jit(solution)/shard_map/all_to_all | solution.py:237
  387.5 20.9 %reduce-scatter.5.cloned.1.call-done = bf16[1,128,2048]{2,1,0:T(8,128)(2,1)} async-done(((bf16[4,128,2048]{2,1,0:T(8,128)(2,1)}), bf16[1,128,2048]{2,1,0:T(8,128)(2,1)}) %reduce-scatter.5.cloned.1.call-update) | async-done | bytes 524304 | tf_op jit(solution)/shard_map/reduce_scatter | solution.py:247
  408.4 9.1 %all-to-all-done.1 = bf16[32,16,2048]{2,1,0:T(8,128)(2,1)} async-done(((bf16[32,16,2048]{2,1,0:T(8,128)(2,1)}), bf16[32,16,2048]{2,1,0:T(8,128)(2,1)}, u32[]{:S(2)}, u32[]{:S(2)}) %all-to-all-start.1) | async-done | bytes 2097184 | tf_op jit(solution)/shard_map/all_to_all | solution.py:237
  417.5 3.0 fusion.9
  (140 shorter events, 15.7 us)
Async XLA Ops:
  6.5 263.7 %copy-start = (bf16[352,2048]{1,0:T(8,128)(2,1)S(1)}, bf16[352,2048]{1,0:T(8,128)(2,1)}, u32[]{:S(2)}) copy-start(bf16[352,2048]{1,0:T(8,128)(2,1)} %param.33) | copy-start | bytes 4325380
  6.5 16.4 %copy-start.4 = (bf16[128,2048]{1,0:T(8,128)(2,1)S(1)}, bf16[128,2048]{1,0:T(8,128)(2,1)}, u32[]{:S(2)}) copy-start(bf16[128,2048]{1,0:T(8,128)(2,1)} %param.19) | copy-start | bytes 1572868
  6.5 53.4 %all-gather.4.cloned.1.call-start = ((), (), s32[]{:S(2)}) async-start(), calls=%async_computation.6 | async-start | bytes 5242880 | tf_op jit(solution)/shard_map/all_gather | solution.py:137
  6.6 16.8 %copy-start.6 = (bf16[2,128,512]{2,1,0:T(8,128)(2,1)S(1)}, bf16[2,128,512]{2,1,0:T(8,128)(2,1)}, u32[]{:S(2)}) copy-start(bf16[2,128,512]{2,1,0:T(8,128)(2,1)} %param.20) | copy-start | bytes 786436
  6.6 16.9 %copy-start.32 = (s32[2,64]{1,0:T(2,128)S(1)}, s32[2,64]{1,0:T(2,128)}, u32[]{:S(2)}) copy-start(s32[2,64]{1,0:T(2,128)} %param.25) | copy-start | bytes 1540
  9.1 15.8 %copy-start.33 = (s32[2,4]{1,0:T(2,128)S(1)}, s32[2,4]{1,0:T(2,128)}, u32[]{:S(2)}) copy-start(s32[2,4]{1,0:T(2,128)} %param.23) | copy-start | bytes 100
  9.1 16.8 %copy-start.31 = (bf16[2048]{0:T(1024)(128)(2,1)S(1)}, bf16[2048]{0:T(1024)(128)(2,1)}, u32[]{:S(2)}) copy-start(bf16[2048]{0:T(1024)(128)(2,1)} %param.27) | copy-start | bytes 12292
  9.1 17.9 %copy-start.34 = (s32[2]{0:T(128)S(1)}, s32[2]{0:T(128)}, u32[]{:S(2)}) copy-start(s32[2]{0:T(128)} %param.24) | copy-start | bytes 28
  9.1 113.1 %all-gather.8.cloned.1.call-start = ((), (), s32[]{:S(2)}) async-start(), calls=%async_computation.9 | async-start | bytes 2621440 | tf_op jit(solution)/shard_map/all_gather | solution.py:164
  23.4 5.6 %copy-start.1 = (bf16[2,64,4,4,128]{4,3,2,1,0:T(4,128)(2,1)}, bf16[2,64,4,4,128]{4,3,2,1,0:T(4,128)(2,1)S(1)}, u32[]{:S(2)}) copy-start(bf16[2,64,4,4,128]{4,3,2,1,0:T(4,128)(2,1)S(1)} %reshape.106) | copy-start | bytes 1572868
  63.0 3.8 copy-start.2
  72.8 4.8 %copy-start.23 = (f32[2048]{0:T(1024)S(1)}, f32[2048]{0:T(1024)}, u32[]{:S(2)}) copy-start(f32[2048]{0:T(1024)} %convert_element_type.115) | copy-start | bytes 24580
  78.6 119.4 %all-gather.6.cloned.1.call-start = ((), (), s32[]{:S(2)}) async-start(), calls=%async_computation.7 | async-start | bytes 10485760 | tf_op jit(solution)/shard_map/all_gather | solution.py:219
  130.6 110.9 %all-to-all-start.2 = ((bf16[32,64,2048]{2,1,0:T(8,128)(2,1)}), bf16[32,64,2048]{2,1,0:T(8,128)(2,1)}, u32[]{:S(2)}, u32[]{:S(2)}) async-start(bf16[32,64,2048]{2,1,0:T(8,128)(2,1)} %bitcast.150), calls=%async_computation.3 | async-start | bytes 16777216 | tf_op jit(solution)/shard_map/all_to_all | solution.py:212
  135.6 246.9 %reduce-scatter.3.cloned.1.call-start = ((), (), s32[]{:S(2)}) async-start(), calls=%async_computation.8 | async-start | bytes 10485760 | tf_op jit(solution)/shard_map/reduce_scatter | solution.py:224
  198.0 6.5 %copy-start.35 = (bf16[128,16,2048]{2,1,0:T(8,128)(2,1)S(1)}, bf16[128,16,2048]{2,1,0:T(8,128)(2,1)}, u32[]{:S(2)}) copy-start(bf16[128,16,2048]{2,1,0:T(8,128)(2,1)} %all-gather.6.cloned.1.call-done) | copy-start | bytes 25165828
  198.0 7.1 %copy-start.36 = (bf16[2,352,2048]{2,1,0:T(8,128)(2,1)S(1)}, bf16[2,352,2048]{2,1,0:T(8,128)(2,1)}, u32[]{:S(2)}) copy-start(bf16[2,352,2048]{2,1,0:T(8,128)(2,1)} %param.29) | copy-start | bytes 8650756
  205.1 3.5 copy-start.38
  241.5 6.2 %copy-start.37 = (bf16[2,352,2048]{2,1,0:T(8,128)(2,1)S(1)}, bf16[2,352,2048]{2,1,0:T(8,128)(2,1)}, u32[]{:S(2)}) copy-start(bf16[2,352,2048]{2,1,0:T(8,128)(2,1)} %param.29) | copy-start | bytes 8650756
  247.7 7.1 %copy-start.39 = (bf16[2,352,2048]{2,1,0:T(8,128)(2,1)S(1)}, bf16[2,352,2048]{2,1,0:T(8,128)(2,1)}, u32[]{:S(2)}) copy-start(bf16[2,352,2048]{2,1,0:T(8,128)(2,1)} %param.30) | copy-start | bytes 8650756
  262.0 5.2 %copy-start.8 = (f32[512,12]{0,1:T(8,128)S(1)}, f32[512,12]{0,1:T(8,128)}, u32[]{:S(2)}) copy-start(f32[512,12]{0,1:T(8,128)} %all_gather.12) | copy-start | bytes 73732
  262.0 5.2 %copy-start.22 = (pred[512,6]{0,1:T(8,128)(4,1)S(1)}, pred[512,6]{0,1:T(8,128)(4,1)}, u32[]{:S(2)}) copy-start(pred[512,6]{0,1:T(8,128)(4,1)} %copy-done.21) | copy-start | bytes 9220
  262.0 111.0 %all-to-all-start.3 = ((bf16[32,64,2048]{2,1,0:T(8,128)(2,1)}), bf16[32,64,2048]{2,1,0:T(8,128)(2,1)}, u32[]{:S(2)}, u32[]{:S(2)}) async-start(bf16[32,64,2048]{2,1,0:T(8,128)(2,1)} %bitcast.151), calls=%async_computation.4 | async-start | bytes 16777216 | tf_op jit(solution)/shard_map/all_to_all | solution.py:230
  267.1 141.3 %reduce-scatter.5.cloned.1.call-start = ((), (), s32[]{:S(2)}) async-start(), calls=%async_computation.10 | async-start | bytes 2621440 | tf_op jit(solution)/shard_map/reduce_scatter | solution.py:247
  270.2 102.8 %copy-start.12 = (pred[512,32]{0,1:T(8,128)(4,1)S(1)}, pred[512,32]{0,1:T(8,128)(4,1)}, u32[]{:S(2)}) copy-start(pred[512,32]{0,1:T(8,128)(4,1)} %copy-done.11) | copy-start | bytes 49156
  270.2 102.8 %copy-start.16 = (s32[512,32]{0,1:T(8,128)S(1)}, s32[512,32]{0,1:T(8,128)}, u32[]{:S(2)}) copy-start(s32[512,32]{0,1:T(8,128)} %copy-done.15) | copy-start | bytes 196612
  382.6 4.8 %copy-start.20 = (s32[128,6]{0,1:T(8,128)S(1)}, s32[128,6]{0,1:T(8,128)}, u32[]{:S(2)}) copy-start(s32[128,6]{0,1:T(8,128)} %get-tuple-element.22) | copy-start | bytes 9220
  382.6 4.8 %copy-start.27 = (f32[128,6]{0,1:T(8,128)S(1)}, f32[128,6]{0,1:T(8,128)}, u32[]{:S(2)}) copy-start(f32[128,6]{0,1:T(8,128)} %param.35) | copy-start | bytes 9220
  382.6 4.8 %copy-start.30 = (pred[128,6]{0,1:T(8,128)(4,1)S(1)}, pred[128,6]{0,1:T(8,128)(4,1)}, u32[]{:S(2)}) copy-start(pred[128,6]{0,1:T(8,128)(4,1)} %copy-done.29) | copy-start | bytes 2308
  382.6 34.9 %copy-start.14 = (s32[128,32]{0,1:T(8,128)S(1)}, s32[128,32]{0,1:T(8,128)}, u32[]{:S(2)}) copy-start(s32[128,32]{0,1:T(8,128)} %copy-done.13) | copy-start | bytes 49156
  382.6 34.9 %copy-start.18 = (pred[128,32]{0,1:T(8,128)(4,1)S(1)}, pred[128,32]{0,1:T(8,128)(4,1)}, u32[]{:S(2)}) copy-start(pred[128,32]{0,1:T(8,128)(4,1)} %copy-done.17) | copy-start | bytes 12292
  382.6 34.9 %all-to-all-start.1 = ((bf16[32,16,2048]{2,1,0:T(8,128)(2,1)}), bf16[32,16,2048]{2,1,0:T(8,128)(2,1)}, u32[]{:S(2)}, u32[]{:S(2)}) async-start(bf16[32,16,2048]{2,1,0:T(8,128)(2,1)} %bitcast.155), calls=%async_computation.2 | async-start | bytes 4194304 | tf_op jit(solution)/shard_map/all_to_all | solution.py:237
  (16 other events, 21.2 us)
Sparse Core Ops, SparseCore 0:
  9.2 50.6 all-gather.3
  78.7 31.1 all-gather.7
  118.1 79.8 all-gather.5
  215.7 81.4 reduce-scatter.2
  382.7 25.6 reduce-scatter.4

commit v4 on v3

--- a/solution.py
+++ b/solution.py
@@ -134,7 +134,23 @@
         tree_mask,
         draft_values,
     )
-    both_pools = lax.all_gather(jnp.stack([key_pool, value_pool]), "dp", axis=1, tiled=True)
+    own_pools = jnp.stack([key_pool, value_pool])
+    row_span = lax.axis_size("dp")
+    both_pools = jnp.concatenate(
+        [own_pools]
+        + [
+            lax.ppermute(
+                own_pools, "dp", [(i, (i + shift) % row_span) for i in range(row_span)]
+            )
+            for shift in range(1, row_span)
+        ],
+        axis=1,
+    )
+    pool_pages = key_pool.shape[0]
+    page_table = (
+        (lax.axis_index("dp") - page_table // pool_pages) % row_span * pool_pages
+        + page_table % pool_pages
+    )
     final_top, final_total, final_sum = pool_state(
         tree_state,
         query_heads,

time: 428 us -> 448 us (1.047)
  blocking collectives: 48.8 us -> 85 us
  waiting for transfers between devices: 247 us -> 216 us
  starting transfers between devices: 15.1 us -> 21 us
  other arithmetic: 9.05 us -> 14.8 us
    all_gather x1, blocking collectives: 13.2 us -> 48.4 us  [on_device(): lax.all_gather(jnp.concatenate([expert_ids.astype(jnp.float32), expert_we...]
    all_gather x1 -> x0, waiting for transfers between devices: 31 us -> none  [on_device(): lax.all_gather(jnp.stack([key_pool, value_pool]), 'dp', axis=1, tiled=True)]
    ppermute x0 -> x3, starting transfers between devices: none -> 5.94 us  [on_device(): lax.ppermute(own_pools, 'dp', [(i, (i + shift) % row_span) for i in range...]
  transfers between devices with their start and end apart: 8 -> 10, of which waited for: 6 -> 5; matrix products, arithmetic and copies ran while one was open for 18% -> 18% of each run, Pallas kernels for 0% -> 0%
where the time goes in v4:
time: 448 us; the launch traced here: 447 us
  waiting for transfers between devices  216 us (48%)
  blocking collectives  85 us (19%)
  matrix products  80.8 us (18%)
  starting transfers between devices  21 us (5%)
  local copies, waits for them, and re-layouts  16 us (4%)
  other arithmetic  14.8 us (3%)
  between operations  13.7 us (3%)
    all_to_all x1, waiting for transfers between devices, on_device(): lax.all_to_all(far_terms.astype(jnp.bfloat16).reshape(column_count, far_c...  97.2 us
    all_gather x1, waiting for transfers between devices, on_device(): lax.all_gather(near_arrived, 'dp', axis=0, tiled=True)  62.9 us
    all_gather x1, blocking collectives, on_device(): lax.all_gather(jnp.concatenate([expert_ids.astype(jnp.float32), expert_we...  48.4 us
    all_to_all x1, blocking collectives, on_device(): lax.all_to_all(near_out.reshape(column_count, near_cap, model_width), 'ex...  36.5 us
    all_to_all x1, waiting for transfers between devices, on_device(): lax.all_to_all(far_out.reshape(column_count, far_cap, model_width), 'exp'...  25.4 us
    reduce_scatter x1, waiting for transfers between devices, on_device(): lax.psum_scatter(far_part.astype(jnp.bfloat16).reshape(row_count, tok_row...  21.4 us
    dot_general x3, matrix products, shared_block(): return jnp.dot(inner, down_rows, preferred_element_type=jnp.float32)  19.6 us
    dot_general x3, matrix products, shared_block(): jnp.einsum('td,fd->tf', tokens, gate_rows, preferred_element_type=jnp.flo...  15.6 us
  transfers between devices with their start and end apart: 10, of which 5 were waited for; matrix products, arithmetic and copies ran while one was open for 18% of the time, Pallas kernels for 0%

profile of v4, /device:TPU:0, one launch (start us, length us, event | category | flops | bytes accessed | tf_op | source)
XLA Modules:
  0.0 446.9 jit_solution(18352173981653136302)
XLA Ops:
  6.6 2.4 pad_maximum_fusion.1
  9.0 1.7 collective-permute-start
  10.7 2.9 collective-permute-start.1
  17.8 48.4 %all_gather.9 = f32[512,12]{0,1:T(8,128)} all-gather(f32[128,12]{0,1:T(8,128)S(1)} %pad_maximum_fusion.2), channel_id=1, replica_groups=mesh['dp'=4,'exp'=32] {'dp'}, dimensions={0}, use_global_device_ids=true | all-gather | bytes 30720 | tf_op jit(solution)/shard_map/all_gather | solution.py:115
  66.2 2.2 reshape.106
  73.2 2.4 fusion.111
  75.6 3.6 pad_maximum_fusion
  79.3 2.9 gather_fusion
  83.2 2.0 reshape_squeeze.14
  86.1 1.7 bitcast_reduce_fusion
  92.0 4.8 %multiply_reduce_fusion = (f32[128]{0:T(128)S(1)}, f32[128,2048]{1,0:T(8,128)S(1)}) fusion(bf16[128,2048]{1,0:T(8,128)(2,1)S(1)} %convert_element_type.110, bf16[2048,2048]{1,0:T(8,128)(2,1)} %param.26, bf16[128,2048]{1,0:T(8,128)(2,1)S(1)} %copy-done.4), kind=kOutput, calls=%fused_computation.75 | convolution fusion | flops 1075314560 | bytes 10486272 | tf_op jit(solution)/shard_map/dot_general | solution.py:168
  99.8 1.7 convolution_convert_fusion.4
  101.6 36.5 %all_to_all.20 = bf16[32,16,2048]{2,1,0:T(8,128)(2,1)} all-to-all(bf16[32,16,2048]{2,1,0:T(8,128)(2,1)S(1)} %bitcast.152), channel_id=1, replica_groups=mesh['dp'=4,'exp'=32] {'exp'}, dimensions={0} | all-to-all | bytes 4194304 | tf_op jit(solution)/shard_map/all_to_all | solution.py:221
  142.2 8.3 %convolution_convert_fusion.1 = bf16[2048,2048]{1,0:T(8,128)(2,1)} fusion(pred[512,2048]{0,1:T(32,128)(4,1)S(1)} %fusion.2, bf16[512,2048]{1,0:T(8,128)(2,1)} %all-gather.5.cloned.1.call-done), kind=kOutput, calls=%fused_computation.2 | convolution fusion | flops 4299161600 | bytes 11534336 | tf_op jit(solution)/shard_map/ts,td->sd/dot_general | solution.py:215
  150.5 5.0 %all-to-all-start.2 = ((bf16[32,64,2048]{2,1,0:T(8,128)(2,1)}), bf16[32,64,2048]{2,1,0:T(8,128)(2,1)}, u32[]{:S(2)}, u32[]{:S(2)}) async-start(bf16[32,64,2048]{2,1,0:T(8,128)(2,1)} %bitcast.150), calls=%async_computation.3 | async-start | bytes 16777216 | tf_op jit(solution)/shard_map/all_to_all | solution.py:228
  155.6 62.9 %all-gather.3.cloned.1.call-done = bf16[128,16,2048]{2,1,0:T(8,128)(2,1)} async-done(((bf16[32,16,2048]{2,1,0:T(8,128)(2,1)}), bf16[128,16,2048]{2,1,0:T(8,128)(2,1)}) %all-gather.3.cloned.1.call-update) | async-done | bytes 8388624 | tf_op jit(solution)/shard_map/all_gather | solution.py:235
  218.4 6.5 %fusion.24 = f32[2048,352]{0,1:T(8,128)S(1)} fusion(bf16[2048,2048]{1,0:T(8,128)(2,1)} %bitcast.165, bf16[2,352,2048]{2,1,0:T(8,128)(2,1)} %param.28), kind=kOutput, calls=%fused_computation.42 | convolution fusion | flops 2952790016 | bytes 12713984 | tf_op jit(solution)/shard_map/td,fd->tf/dot_general | solution.py:88
  225.5 3.5 fusion.3
  229.0 6.9 %convolution_convert_fusion.2 = bf16[2048,2048]{1,0:T(8,128)(2,1)} fusion(bf16[2048,352]{0,1:T(8,128)(2,1)S(1)} %fusion.3, bf16[2,352,2048]{2,1,0:T(8,128)(2,1)S(1)} %copy-done.35), kind=kOutput, calls=%fused_computation.3 | convolution fusion | flops 2956984320 | bytes 11272192 | tf_op jit(solution)/shard_map/dot_general | solution.py:91
  236.0 25.4 %all-to-all-done.2 = bf16[32,64,2048]{2,1,0:T(8,128)(2,1)} async-done(((bf16[32,64,2048]{2,1,0:T(8,128)(2,1)}), bf16[32,64,2048]{2,1,0:T(8,128)(2,1)}, u32[]{:S(2)}, u32[]{:S(2)}) %all-to-all-start.2) | async-done | bytes 8388640 | tf_op jit(solution)/shard_map/all_to_all | solution.py:228
  261.4 6.2 %fusion.20 = f32[2048,352]{0,1:T(8,128)S(1)} fusion(bf16[2048,2048]{1,0:T(8,128)(2,1)} %bitcast.29, bf16[2,352,2048]{2,1,0:T(8,128)(2,1)} %param.28), kind=kOutput, calls=%fused_computation.38 | convolution fusion | flops 2952790016 | bytes 12713984 | tf_op jit(solution)/shard_map/td,fd->tf/dot_general | solution.py:88
  267.7 7.1 %fusion.4 = bf16[2048,352]{0,1:T(8,128)(2,1)S(1)} fusion(bf16[2048,2048]{1,0:T(8,128)(2,1)} %bitcast.29, f32[2048,352]{0,1:T(8,128)S(1)} %fusion.20, bf16[2,352,2048]{2,1,0:T(8,128)(2,1)S(1)} %copy-done.34), kind=kOutput, calls=%fused_computation.17 | convolution fusion | flops 2957115392 | bytes 14155776 | tf_op jit(solution)/shard_map/td,fd->tf/dot_general | solution.py:89
  274.7 7.1 %convolution_convert_fusion = bf16[2048,2048]{1,0:T(8,128)(2,1)} fusion(bf16[2048,352]{0,1:T(8,128)(2,1)S(1)} %fusion.4, bf16[2,352,2048]{2,1,0:T(8,128)(2,1)S(1)} %copy-done.36), kind=kOutput, calls=%fused_computation.1 | convolution fusion | flops 2956984320 | bytes 11272192 | tf_op jit(solution)/shard_map/dot_general | solution.py:91
  281.9 5.2 %all-to-all-start.3 = ((bf16[32,64,2048]{2,1,0:T(8,128)(2,1)}), bf16[32,64,2048]{2,1,0:T(8,128)(2,1)}, u32[]{:S(2)}, u32[]{:S(2)}) async-start(bf16[32,64,2048]{2,1,0:T(8,128)(2,1)} %bitcast.151), calls=%async_computation.4 | async-start | bytes 16777216 | tf_op jit(solution)/shard_map/all_to_all | solution.py:246
  287.2 2.9 fusion.112
  290.2 5.5 %convolution_convert_fusion.3 = bf16[512,2048]{1,0:T(8,128)(2,1)} fusion(bf16[352,2048]{1,0:T(8,128)(2,1)S(1)} %copy-done, bf16[512,2048]{1,0:T(8,128)(2,1)} %all-gather.5.cloned.1.call-done, bf16[352,2048]{1,0:T(8,128)(2,1)} %param.32, f32[512,352]{0,1:T(8,128)S(1)} %fusion.112), kind=kOutput, calls=%fused_computation.12 | convolution fusion | flops 1478524928 | bytes 7798784 | tf_op jit(solution)/shard_map/dot_general | solution.py:91
  295.7 97.2 %all-to-all-done.3 = bf16[32,64,2048]{2,1,0:T(8,128)(2,1)} async-done(((bf16[32,64,2048]{2,1,0:T(8,128)(2,1)}), bf16[32,64,2048]{2,1,0:T(8,128)(2,1)}, u32[]{:S(2)}, u32[]{:S(2)}) %all-to-all-start.3) | async-done | bytes 8388640 | tf_op jit(solution)/shard_map/all_to_all | solution.py:246
  392.9 9.5 %fusion = bf16[512,2048]{1,0:T(8,128)(2,1)} fusion(bf16[512,2048]{1,0:T(8,128)(2,1)} %convolution_convert_fusion.3, bf16[32,64,2048]{2,1,0:T(8,128)(2,1)} %all-to-all-done.3, bf16[512,32]{0,1:T(8,128)(2,1)S(1)} %select_reduce_fusion, s32[512,32]{0,1:T(8,128)S(1)} %copy-done.16, pred[512,32]{0,1:T(8,128)(4,1)S(1)} %copy-done.12), kind=kOutput, calls=%fused_computation.6 | convolution fusion | flops 4301258752 | bytes 12697600 | tf_op jit(solution)/shard_map/dot_general | solution.py:258
  402.5 4.8 %all-to-all-start.1 = ((bf16[32,16,2048]{2,1,0:T(8,128)(2,1)}), bf16[32,16,2048]{2,1,0:T(8,128)(2,1)}, u32[]{:S(2)}, u32[]{:S(2)}) async-start(bf16[32,16,2048]{2,1,0:T(8,128)(2,1)} %bitcast.155), calls=%async_computation.2 | async-start | bytes 4194304 | tf_op jit(solution)/shard_map/all_to_all | solution.py:253
  407.4 21.4 %reduce-scatter.5.cloned.1.call-done = bf16[1,128,2048]{2,1,0:T(8,128)(2,1)} async-done(((bf16[4,128,2048]{2,1,0:T(8,128)(2,1)}), bf16[1,128,2048]{2,1,0:T(8,128)(2,1)}) %reduce-scatter.5.cloned.1.call-update) | async-done | bytes 524304 | tf_op jit(solution)/shard_map/reduce_scatter | solution.py:263
  428.7 8.6 %all-to-all-done.1 = bf16[32,16,2048]{2,1,0:T(8,128)(2,1)} async-done(((bf16[32,16,2048]{2,1,0:T(8,128)(2,1)}), bf16[32,16,2048]{2,1,0:T(8,128)(2,1)}, u32[]{:S(2)}, u32[]{:S(2)}) %all-to-all-start.1) | async-done | bytes 2097184 | tf_op jit(solution)/shard_map/all_to_all | solution.py:253
  437.4 3.0 fusion.9
  (138 shorter events, 22.9 us)
Async XLA Ops:
  6.5 283.6 %copy-start = (bf16[352,2048]{1,0:T(8,128)(2,1)S(1)}, bf16[352,2048]{1,0:T(8,128)(2,1)}, u32[]{:S(2)}) copy-start(bf16[352,2048]{1,0:T(8,128)(2,1)} %param.33) | copy-start | bytes 4325380
  6.5 62.0 %copy-start.6 = (bf16[2,128,512]{2,1,0:T(8,128)(2,1)S(1)}, bf16[2,128,512]{2,1,0:T(8,128)(2,1)}, u32[]{:S(2)}) copy-start(bf16[2,128,512]{2,1,0:T(8,128)(2,1)} %param.20) | copy-start | bytes 786436
  6.5 62.8 %copy-start.30 = (s32[2,64]{1,0:T(2,128)S(1)}, s32[2,64]{1,0:T(2,128)}, u32[]{:S(2)}) copy-start(s32[2,64]{1,0:T(2,128)} %param.25) | copy-start | bytes 1540
  6.5 64.8 %copy-start.29 = (bf16[2048]{0:T(1024)(128)(2,1)S(1)}, bf16[2048]{0:T(1024)(128)(2,1)}, u32[]{:S(2)}) copy-start(bf16[2048]{0:T(1024)(128)(2,1)} %param.27) | copy-start | bytes 12292
  6.5 66.0 %copy-start.31 = (s32[2]{0:T(128)S(1)}, s32[2]{0:T(128)}, u32[]{:S(2)}) copy-start(s32[2]{0:T(128)} %param.24) | copy-start | bytes 28
  6.5 135.7 %all-gather.5.cloned.1.call-start = ((), (), s32[]{:S(2)}) async-start(), calls=%async_computation.8 | async-start | bytes 2621440 | tf_op jit(solution)/shard_map/all_gather | solution.py:180
  9.0 66.6 %copy-start.1 = (bf16[8,64,512]{2,1,0:T(8,128)(2,1)S(1)}, bf16[8,64,512]{2,1,0:T(8,128)(2,1)}, u32[]{:S(2)}) copy-start(bf16[8,64,512]{2,1,0:T(8,128)(2,1)} %param.22) | copy-start | bytes 1572868
  9.0 66.6 %copy-start.2 = (bf16[8,64,512]{2,1,0:T(8,128)(2,1)S(1)}, bf16[8,64,512]{2,1,0:T(8,128)(2,1)}, u32[]{:S(2)}) copy-start(bf16[8,64,512]{2,1,0:T(8,128)(2,1)} %param.21) | copy-start | bytes 1572868
  9.0 66.6 %collective-permute-start = (bf16[2,8,64,512]{3,2,1,0:T(8,128)(2,1)}, bf16[2,8,64,512]{3,2,1,0:T(8,128)(2,1)}, u32[]{:S(2)}, u32[]{:S(2)}) collective-permute-start(bf16[2,8,64,512]{3,2,1,0:T(8,128)(2,1)} %pad_maximum_fusion.1), channel_id=1, source_target_pairs={{0,32},{32,64},{64,96},{96,0},{1,33},{33,65},{65,97},{97,1},{2,34}... | collective-permute-start | bytes 3145736 | tf_op jit(solution)/shard_map/ppermute | solution.py:142
  10.7 64.9 %collective-permute-start.1 = (bf16[2,8,64,512]{3,2,1,0:T(8,128)(2,1)}, bf16[2,8,64,512]{3,2,1,0:T(8,128)(2,1)}, u32[]{:S(2)}, u32[]{:S(2)}) collective-permute-start(bf16[2,8,64,512]{3,2,1,0:T(8,128)(2,1)} %pad_maximum_fusion.1), channel_id=1, source_target_pairs={{0,64},{32,96},{64,0},{96,32},{1,65},{33,97},{65,1},{97,33},{2,66}... | collective-permute-start | bytes 3145736 | tf_op jit(solution)/shard_map/ppermute | solution.py:142
  13.6 62.0 %collective-permute-start.2 = (bf16[2,8,64,512]{3,2,1,0:T(8,128)(2,1)}, bf16[2,8,64,512]{3,2,1,0:T(8,128)(2,1)}, u32[]{:S(2)}, u32[]{:S(2)}) collective-permute-start(bf16[2,8,64,512]{3,2,1,0:T(8,128)(2,1)} %pad_maximum_fusion.1), channel_id=1, source_target_pairs={{0,96},{32,0},{64,32},{96,64},{1,97},{33,1},{65,33},{97,65},{2,98}... | collective-permute-start | bytes 3145736 | tf_op jit(solution)/shard_map/ppermute | solution.py:142
  91.9 5.9 %copy-start.24 = (s32[128,6]{0,1:T(8,128)S(1)}, s32[128,6]{0,1:T(8,128)}, u32[]{:S(2)}) copy-start(s32[128,6]{0,1:T(8,128)} %param.34) | copy-start | bytes 9220
  91.9 6.5 %copy-start.19 = (s32[128,6]{0,1:T(8,128)S(1)}, s32[128,6]{0,1:T(8,128)}, u32[]{:S(2)}) copy-start(s32[128,6]{0,1:T(8,128)} %get-tuple-element.24) | copy-start | bytes 9220
  97.7 120.7 %all-gather.3.cloned.1.call-start = ((), (), s32[]{:S(2)}) async-start(), calls=%async_computation.6 | async-start | bytes 10485760 | tf_op jit(solution)/shard_map/all_gather | solution.py:235
  101.6 37.2 %copy-start.7 = (f32[512,12]{0,1:T(8,128)S(1)}, f32[512,12]{0,1:T(8,128)}, u32[]{:S(2)}) copy-start(f32[512,12]{0,1:T(8,128)} %all_gather.9) | copy-start | bytes 73732
  150.5 110.9 %all-to-all-start.2 = ((bf16[32,64,2048]{2,1,0:T(8,128)(2,1)}), bf16[32,64,2048]{2,1,0:T(8,128)(2,1)}, u32[]{:S(2)}, u32[]{:S(2)}) async-start(bf16[32,64,2048]{2,1,0:T(8,128)(2,1)} %bitcast.150), calls=%async_computation.3 | async-start | bytes 16777216 | tf_op jit(solution)/shard_map/all_to_all | solution.py:228
  155.5 247.0 %reduce-scatter.3.cloned.1.call-start = ((), (), s32[]{:S(2)}) async-start(), calls=%async_computation.7 | async-start | bytes 10485760 | tf_op jit(solution)/shard_map/reduce_scatter | solution.py:240
  218.4 6.5 %copy-start.32 = (bf16[128,16,2048]{2,1,0:T(8,128)(2,1)S(1)}, bf16[128,16,2048]{2,1,0:T(8,128)(2,1)}, u32[]{:S(2)}) copy-start(bf16[128,16,2048]{2,1,0:T(8,128)(2,1)} %all-gather.3.cloned.1.call-done) | copy-start | bytes 25165828
  218.4 7.1 %copy-start.33 = (bf16[2,352,2048]{2,1,0:T(8,128)(2,1)S(1)}, bf16[2,352,2048]{2,1,0:T(8,128)(2,1)}, u32[]{:S(2)}) copy-start(bf16[2,352,2048]{2,1,0:T(8,128)(2,1)} %param.29) | copy-start | bytes 8650756
  261.4 6.2 %copy-start.34 = (bf16[2,352,2048]{2,1,0:T(8,128)(2,1)S(1)}, bf16[2,352,2048]{2,1,0:T(8,128)(2,1)}, u32[]{:S(2)}) copy-start(bf16[2,352,2048]{2,1,0:T(8,128)(2,1)} %param.29) | copy-start | bytes 8650756
  267.6 7.1 %copy-start.36 = (bf16[2,352,2048]{2,1,0:T(8,128)(2,1)S(1)}, bf16[2,352,2048]{2,1,0:T(8,128)(2,1)}, u32[]{:S(2)}) copy-start(bf16[2,352,2048]{2,1,0:T(8,128)(2,1)} %param.30) | copy-start | bytes 8650756
  281.9 5.2 %copy-start.8 = (f32[512,12]{0,1:T(8,128)S(1)}, f32[512,12]{0,1:T(8,128)}, u32[]{:S(2)}) copy-start(f32[512,12]{0,1:T(8,128)} %all_gather.9) | copy-start | bytes 73732
  281.9 5.2 %copy-start.22 = (pred[512,6]{0,1:T(8,128)(4,1)S(1)}, pred[512,6]{0,1:T(8,128)(4,1)}, u32[]{:S(2)}) copy-start(pred[512,6]{0,1:T(8,128)(4,1)} %copy-done.21) | copy-start | bytes 9220
  281.9 111.0 %all-to-all-start.3 = ((bf16[32,64,2048]{2,1,0:T(8,128)(2,1)}), bf16[32,64,2048]{2,1,0:T(8,128)(2,1)}, u32[]{:S(2)}, u32[]{:S(2)}) async-start(bf16[32,64,2048]{2,1,0:T(8,128)(2,1)} %bitcast.151), calls=%async_computation.4 | async-start | bytes 16777216 | tf_op jit(solution)/shard_map/all_to_all | solution.py:246
  287.0 141.7 %reduce-scatter.5.cloned.1.call-start = ((), (), s32[]{:S(2)}) async-start(), calls=%async_computation.9 | async-start | bytes 2621440 | tf_op jit(solution)/shard_map/reduce_scatter | solution.py:263
  290.2 102.8 %copy-start.12 = (pred[512,32]{0,1:T(8,128)(4,1)S(1)}, pred[512,32]{0,1:T(8,128)(4,1)}, u32[]{:S(2)}) copy-start(pred[512,32]{0,1:T(8,128)(4,1)} %copy-done.11) | copy-start | bytes 49156
  290.2 102.7 %copy-start.16 = (s32[512,32]{0,1:T(8,128)S(1)}, s32[512,32]{0,1:T(8,128)}, u32[]{:S(2)}) copy-start(s32[512,32]{0,1:T(8,128)} %copy-done.15) | copy-start | bytes 196612
  402.4 4.9 %copy-start.25 = (f32[128,6]{0,1:T(8,128)S(1)}, f32[128,6]{0,1:T(8,128)}, u32[]{:S(2)}) copy-start(f32[128,6]{0,1:T(8,128)} %param.35) | copy-start | bytes 9220
  402.4 4.9 %copy-start.28 = (pred[128,6]{0,1:T(8,128)(4,1)S(1)}, pred[128,6]{0,1:T(8,128)(4,1)}, u32[]{:S(2)}) copy-start(pred[128,6]{0,1:T(8,128)(4,1)} %copy-done.27) | copy-start | bytes 2308
  402.4 34.9 %copy-start.14 = (s32[128,32]{0,1:T(8,128)S(1)}, s32[128,32]{0,1:T(8,128)}, u32[]{:S(2)}) copy-start(s32[128,32]{0,1:T(8,128)} %copy-done.13) | copy-start | bytes 49156
  402.5 34.9 %copy-start.18 = (pred[128,32]{0,1:T(8,128)(4,1)S(1)}, pred[128,32]{0,1:T(8,128)(4,1)}, u32[]{:S(2)}) copy-start(pred[128,32]{0,1:T(8,128)(4,1)} %copy-done.17) | copy-start | bytes 12292
  402.5 34.9 %all-to-all-start.1 = ((bf16[32,16,2048]{2,1,0:T(8,128)(2,1)}), bf16[32,16,2048]{2,1,0:T(8,128)(2,1)}, u32[]{:S(2)}, u32[]{:S(2)}) async-start(bf16[32,16,2048]{2,1,0:T(8,128)(2,1)} %bitcast.155), calls=%async_computation.2 | async-start | bytes 4194304 | tf_op jit(solution)/shard_map/all_to_all | solution.py:253
  (15 other events, 29.8 us)
Sparse Core Ops, SparseCore 0:
  97.9 32.4 all-gather.4
  138.2 80.1 all-gather.2
  236.1 81.4 reduce-scatter.2
  402.6 26.0 reduce-scatter.4

commit v5 on v3

--- a/solution.py
+++ b/solution.py
@@ -227,12 +227,23 @@
         scatter_dimension=0,
         tiled=False,
     )
+    far_split = far_cap // 2
+    far_quarter = far_split // row_count
+    far_terms = far_terms.astype(jnp.bfloat16).reshape(column_count, far_cap, model_width)
     far_back = lax.all_to_all(
-        far_terms.astype(jnp.bfloat16).reshape(column_count, far_cap, model_width),
-        "exp",
-        split_axis=0,
-        concat_axis=0,
-        tiled=True,
+        far_terms[:, :far_split], "exp", split_axis=0, concat_axis=0, tiled=True
+    ).reshape(-1, model_width)
+    far_rest = lax.psum_scatter(
+        jnp.transpose(
+            far_terms[:, far_split:].reshape(column_count, row_count, far_quarter, model_width),
+            (1, 0, 2, 3),
+        ),
+        "dp",
+        scatter_dimension=0,
+        tiled=False,
+    )
+    far_rest_back = lax.all_to_all(
+        far_rest, "exp", split_axis=0, concat_axis=0, tiled=True
     ).reshape(-1, model_width)
     near_back = lax.all_to_all(
         near_sum, "exp", split_axis=0, concat_axis=0, tiled=True
@@ -241,9 +252,15 @@
     def combine(slot_weights, rows):
         return jnp.dot(slot_weights.astype(jnp.bfloat16), rows, preferred_element_type=jnp.float32)
 
-    far_part = combine(far_weights, far_back) + shared_terms.astype(
-        jnp.bfloat16
-    ).astype(jnp.float32)
+    far_grid = far_weights.reshape(-1, column_count, far_cap)
+    rest_weights = lax.dynamic_slice_in_dim(
+        far_grid, far_split + lax.axis_index("dp") * far_quarter, far_quarter, axis=2
+    )
+    far_part = (
+        combine(far_grid[:, :, :far_split].reshape(-1, column_count * far_split), far_back)
+        + combine(rest_weights.reshape(-1, column_count * far_quarter), far_rest_back)
+        + shared_terms.astype(jnp.bfloat16).astype(jnp.float32)
+    )
     far_sum = lax.psum_scatter(
         far_part.astype(jnp.bfloat16).reshape(row_count, tok_rows, model_width),
         "dp",

time: 428 us -> 428 us (level); the launches traced: 427 us -> 420 us
  waiting for transfers between devices: 247 us -> 166 us
  blocking collectives: 48.8 us -> 112 us
  starting transfers between devices: 15.1 us -> 24.8 us
  matrix products: 79.9 us -> 72.3 us
  local copies, waits for them, and re-layouts: 13.8 us -> 18.4 us
    all_to_all x1, blocking collectives: 35.6 us -> 99.2 us  [on_device(): lax.all_to_all(far_out.reshape(column_count, far_cap, model_width), 'exp'...]
    all_gather x1, waiting for transfers between devices: 62.4 us -> 0.02 us  [on_device(): lax.all_gather(near_arrived, 'dp', axis=0, tiled=True)]
    all_to_all x2 -> x3, waiting for transfers between devices: 123 us -> 82.1 us  [the longest x1 42.9 us: on_device(): lax.all_to_all(far_terms[:, :far_split], 'exp', split_axis=0, concat_axis...]
    reduce_scatter x1, waiting for transfers between devices: 0.02 us -> 22.4 us  [on_device(): lax.psum_scatter(near_terms.astype(jnp.bfloat16).reshape(row_count, colum...]
    all_to_all x2 -> x3, starting transfers between devices: 10.1 us -> 16.4 us  [the longest x1 7.51 us: on_device(): lax.all_to_all(near_out.reshape(column_count, near_cap, model_width), 'ex...]
    reshape x0 -> x2, local copies, waits for them, and re-layouts: none -> 4.73 us  [on_device(): far_terms[:, far_split:]]
    dot_general x2 -> x3, matrix products: 12.5 us -> 15 us  [combine(): jnp.dot(slot_weights.astype(jnp.bfloat16), rows, preferred_element_type=j...]
  transfers between devices with their start and end apart: 8 -> 10, of which waited for: 6 -> 7; matrix products, arithmetic and copies ran while one was open for 18% -> 18% of each run, Pallas kernels for 0% -> 0%
where the time goes in v5:
time: 428 us; the launch traced here: 420 us
  waiting for transfers between devices  166 us (39%)
  blocking collectives  112 us (26%)
  matrix products  72.3 us (17%)
  starting transfers between devices  24.8 us (6%)
  local copies, waits for them, and re-layouts  18.4 us (4%)
  between operations  14.6 us (3%)
  other arithmetic  11.8 us (3%)
    all_to_all x1, blocking collectives, on_device(): lax.all_to_all(far_out.reshape(column_count, far_cap, model_width), 'exp'...  99.2 us
    all_to_all x1, waiting for transfers between devices, on_device(): lax.all_to_all(far_terms[:, :far_split], 'exp', split_axis=0, concat_axis...  42.9 us
    all_gather x1, waiting for transfers between devices, on_device(): lax.all_gather(jnp.stack([key_pool, value_pool]), 'dp', axis=1, tiled=True)  31.2 us
    all_to_all x1, waiting for transfers between devices, on_device(): lax.all_to_all(near_out.reshape(column_count, near_cap, model_width), 'ex...  29.2 us
    reduce_scatter x1, waiting for transfers between devices, on_device(): lax.psum_scatter(far_part.astype(jnp.bfloat16).reshape(row_count, tok_row...  24.1 us
    reduce_scatter x1, waiting for transfers between devices, on_device(): lax.psum_scatter(near_terms.astype(jnp.bfloat16).reshape(row_count, colum...  22.4 us
    dot_general x3, matrix products, shared_block(): return jnp.dot(inner, down_rows, preferred_element_type=jnp.float32)  17.4 us
    dot_general x3, matrix products, combine(): jnp.dot(slot_weights.astype(jnp.bfloat16), rows, preferred_element_type=j...  15 us
  transfers between devices with their start and end apart: 10, of which 7 were waited for; matrix products, arithmetic and copies ran while one was open for 18% of the time, Pallas kernels for 0%

profile of v5, /device:TPU:0, one launch (start us, length us, event | category | flops | bytes accessed | tf_op | source)
XLA Modules:
  0.0 420.1 jit_solution(3971838567712107418)
XLA Ops:
  6.6 2.5 pad_maximum_fusion
  9.8 13.1 %all_gather.12 = f32[512,12]{0,1:T(8,128)} all-gather(f32[128,12]{0,1:T(8,128)S(1)} %pad_maximum_fusion.1), channel_id=1, replica_groups=mesh['dp'=4,'exp'=32] {'dp'}, dimensions={0}, use_global_device_ids=true | all-gather | bytes 30720 | tf_op jit(solution)/shard_map/all_gather | solution.py:115
  28.8 31.2 %all-gather.4.cloned.1.call-done = bf16[2,32,64,512]{3,2,1,0:T(8,128)(2,1)} async-done(((bf16[2,8,64,512]{3,2,1,0:T(8,128)(2,1)}), bf16[2,32,64,512]{3,2,1,0:T(8,128)(2,1)}) %all-gather.4.cloned.1.call-update) | async-done | bytes 4194320 | tf_op jit(solution)/shard_map/all_gather | solution.py:137
  60.0 2.9 gather_fusion
  72.8 4.8 %multiply_reduce_fusion = (f32[128]{0:T(128)S(1)}, f32[128,2048]{1,0:T(8,128)S(1)}) fusion(bf16[128,2048]{1,0:T(8,128)(2,1)S(1)} %convert_element_type.112, bf16[2048,2048]{1,0:T(8,128)(2,1)} %param.26, bf16[128,2048]{1,0:T(8,128)(2,1)S(1)} %copy-done.3), kind=kOutput, calls=%fused_computation.75 | convolution fusion | flops 1075314560 | bytes 10486272 | tf_op jit(solution)/shard_map/dot_general | solution.py:152
  80.6 3.1 convolution_convert_fusion.4
  83.7 7.5 %all-to-all-start = ((bf16[32,16,2048]{2,1,0:T(8,128)(2,1)}), bf16[32,16,2048]{2,1,0:T(8,128)(2,1)}, u32[]{:S(2)}, u32[]{:S(2)}) async-start(bf16[32,16,2048]{2,1,0:T(8,128)(2,1)} %bitcast.166), calls=%async_computation | async-start | bytes 4194304 | tf_op jit(solution)/shard_map/all_to_all | solution.py:205
  92.0 29.2 %all-to-all-done = bf16[32,16,2048]{2,1,0:T(8,128)(2,1)} async-done(((bf16[32,16,2048]{2,1,0:T(8,128)(2,1)}), bf16[32,16,2048]{2,1,0:T(8,128)(2,1)}, u32[]{:S(2)}, u32[]{:S(2)}) %all-to-all-start) | async-done | bytes 2097184 | tf_op jit(solution)/shard_map/all_to_all | solution.py:205
  124.1 6.3 %convolution_convert_fusion.1 = bf16[2048,2048]{1,0:T(8,128)(2,1)S(1)} fusion(pred[512,2048]{0,1:T(32,128)(4,1)S(1)} %fusion.4, bf16[512,2048]{1,0:T(8,128)(2,1)} %all-gather.8.cloned.1.call-done), kind=kOutput, calls=%fused_computation.2 | convolution fusion | flops 4299161600 | bytes 11534336 | tf_op jit(solution)/shard_map/ts,td->sd/dot_general | solution.py:199
  130.4 99.2 %all_to_all.25 = bf16[32,64,2048]{2,1,0:T(8,128)(2,1)S(1)} all-to-all(bf16[32,64,2048]{2,1,0:T(8,128)(2,1)S(1)} %bitcast.165), channel_id=1, replica_groups=mesh['dp'=4,'exp'=32] {'exp'}, dimensions={0} | all-to-all | bytes 16777216 | tf_op jit(solution)/shard_map/all_to_all | solution.py:212
  229.6 3.2 fusion.18
  232.9 3.5 fusion.6
  236.4 4.8 %convolution_convert_fusion = bf16[2048,2048]{1,0:T(8,128)(2,1)S(1)} fusion(bf16[2048,352]{0,1:T(8,128)(2,1)S(1)} %fusion.6, bf16[2,352,2048]{2,1,0:T(8,128)(2,1)S(1)} %copy-done.39), kind=kOutput, calls=%fused_computation.1 | convolution fusion | flops 2956984320 | bytes 11272192 | tf_op jit(solution)/shard_map/dot_general | solution.py:91
  241.2 2.5 slice_bitcast_fusion
  243.7 2.2 copy.115
  246.2 6.6 %fusion.22 = f32[2048,352]{0,1:T(8,128)S(1)} fusion(bf16[2048,2048]{1,0:T(8,128)(2,1)} %bitcast.178, bf16[2,352,2048]{2,1,0:T(8,128)(2,1)} %param.28), kind=kOutput, calls=%fused_computation.41 | convolution fusion | flops 2952790016 | bytes 12713984 | tf_op jit(solution)/shard_map/td,fd->tf/dot_general | solution.py:88
  254.1 3.5 fusion.5
  257.6 6.9 %convolution_convert_fusion.2 = bf16[2048,2048]{1,0:T(8,128)(2,1)} fusion(bf16[2048,352]{0,1:T(8,128)(2,1)S(1)} %fusion.5, bf16[2,352,2048]{2,1,0:T(8,128)(2,1)S(1)} %copy-done.40), kind=kOutput, calls=%fused_computation.3 | convolution fusion | flops 2956984320 | bytes 11272192 | tf_op jit(solution)/shard_map/dot_general | solution.py:91
  264.6 5.0 %all-to-all-start.3 = ((bf16[32,32,2048]{2,1,0:T(8,128)(2,1)}), bf16[32,32,2048]{2,1,0:T(8,128)(2,1)}, u32[]{:S(2)}, u32[]{:S(2)}) async-start(bf16[32,32,2048]{2,1,0:T(8,128)(2,1)} %get-tuple-element.16), calls=%async_computation.4 | async-start | bytes 8388608 | tf_op jit(solution)/shard_map/all_to_all | solution.py:233
  269.7 2.8 fusion.3
  272.6 2.4 fusion.107
  275.0 5.7 %convolution_convert_fusion.3 = bf16[512,2048]{1,0:T(8,128)(2,1)} fusion(bf16[352,2048]{1,0:T(8,128)(2,1)S(1)} %copy-done, bf16[512,2048]{1,0:T(8,128)(2,1)} %all-gather.8.cloned.1.call-done, bf16[352,2048]{1,0:T(8,128)(2,1)} %param.32, f32[512,352]{0,1:T(8,128)S(1)} %fusion.107), kind=kOutput, calls=%fused_computation.14 | convolution fusion | flops 1478524928 | bytes 7798784 | tf_op jit(solution)/shard_map/dot_general | solution.py:91
  280.6 42.9 %all-to-all-done.3 = bf16[32,32,2048]{2,1,0:T(8,128)(2,1)} async-done(((bf16[32,32,2048]{2,1,0:T(8,128)(2,1)}), bf16[32,32,2048]{2,1,0:T(8,128)(2,1)}, u32[]{:S(2)}, u32[]{:S(2)}) %all-to-all-start.3) | async-done | bytes 4194336 | tf_op jit(solution)/shard_map/all_to_all | solution.py:233
  323.5 3.9 all-to-all-start.4
  327.8 6.9 %fusion.40 = f32[512,2048,1]{1,0,2:T(8,128)} fusion(bf16[32,32,2048]{2,1,0:T(8,128)(2,1)} %all-to-all-done.3, bf16[512,32,64]{0,2,1:T(8,128)(2,1)} %fusion.3), kind=kOutput, calls=%fused_computation.70 | convolution fusion | flops 2147483648 | bytes 9437184 | tf_op jit(solution)/shard_map/dot_general | solution.py:253
  334.7 10.0 %all-to-all-done.4 = bf16[32,8,2048]{2,1,0:T(8,128)(2,1)S(1)} async-done(((bf16[32,8,2048]{2,1,0:T(8,128)(2,1)}), bf16[32,8,2048]{2,1,0:T(8,128)(2,1)S(1)}, u32[]{:S(2)}, u32[]{:S(2)}) %all-to-all-start.4) | async-done | bytes 1048608 | tf_op jit(solution)/shard_map/all_to_all | solution.py:245
  344.7 5.1 %fusion.1 = bf16[512,2048]{1,0:T(8,128)(2,1)} fusion(f32[512,2048,1]{1,0,2:T(8,128)} %fusion.40, bf16[512,2048]{1,0:T(8,128)(2,1)} %convolution_convert_fusion.3, bf16[32,8,2048]{2,1,0:T(8,128)(2,1)S(1)} %all-to-all-done.4, bf16[512,32,64]{0,2,1:T(8,128)(2,1)} %fusion.3, s32[]{:T(128)S(6)} %select_n.78), kind=kOutput, calls=%fused_computation.7 | convolution fusion | flops 541065216 | bytes 9699332 | tf_op jit(solution)/shard_map/dot_general | solution.py:253
  349.8 22.4 %reduce-scatter.4.cloned.1.call-done = bf16[1,32,16,2048]{3,2,1,0:T(8,128)(2,1)} async-done(((bf16[4,32,16,2048]{3,2,1,0:T(8,128)(2,1)}), bf16[1,32,16,2048]{3,2,1,0:T(8,128)(2,1)}) %reduce-scatter.4.cloned.1.call-update) | async-done | bytes 2097168 | tf_op jit(solution)/shard_map/reduce_scatter | solution.py:224
  372.3 7.5 %all-to-all-start.1 = ((bf16[32,16,2048]{2,1,0:T(8,128)(2,1)}), bf16[32,16,2048]{2,1,0:T(8,128)(2,1)}, u32[]{:S(2)}, u32[]{:S(2)}) async-start(bf16[32,16,2048]{2,1,0:T(8,128)(2,1)} %bitcast.169), calls=%async_computation.2 | async-start | bytes 4194304 | tf_op jit(solution)/shard_map/all_to_all | solution.py:248
  379.8 24.1 %reduce-scatter.8.cloned.1.call-done = bf16[1,128,2048]{2,1,0:T(8,128)(2,1)} async-done(((bf16[4,128,2048]{2,1,0:T(8,128)(2,1)}), bf16[1,128,2048]{2,1,0:T(8,128)(2,1)}) %reduce-scatter.8.cloned.1.call-update) | async-done | bytes 524304 | tf_op jit(solution)/shard_map/reduce_scatter | solution.py:264
  404.0 5.8 %all-to-all-done.1 = bf16[32,16,2048]{2,1,0:T(8,128)(2,1)} async-done(((bf16[32,16,2048]{2,1,0:T(8,128)(2,1)}), bf16[32,16,2048]{2,1,0:T(8,128)(2,1)}, u32[]{:S(2)}, u32[]{:S(2)}) %all-to-all-start.1) | async-done | bytes 2097184 | tf_op jit(solution)/shard_map/all_to_all | solution.py:248
  409.8 3.0 fusion.11
  (153 shorter events, 24.9 us)
Async XLA Ops:
  6.5 268.4 %copy-start = (bf16[352,2048]{1,0:T(8,128)(2,1)S(1)}, bf16[352,2048]{1,0:T(8,128)(2,1)}, u32[]{:S(2)}) copy-start(bf16[352,2048]{1,0:T(8,128)(2,1)} %param.33) | copy-start | bytes 4325380
  6.5 16.3 %copy-start.4 = (bf16[128,2048]{1,0:T(8,128)(2,1)S(1)}, bf16[128,2048]{1,0:T(8,128)(2,1)}, u32[]{:S(2)}) copy-start(bf16[128,2048]{1,0:T(8,128)(2,1)} %param.19) | copy-start | bytes 1572868
  6.5 53.4 %all-gather.4.cloned.1.call-start = ((), (), s32[]{:S(2)}) async-start(), calls=%async_computation.8 | async-start | bytes 5242880 | tf_op jit(solution)/shard_map/all_gather | solution.py:137
  6.6 16.6 %copy-start.8 = (bf16[2,128,512]{2,1,0:T(8,128)(2,1)S(1)}, bf16[2,128,512]{2,1,0:T(8,128)(2,1)}, u32[]{:S(2)}) copy-start(bf16[2,128,512]{2,1,0:T(8,128)(2,1)} %param.20) | copy-start | bytes 786436
  6.6 16.7 %copy-start.32 = (s32[2,64]{1,0:T(2,128)S(1)}, s32[2,64]{1,0:T(2,128)}, u32[]{:S(2)}) copy-start(s32[2,64]{1,0:T(2,128)} %param.25) | copy-start | bytes 1540
  9.1 15.7 %copy-start.33 = (s32[2,4]{1,0:T(2,128)S(1)}, s32[2,4]{1,0:T(2,128)}, u32[]{:S(2)}) copy-start(s32[2,4]{1,0:T(2,128)} %param.23) | copy-start | bytes 100
  9.1 16.7 %copy-start.31 = (bf16[2048]{0:T(1024)(128)(2,1)S(1)}, bf16[2048]{0:T(1024)(128)(2,1)}, u32[]{:S(2)}) copy-start(bf16[2048]{0:T(1024)(128)(2,1)} %param.27) | copy-start | bytes 12292
  9.1 17.9 %copy-start.34 = (s32[2]{0:T(128)S(1)}, s32[2]{0:T(128)}, u32[]{:S(2)}) copy-start(s32[2]{0:T(128)} %param.24) | copy-start | bytes 28
  9.1 115.0 %all-gather.8.cloned.1.call-start = ((), (), s32[]{:S(2)}) async-start(), calls=%async_computation.11 | async-start | bytes 2621440 | tf_op jit(solution)/shard_map/all_gather | solution.py:164
  23.2 5.5 %copy-start.1 = (bf16[2,64,4,4,128]{4,3,2,1,0:T(4,128)(2,1)}, bf16[2,64,4,4,128]{4,3,2,1,0:T(4,128)(2,1)S(1)}, u32[]{:S(2)}) copy-start(bf16[2,64,4,4,128]{4,3,2,1,0:T(4,128)(2,1)S(1)} %reshape.103) | copy-start | bytes 1572868
  83.7 8.3 %copy-start.9 = (f32[512,12]{0,1:T(8,128)S(1)}, f32[512,12]{0,1:T(8,128)}, u32[]{:S(2)}) copy-start(f32[512,12]{0,1:T(8,128)} %all_gather.12) | copy-start | bytes 73732
  83.7 37.6 %all-to-all-start = ((bf16[32,16,2048]{2,1,0:T(8,128)(2,1)}), bf16[32,16,2048]{2,1,0:T(8,128)(2,1)}, u32[]{:S(2)}, u32[]{:S(2)}) async-start(bf16[32,16,2048]{2,1,0:T(8,128)(2,1)} %bitcast.166), calls=%async_computation | async-start | bytes 4194304 | tf_op jit(solution)/shard_map/all_to_all | solution.py:205
  91.2 155.0 %all-gather.6.cloned.1.call-start = ((), (), s32[]{:S(2)}) async-start(), calls=%async_computation.9 | async-start | bytes 10485760 | tf_op jit(solution)/shard_map/all_gather | solution.py:219
  92.0 29.6 %copy-start.21 = (pred[512,6]{0,1:T(8,128)(4,1)}, pred[512,6]{0,1:T(8,128)(4,1)S(1)}, u32[]{:S(2)}) copy-start(pred[512,6]{0,1:T(8,128)(4,1)S(1)} %get-tuple-element.11) | copy-start | bytes 9220
  92.0 29.6 %copy-start.12 = (s32[512,6]{0,1:T(8,128)}, s32[512,6]{0,1:T(8,128)S(1)}, u32[]{:S(2)}) copy-start(s32[512,6]{0,1:T(8,128)S(1)} %add_select_fusion.1) | copy-start | bytes 36868
  121.3 202.3 %reduce-scatter.6.cloned.1.call-start = ((), (), s32[]{:S(2)}) async-start(), calls=%async_computation.12 | async-start | bytes 5242880 | tf_op jit(solution)/shard_map/reduce_scatter | solution.py:236
  130.4 99.2 %copy-start.36 = (bf16[2,352,2048]{2,1,0:T(8,128)(2,1)S(1)}, bf16[2,352,2048]{2,1,0:T(8,128)(2,1)}, u32[]{:S(2)}) copy-start(bf16[2,352,2048]{2,1,0:T(8,128)(2,1)} %param.28) | copy-start | bytes 8650756
  245.9 126.3 %reduce-scatter.4.cloned.1.call-start = ((), (), s32[]{:S(2)}) async-start(), calls=%async_computation.10 | async-start | bytes 10485760 | tf_op jit(solution)/shard_map/reduce_scatter | solution.py:224
  246.2 7.0 %copy-start.35 = (bf16[128,16,2048]{2,1,0:T(8,128)(2,1)S(1)}, bf16[128,16,2048]{2,1,0:T(8,128)(2,1)}, u32[]{:S(2)}) copy-start(bf16[128,16,2048]{2,1,0:T(8,128)(2,1)} %all-gather.6.cloned.1.call-done) | copy-start | bytes 25165828
  246.2 7.9 %copy-start.38 = (bf16[2,352,2048]{2,1,0:T(8,128)(2,1)S(1)}, bf16[2,352,2048]{2,1,0:T(8,128)(2,1)}, u32[]{:S(2)}) copy-start(bf16[2,352,2048]{2,1,0:T(8,128)(2,1)} %param.29) | copy-start | bytes 8650756
  264.5 5.1 %copy-start.13 = (s32[512,6]{0,1:T(8,128)S(1)}, s32[512,6]{0,1:T(8,128)}, u32[]{:S(2)}) copy-start(s32[512,6]{0,1:T(8,128)} %copy-done.12) | copy-start | bytes 36868
  264.5 5.1 %copy-start.22 = (pred[512,6]{0,1:T(8,128)(4,1)S(1)}, pred[512,6]{0,1:T(8,128)(4,1)}, u32[]{:S(2)}) copy-start(pred[512,6]{0,1:T(8,128)(4,1)} %copy-done.21) | copy-start | bytes 9220
  264.5 5.2 %copy-start.7 = (s32[512,32]{0,1:T(8,128)S(1)}, s32[512,32]{0,1:T(8,128)}, u32[]{:S(2)}) copy-start(s32[512,32]{0,1:T(8,128)} %copy-done.6) | copy-start | bytes 196612
  264.6 59.0 %all-to-all-start.3 = ((bf16[32,32,2048]{2,1,0:T(8,128)(2,1)}), bf16[32,32,2048]{2,1,0:T(8,128)(2,1)}, u32[]{:S(2)}, u32[]{:S(2)}) async-start(bf16[32,32,2048]{2,1,0:T(8,128)(2,1)} %get-tuple-element.16), calls=%async_computation.4 | async-start | bytes 8388608 | tf_op jit(solution)/shard_map/all_to_all | solution.py:233
  323.5 21.1 %all-to-all-start.4 = ((bf16[32,8,2048]{2,1,0:T(8,128)(2,1)}), bf16[32,8,2048]{2,1,0:T(8,128)(2,1)S(1)}, u32[]{:S(2)}, u32[]{:S(2)}) async-start(bf16[32,8,2048]{2,1,0:T(8,128)(2,1)} %bitcast.171), calls=%async_computation.6 | async-start | bytes 2097152 | tf_op jit(solution)/shard_map/all_to_all | solution.py:245
  327.5 76.5 %reduce-scatter.8.cloned.1.call-start = ((), (), s32[]{:S(2)}) async-start(), calls=%async_computation.13 | async-start | bytes 2621440 | tf_op jit(solution)/shard_map/reduce_scatter | solution.py:264
  372.3 7.5 %copy-start.20 = (s32[128,6]{0,1:T(8,128)S(1)}, s32[128,6]{0,1:T(8,128)}, u32[]{:S(2)}) copy-start(s32[128,6]{0,1:T(8,128)} %get-tuple-element.24) | copy-start | bytes 9220
  372.3 7.5 %copy-start.27 = (f32[128,6]{0,1:T(8,128)S(1)}, f32[128,6]{0,1:T(8,128)}, u32[]{:S(2)}) copy-start(f32[128,6]{0,1:T(8,128)} %param.35) | copy-start | bytes 9220
  372.3 7.5 %copy-start.30 = (pred[128,6]{0,1:T(8,128)(4,1)S(1)}, pred[128,6]{0,1:T(8,128)(4,1)}, u32[]{:S(2)}) copy-start(pred[128,6]{0,1:T(8,128)(4,1)} %copy-done.29) | copy-start | bytes 2308
  372.3 37.5 %copy-start.16 = (s32[128,32]{0,1:T(8,128)S(1)}, s32[128,32]{0,1:T(8,128)}, u32[]{:S(2)}) copy-start(s32[128,32]{0,1:T(8,128)} %copy-done.15) | copy-start | bytes 49156
  372.3 37.6 %copy-start.18 = (pred[128,32]{0,1:T(8,128)(4,1)S(1)}, pred[128,32]{0,1:T(8,128)(4,1)}, u32[]{:S(2)}) copy-start(pred[128,32]{0,1:T(8,128)(4,1)} %copy-done.17) | copy-start | bytes 12292
  372.3 37.5 %all-to-all-start.1 = ((bf16[32,16,2048]{2,1,0:T(8,128)(2,1)}), bf16[32,16,2048]{2,1,0:T(8,128)(2,1)}, u32[]{:S(2)}, u32[]{:S(2)}) async-start(bf16[32,16,2048]{2,1,0:T(8,128)(2,1)} %bitcast.169), calls=%async_computation.2 | async-start | bytes 4194304 | tf_op jit(solution)/shard_map/all_to_all | solution.py:248
  (20 other events, 46.1 us)
Sparse Core Ops, SparseCore 0:
  9.2 50.6 all-gather.3
  78.7 31.0 all-gather.7
  121.4 79.4 all-gather.5
  246.1 43.5 reduce-scatter.5
  292.0 80.2 reduce-scatter.3
  374.5 29.4 reduce-scatter.7

commit v6 on v3

--- a/solution.py
+++ b/solution.py
@@ -20,8 +20,9 @@
     linked = (parents[:, :, None] == node_index[None, None, :]).astype(jnp.float32)
     reached = jnp.minimum(linked + jnp.eye(node_count, dtype=jnp.float32)[None], 1.0)
     for rounds in range(max(1, (node_count - 1).bit_length())):
+        flags = reached.astype(jnp.bfloat16)
         reached = jnp.minimum(
-            jnp.einsum("rij,rjk->rik", reached, reached, precision=HIGHEST_PRECISION), 1.0
+            jnp.einsum("rij,rjk->rik", flags, flags, preferred_element_type=jnp.float32), 1.0
         )
     return reached
 

time: 428 us -> 428 us (level)
  no operation moved by 1% of the time
where the time goes in v6:
time: 428 us; the launch traced here: 427 us
  waiting for transfers between devices  247 us (58%)
  matrix products  79.6 us (19%)
  blocking collectives  48.8 us (11%)
  starting transfers between devices  15.3 us (4%)
  local copies, waits for them, and re-layouts  13.8 us (3%)
  between operations  13.8 us (3%)
  other arithmetic  9.05 us (2%)
    all_to_all x1, waiting for transfers between devices, on_device(): lax.all_to_all(far_terms.astype(jnp.bfloat16).reshape(column_count, far_c...  97.2 us
    all_gather x1, waiting for transfers between devices, on_device(): lax.all_gather(near_arrived, 'dp', axis=0, tiled=True)  62.2 us
    all_to_all x1, blocking collectives, on_device(): lax.all_to_all(near_out.reshape(column_count, near_cap, model_width), 'ex...  35.6 us
    all_gather x1, waiting for transfers between devices, on_device(): lax.all_gather(jnp.stack([key_pool, value_pool]), 'dp', axis=1, tiled=True)  31.4 us
    all_to_all x1, waiting for transfers between devices, on_device(): lax.all_to_all(far_out.reshape(column_count, far_cap, model_width), 'exp'...  26.1 us
    reduce_scatter x1, waiting for transfers between devices, on_device(): lax.psum_scatter(far_part.astype(jnp.bfloat16).reshape(row_count, tok_row...  20.9 us
    dot_general x3, matrix products, shared_block(): return jnp.dot(inner, down_rows, preferred_element_type=jnp.float32)  19.6 us
    dot_general x3, matrix products, shared_block(): jnp.einsum('td,fd->tf', tokens, gate_rows, preferred_element_type=jnp.flo...  15.7 us
  transfers between devices with their start and end apart: 8, of which 6 were waited for; matrix products, arithmetic and copies ran while one was open for 18% of the time, Pallas kernels for 0%

profile of v6, /device:TPU:0, one launch (start us, length us, event | category | flops | bytes accessed | tf_op | source)
XLA Modules:
  0.0 427.2 jit_solution(12164399394184050951)
XLA Ops:
  6.6 2.5 pad_maximum_fusion
  9.8 13.2 %all_gather.12 = f32[512,12]{0,1:T(8,128)} all-gather(f32[128,12]{0,1:T(8,128)S(1)} %pad_maximum_fusion.1), channel_id=1, replica_groups=mesh['dp'=4,'exp'=32] {'dp'}, dimensions={0}, use_global_device_ids=true | all-gather | bytes 30720 | tf_op jit(solution)/shard_map/all_gather | solution.py:116
  27.3 1.3 fusion.117
  28.6 31.4 %all-gather.4.cloned.1.call-done = bf16[2,32,64,512]{3,2,1,0:T(8,128)(2,1)} async-done(((bf16[2,8,64,512]{3,2,1,0:T(8,128)(2,1)}), bf16[2,32,64,512]{3,2,1,0:T(8,128)(2,1)}) %all-gather.4.cloned.1.call-update) | async-done | bytes 4194320 | tf_op jit(solution)/shard_map/all_gather | solution.py:138
  60.0 2.9 gather_fusion
  63.9 2.0 reshape_squeeze.14
  66.8 1.7 bitcast_reduce_fusion
  70.5 1.2 fusion.38
  72.8 4.8 %multiply_reduce_fusion = (f32[128]{0:T(128)S(1)}, f32[128,2048]{1,0:T(8,128)S(1)}) fusion(bf16[128,2048]{1,0:T(8,128)(2,1)S(1)} %convert_element_type.134, bf16[2048,2048]{1,0:T(8,128)(2,1)} %param.26, bf16[128,2048]{1,0:T(8,128)(2,1)S(1)} %copy-done.3), kind=kOutput, calls=%fused_computation.79 | convolution fusion | flops 1075314560 | bytes 10486272 | tf_op jit(solution)/shard_map/dot_general | solution.py:153
  77.6 1.0 multiply_convert_fusion
  80.7 1.7 convolution_convert_fusion.4
  82.4 35.6 %all_to_all.20 = bf16[32,16,2048]{2,1,0:T(8,128)(2,1)} all-to-all(bf16[32,16,2048]{2,1,0:T(8,128)(2,1)S(1)} %bitcast.146), channel_id=1, replica_groups=mesh['dp'=4,'exp'=32] {'exp'}, dimensions={0} | all-to-all | bytes 4194304 | tf_op jit(solution)/shard_map/all_to_all | solution.py:206
  120.6 1.6 fusion.2
  122.2 8.4 %convolution_convert_fusion.1 = bf16[2048,2048]{1,0:T(8,128)(2,1)} fusion(pred[512,2048]{0,1:T(32,128)(4,1)S(1)} %fusion.2, bf16[512,2048]{1,0:T(8,128)(2,1)} %all-gather.8.cloned.1.call-done), kind=kOutput, calls=%fused_computation.2 | convolution fusion | flops 4299161600 | bytes 11534336 | tf_op jit(solution)/shard_map/ts,td->sd/dot_general | solution.py:200
  130.6 5.2 %all-to-all-start.2 = ((bf16[32,64,2048]{2,1,0:T(8,128)(2,1)}), bf16[32,64,2048]{2,1,0:T(8,128)(2,1)}, u32[]{:S(2)}, u32[]{:S(2)}) async-start(bf16[32,64,2048]{2,1,0:T(8,128)(2,1)} %bitcast.144), calls=%async_computation.3 | async-start | bytes 16777216 | tf_op jit(solution)/shard_map/all_to_all | solution.py:213
  135.9 62.2 %all-gather.6.cloned.1.call-done = bf16[128,16,2048]{2,1,0:T(8,128)(2,1)} async-done(((bf16[32,16,2048]{2,1,0:T(8,128)(2,1)}), bf16[128,16,2048]{2,1,0:T(8,128)(2,1)}) %all-gather.6.cloned.1.call-update) | async-done | bytes 8388624 | tf_op jit(solution)/shard_map/all_gather | solution.py:220
  198.1 6.5 %fusion.24 = f32[2048,352]{0,1:T(8,128)S(1)} fusion(bf16[2048,2048]{1,0:T(8,128)(2,1)} %bitcast.157, bf16[2,352,2048]{2,1,0:T(8,128)(2,1)} %param.28), kind=kOutput, calls=%fused_computation.41 | convolution fusion | flops 2952790016 | bytes 12713984 | tf_op jit(solution)/shard_map/td,fd->tf/dot_general | solution.py:89
  205.1 3.5 fusion.3
  208.7 6.9 %convolution_convert_fusion.2 = bf16[2048,2048]{1,0:T(8,128)(2,1)} fusion(bf16[2048,352]{0,1:T(8,128)(2,1)S(1)} %fusion.3, bf16[2,352,2048]{2,1,0:T(8,128)(2,1)S(1)} %copy-done.37), kind=kOutput, calls=%fused_computation.3 | convolution fusion | flops 2956984320 | bytes 11272192 | tf_op jit(solution)/shard_map/dot_general | solution.py:92
  215.6 26.1 %all-to-all-done.2 = bf16[32,64,2048]{2,1,0:T(8,128)(2,1)} async-done(((bf16[32,64,2048]{2,1,0:T(8,128)(2,1)}), bf16[32,64,2048]{2,1,0:T(8,128)(2,1)}, u32[]{:S(2)}, u32[]{:S(2)}) %all-to-all-start.2) | async-done | bytes 8388640 | tf_op jit(solution)/shard_map/all_to_all | solution.py:213
  241.7 6.2 %fusion.20 = f32[2048,352]{0,1:T(8,128)S(1)} fusion(bf16[2048,2048]{1,0:T(8,128)(2,1)} %bitcast.29, bf16[2,352,2048]{2,1,0:T(8,128)(2,1)} %param.28), kind=kOutput, calls=%fused_computation.37 | convolution fusion | flops 2952790016 | bytes 12713984 | tf_op jit(solution)/shard_map/td,fd->tf/dot_general | solution.py:89
  247.9 7.1 %fusion.4 = bf16[2048,352]{0,1:T(8,128)(2,1)S(1)} fusion(bf16[2048,2048]{1,0:T(8,128)(2,1)} %bitcast.29, f32[2048,352]{0,1:T(8,128)S(1)} %fusion.20, bf16[2,352,2048]{2,1,0:T(8,128)(2,1)S(1)} %copy-done.36), kind=kOutput, calls=%fused_computation.16 | convolution fusion | flops 2957115392 | bytes 14155776 | tf_op jit(solution)/shard_map/td,fd->tf/dot_general | solution.py:90
  255.0 7.1 %convolution_convert_fusion = bf16[2048,2048]{1,0:T(8,128)(2,1)} fusion(bf16[2048,352]{0,1:T(8,128)(2,1)S(1)} %fusion.4, bf16[2,352,2048]{2,1,0:T(8,128)(2,1)S(1)} %copy-done.38), kind=kOutput, calls=%fused_computation.1 | convolution fusion | flops 2956984320 | bytes 11272192 | tf_op jit(solution)/shard_map/dot_general | solution.py:92
  262.2 5.1 %all-to-all-start.3 = ((bf16[32,64,2048]{2,1,0:T(8,128)(2,1)}), bf16[32,64,2048]{2,1,0:T(8,128)(2,1)}, u32[]{:S(2)}, u32[]{:S(2)}) async-start(bf16[32,64,2048]{2,1,0:T(8,128)(2,1)} %bitcast.145), calls=%async_computation.4 | async-start | bytes 16777216 | tf_op jit(solution)/shard_map/all_to_all | solution.py:231
  267.5 2.9 fusion.118
  270.4 5.5 %convolution_convert_fusion.3 = bf16[512,2048]{1,0:T(8,128)(2,1)} fusion(bf16[352,2048]{1,0:T(8,128)(2,1)S(1)} %copy-done, bf16[512,2048]{1,0:T(8,128)(2,1)} %all-gather.8.cloned.1.call-done, bf16[352,2048]{1,0:T(8,128)(2,1)} %param.32, f32[512,352]{0,1:T(8,128)S(1)} %fusion.118), kind=kOutput, calls=%fused_computation.11 | convolution fusion | flops 1478524928 | bytes 7798784 | tf_op jit(solution)/shard_map/dot_general | solution.py:92
  276.0 97.2 %all-to-all-done.3 = bf16[32,64,2048]{2,1,0:T(8,128)(2,1)} async-done(((bf16[32,64,2048]{2,1,0:T(8,128)(2,1)}), bf16[32,64,2048]{2,1,0:T(8,128)(2,1)}, u32[]{:S(2)}, u32[]{:S(2)}) %all-to-all-start.3) | async-done | bytes 8388640 | tf_op jit(solution)/shard_map/all_to_all | solution.py:231
  373.2 9.5 %fusion = bf16[512,2048]{1,0:T(8,128)(2,1)} fusion(bf16[512,2048]{1,0:T(8,128)(2,1)} %convolution_convert_fusion.3, bf16[32,64,2048]{2,1,0:T(8,128)(2,1)} %all-to-all-done.3, bf16[512,32]{0,1:T(8,128)(2,1)S(1)} %select_reduce_fusion, s32[512,32]{0,1:T(8,128)S(1)} %copy-done.16, pred[512,32]{0,1:T(8,128)(4,1)S(1)} %copy-done.12), kind=kOutput, calls=%fused_computation.5 | convolution fusion | flops 4301258752 | bytes 12697600 | tf_op jit(solution)/shard_map/dot_general | solution.py:243
  382.8 4.8 %all-to-all-start.1 = ((bf16[32,16,2048]{2,1,0:T(8,128)(2,1)}), bf16[32,16,2048]{2,1,0:T(8,128)(2,1)}, u32[]{:S(2)}, u32[]{:S(2)}) async-start(bf16[32,16,2048]{2,1,0:T(8,128)(2,1)} %bitcast.149), calls=%async_computation.2 | async-start | bytes 4194304 | tf_op jit(solution)/shard_map/all_to_all | solution.py:238
  387.7 20.9 %reduce-scatter.5.cloned.1.call-done = bf16[1,128,2048]{2,1,0:T(8,128)(2,1)} async-done(((bf16[4,128,2048]{2,1,0:T(8,128)(2,1)}), bf16[1,128,2048]{2,1,0:T(8,128)(2,1)}) %reduce-scatter.5.cloned.1.call-update) | async-done | bytes 524304 | tf_op jit(solution)/shard_map/reduce_scatter | solution.py:248
  408.6 9.1 %all-to-all-done.1 = bf16[32,16,2048]{2,1,0:T(8,128)(2,1)} async-done(((bf16[32,16,2048]{2,1,0:T(8,128)(2,1)}), bf16[32,16,2048]{2,1,0:T(8,128)(2,1)}, u32[]{:S(2)}, u32[]{:S(2)}) %all-to-all-start.1) | async-done | bytes 2097184 | tf_op jit(solution)/shard_map/all_to_all | solution.py:238
  417.7 3.0 fusion.9
  (137 shorter events, 15.4 us)
Async XLA Ops:
  6.5 263.9 %copy-start = (bf16[352,2048]{1,0:T(8,128)(2,1)S(1)}, bf16[352,2048]{1,0:T(8,128)(2,1)}, u32[]{:S(2)}) copy-start(bf16[352,2048]{1,0:T(8,128)(2,1)} %param.33) | copy-start | bytes 4325380
  6.5 16.4 %copy-start.4 = (bf16[128,2048]{1,0:T(8,128)(2,1)S(1)}, bf16[128,2048]{1,0:T(8,128)(2,1)}, u32[]{:S(2)}) copy-start(bf16[128,2048]{1,0:T(8,128)(2,1)} %param.19) | copy-start | bytes 1572868
  6.5 53.4 %all-gather.4.cloned.1.call-start = ((), (), s32[]{:S(2)}) async-start(), calls=%async_computation.6 | async-start | bytes 5242880 | tf_op jit(solution)/shard_map/all_gather | solution.py:138
  6.6 16.8 %copy-start.6 = (bf16[2,128,512]{2,1,0:T(8,128)(2,1)S(1)}, bf16[2,128,512]{2,1,0:T(8,128)(2,1)}, u32[]{:S(2)}) copy-start(bf16[2,128,512]{2,1,0:T(8,128)(2,1)} %param.20) | copy-start | bytes 786436
  6.6 16.9 %copy-start.39 = (s32[2,64]{1,0:T(2,128)S(1)}, s32[2,64]{1,0:T(2,128)}, u32[]{:S(2)}) copy-start(s32[2,64]{1,0:T(2,128)} %param.25) | copy-start | bytes 1540
  9.1 15.4 %copy-start.32 = (s32[2,4]{1,0:T(2,128)S(1)}, s32[2,4]{1,0:T(2,128)}, u32[]{:S(2)}) copy-start(s32[2,4]{1,0:T(2,128)} %param.23) | copy-start | bytes 100
  9.1 16.4 %copy-start.31 = (bf16[2048]{0:T(1024)(128)(2,1)S(1)}, bf16[2048]{0:T(1024)(128)(2,1)}, u32[]{:S(2)}) copy-start(bf16[2048]{0:T(1024)(128)(2,1)} %param.27) | copy-start | bytes 12292
  9.1 17.6 %copy-start.33 = (s32[2]{0:T(128)S(1)}, s32[2]{0:T(128)}, u32[]{:S(2)}) copy-start(s32[2]{0:T(128)} %param.24) | copy-start | bytes 28
  9.1 113.1 %all-gather.8.cloned.1.call-start = ((), (), s32[]{:S(2)}) async-start(), calls=%async_computation.9 | async-start | bytes 2621440 | tf_op jit(solution)/shard_map/all_gather | solution.py:165
  23.4 5.2 %copy-start.1 = (bf16[2,64,4,4,128]{4,3,2,1,0:T(4,128)(2,1)}, bf16[2,64,4,4,128]{4,3,2,1,0:T(4,128)(2,1)S(1)}, u32[]{:S(2)}) copy-start(bf16[2,64,4,4,128]{4,3,2,1,0:T(4,128)(2,1)S(1)} %reshape.106) | copy-start | bytes 1572868
  63.0 3.8 copy-start.2
  72.8 4.8 %copy-start.23 = (f32[2048]{0:T(1024)S(1)}, f32[2048]{0:T(1024)}, u32[]{:S(2)}) copy-start(f32[2048]{0:T(1024)} %convert_element_type.139) | copy-start | bytes 24580
  78.6 119.4 %all-gather.6.cloned.1.call-start = ((), (), s32[]{:S(2)}) async-start(), calls=%async_computation.7 | async-start | bytes 10485760 | tf_op jit(solution)/shard_map/all_gather | solution.py:220
  130.6 111.1 %all-to-all-start.2 = ((bf16[32,64,2048]{2,1,0:T(8,128)(2,1)}), bf16[32,64,2048]{2,1,0:T(8,128)(2,1)}, u32[]{:S(2)}, u32[]{:S(2)}) async-start(bf16[32,64,2048]{2,1,0:T(8,128)(2,1)} %bitcast.144), calls=%async_computation.3 | async-start | bytes 16777216 | tf_op jit(solution)/shard_map/all_to_all | solution.py:213
  135.8 246.9 %reduce-scatter.3.cloned.1.call-start = ((), (), s32[]{:S(2)}) async-start(), calls=%async_computation.8 | async-start | bytes 10485760 | tf_op jit(solution)/shard_map/reduce_scatter | solution.py:225
  198.0 6.5 %copy-start.34 = (bf16[128,16,2048]{2,1,0:T(8,128)(2,1)S(1)}, bf16[128,16,2048]{2,1,0:T(8,128)(2,1)}, u32[]{:S(2)}) copy-start(bf16[128,16,2048]{2,1,0:T(8,128)(2,1)} %all-gather.6.cloned.1.call-done) | copy-start | bytes 25165828
  198.0 7.1 %copy-start.35 = (bf16[2,352,2048]{2,1,0:T(8,128)(2,1)S(1)}, bf16[2,352,2048]{2,1,0:T(8,128)(2,1)}, u32[]{:S(2)}) copy-start(bf16[2,352,2048]{2,1,0:T(8,128)(2,1)} %param.29) | copy-start | bytes 8650756
  205.1 3.5 copy-start.37
  241.7 6.2 %copy-start.36 = (bf16[2,352,2048]{2,1,0:T(8,128)(2,1)S(1)}, bf16[2,352,2048]{2,1,0:T(8,128)(2,1)}, u32[]{:S(2)}) copy-start(bf16[2,352,2048]{2,1,0:T(8,128)(2,1)} %param.29) | copy-start | bytes 8650756
  247.9 7.1 %copy-start.38 = (bf16[2,352,2048]{2,1,0:T(8,128)(2,1)S(1)}, bf16[2,352,2048]{2,1,0:T(8,128)(2,1)}, u32[]{:S(2)}) copy-start(bf16[2,352,2048]{2,1,0:T(8,128)(2,1)} %param.30) | copy-start | bytes 8650756
  262.2 5.2 %copy-start.8 = (f32[512,12]{0,1:T(8,128)S(1)}, f32[512,12]{0,1:T(8,128)}, u32[]{:S(2)}) copy-start(f32[512,12]{0,1:T(8,128)} %all_gather.12) | copy-start | bytes 73732
  262.2 5.2 %copy-start.22 = (pred[512,6]{0,1:T(8,128)(4,1)S(1)}, pred[512,6]{0,1:T(8,128)(4,1)}, u32[]{:S(2)}) copy-start(pred[512,6]{0,1:T(8,128)(4,1)} %copy-done.21) | copy-start | bytes 9220
  262.2 111.0 %all-to-all-start.3 = ((bf16[32,64,2048]{2,1,0:T(8,128)(2,1)}), bf16[32,64,2048]{2,1,0:T(8,128)(2,1)}, u32[]{:S(2)}, u32[]{:S(2)}) async-start(bf16[32,64,2048]{2,1,0:T(8,128)(2,1)} %bitcast.145), calls=%async_computation.4 | async-start | bytes 16777216 | tf_op jit(solution)/shard_map/all_to_all | solution.py:231
  267.3 141.3 %reduce-scatter.5.cloned.1.call-start = ((), (), s32[]{:S(2)}) async-start(), calls=%async_computation.10 | async-start | bytes 2621440 | tf_op jit(solution)/shard_map/reduce_scatter | solution.py:248
  270.4 102.8 %copy-start.12 = (pred[512,32]{0,1:T(8,128)(4,1)S(1)}, pred[512,32]{0,1:T(8,128)(4,1)}, u32[]{:S(2)}) copy-start(pred[512,32]{0,1:T(8,128)(4,1)} %copy-done.11) | copy-start | bytes 49156
  270.4 102.8 %copy-start.16 = (s32[512,32]{0,1:T(8,128)S(1)}, s32[512,32]{0,1:T(8,128)}, u32[]{:S(2)}) copy-start(s32[512,32]{0,1:T(8,128)} %copy-done.15) | copy-start | bytes 196612
  382.8 4.8 %copy-start.20 = (s32[128,6]{0,1:T(8,128)S(1)}, s32[128,6]{0,1:T(8,128)}, u32[]{:S(2)}) copy-start(s32[128,6]{0,1:T(8,128)} %get-tuple-element.22) | copy-start | bytes 9220
  382.8 4.8 %copy-start.27 = (f32[128,6]{0,1:T(8,128)S(1)}, f32[128,6]{0,1:T(8,128)}, u32[]{:S(2)}) copy-start(f32[128,6]{0,1:T(8,128)} %param.35) | copy-start | bytes 9220
  382.8 4.8 %copy-start.30 = (pred[128,6]{0,1:T(8,128)(4,1)S(1)}, pred[128,6]{0,1:T(8,128)(4,1)}, u32[]{:S(2)}) copy-start(pred[128,6]{0,1:T(8,128)(4,1)} %copy-done.29) | copy-start | bytes 2308
  382.8 34.9 %copy-start.14 = (s32[128,32]{0,1:T(8,128)S(1)}, s32[128,32]{0,1:T(8,128)}, u32[]{:S(2)}) copy-start(s32[128,32]{0,1:T(8,128)} %copy-done.13) | copy-start | bytes 49156
  382.8 34.9 %copy-start.18 = (pred[128,32]{0,1:T(8,128)(4,1)S(1)}, pred[128,32]{0,1:T(8,128)(4,1)}, u32[]{:S(2)}) copy-start(pred[128,32]{0,1:T(8,128)(4,1)} %copy-done.17) | copy-start | bytes 12292
  382.8 34.9 %all-to-all-start.1 = ((bf16[32,16,2048]{2,1,0:T(8,128)(2,1)}), bf16[32,16,2048]{2,1,0:T(8,128)(2,1)}, u32[]{:S(2)}, u32[]{:S(2)}) async-start(bf16[32,16,2048]{2,1,0:T(8,128)(2,1)} %bitcast.149), calls=%async_computation.2 | async-start | bytes 4194304 | tf_op jit(solution)/shard_map/all_to_all | solution.py:238
  (16 other events, 21.2 us)
Sparse Core Ops, SparseCore 0:
  9.2 50.6 all-gather.3
  78.7 31.1 all-gather.7
  118.1 79.8 all-gather.5
  215.7 81.4 reduce-scatter.2
  382.9 25.6 reduce-scatter.4

commit v7 on v6

--- a/solution.py
+++ b/solution.py
@@ -86,8 +86,15 @@
 
 
 def shared_block(tokens, gate_rows, upper_rows, down_rows):
-    gate_values = jnp.einsum("td,fd->tf", tokens, gate_rows, preferred_element_type=jnp.float32)
-    upper_values = jnp.einsum("td,fd->tf", tokens, upper_rows, preferred_element_type=jnp.float32)
+    unit_count = gate_rows.shape[0]
+    both_values = jnp.einsum(
+        "td,fd->tf",
+        tokens,
+        jnp.concatenate([gate_rows, upper_rows], axis=0),
+        preferred_element_type=jnp.float32,
+    )
+    gate_values = both_values[:, :unit_count]
+    upper_values = both_values[:, unit_count:]
     inner = (jax.nn.silu(gate_values) * upper_values).astype(jnp.bfloat16)
     return jnp.dot(inner, down_rows, preferred_element_type=jnp.float32)
 

time: 428 us -> 424 us (level)
  matrix products: 79.6 us -> 73.9 us
  local copies, waits for them, and re-layouts: 13.8 us -> 18.5 us
    squeeze x0 -> x1, local copies, waits for them, and re-layouts: none -> 5.52 us  [on_device(): expert_up[1]]
    all_gather x1, waiting for transfers between devices: 62.2 us -> 56.8 us  [on_device(): lax.all_gather(near_arrived, 'dp', axis=0, tiled=True)]
    dot_general x5 -> x3, matrix products: 26.2 us -> 23.4 us  [shared_block(): jnp.einsum('td,fd->tf', tokens, jnp.concatenate([gate_rows, upper_rows],...]
where the time goes in v7:
time: 424 us; the launch traced here: 423 us
  waiting for transfers between devices  244 us (58%)
  matrix products  73.9 us (17%)
  blocking collectives  48.8 us (12%)
  local copies, waits for them, and re-layouts  18.5 us (4%)
  starting transfers between devices  15.5 us (4%)
  between operations  13.7 us (3%)
  other arithmetic  9.06 us (2%)
    all_to_all x1, waiting for transfers between devices, on_device(): lax.all_to_all(far_terms.astype(jnp.bfloat16).reshape(column_count, far_c...  98.6 us
    all_gather x1, waiting for transfers between devices, on_device(): lax.all_gather(near_arrived, 'dp', axis=0, tiled=True)  56.8 us
    all_to_all x1, blocking collectives, on_device(): lax.all_to_all(near_out.reshape(column_count, near_cap, model_width), 'ex...  35.6 us
    all_gather x1, waiting for transfers between devices, on_device(): lax.all_gather(jnp.stack([key_pool, value_pool]), 'dp', axis=1, tiled=True)  31.3 us
    all_to_all x1, waiting for transfers between devices, on_device(): lax.all_to_all(far_out.reshape(column_count, far_cap, model_width), 'exp'...  26.9 us
    dot_general x3, matrix products, shared_block(): jnp.einsum('td,fd->tf', tokens, jnp.concatenate([gate_rows, upper_rows],...  23.4 us
    reduce_scatter x1, waiting for transfers between devices, on_device(): lax.psum_scatter(far_part.astype(jnp.bfloat16).reshape(row_count, tok_row...  21 us
    dot_general x3, matrix products, shared_block(): return jnp.dot(inner, down_rows, preferred_element_type=jnp.float32)  16.8 us
  transfers between devices with their start and end apart: 8, of which 6 were waited for; matrix products, arithmetic and copies ran while one was open for 18% of the time, Pallas kernels for 0%

profile of v7, /device:TPU:0, one launch (start us, length us, event | category | flops | bytes accessed | tf_op | source)
XLA Modules:
  0.0 423.2 jit_solution(13663611449779244452)
XLA Ops:
  6.6 2.5 pad_maximum_fusion
  9.8 13.2 %all_gather.12 = f32[512,12]{0,1:T(8,128)} all-gather(f32[128,12]{0,1:T(8,128)S(1)} %pad_maximum_fusion.1), channel_id=1, replica_groups=mesh['dp'=4,'exp'=32] {'dp'}, dimensions={0}, use_global_device_ids=true | all-gather | bytes 30720 | tf_op jit(solution)/shard_map/all_gather | solution.py:123
  27.4 1.3 fusion.124
  28.6 31.3 %all-gather.4.cloned.1.call-done = bf16[2,32,64,512]{3,2,1,0:T(8,128)(2,1)} async-done(((bf16[2,8,64,512]{3,2,1,0:T(8,128)(2,1)}), bf16[2,32,64,512]{3,2,1,0:T(8,128)(2,1)}) %all-gather.4.cloned.1.call-update) | async-done | bytes 4194320 | tf_op jit(solution)/shard_map/all_gather | solution.py:145
  60.0 2.9 gather_fusion
  63.9 2.0 reshape_squeeze.14
  66.8 1.7 bitcast_reduce_fusion
  68.5 0.9 fusion.28
  70.6 1.2 fusion.44
  72.7 4.8 %multiply_reduce_fusion = (f32[128]{0:T(128)S(1)}, f32[128,2048]{1,0:T(8,128)S(1)}) fusion(bf16[128,2048]{1,0:T(8,128)(2,1)S(1)} %convert_element_type.134, bf16[2048,2048]{1,0:T(8,128)(2,1)} %param.26, bf16[128,2048]{1,0:T(8,128)(2,1)S(1)} %copy-done.3), kind=kOutput, calls=%fused_computation.85 | convolution fusion | flops 1075314560 | bytes 10486272 | tf_op jit(solution)/shard_map/dot_general | solution.py:160
  77.5 1.0 multiply_convert_fusion
  80.5 1.7 convolution_convert_fusion.4
  82.3 35.6 %all_to_all.20 = bf16[32,16,2048]{2,1,0:T(8,128)(2,1)} all-to-all(bf16[32,16,2048]{2,1,0:T(8,128)(2,1)S(1)} %bitcast.135), channel_id=1, replica_groups=mesh['dp'=4,'exp'=32] {'exp'}, dimensions={0} | all-to-all | bytes 4194304 | tf_op jit(solution)/shard_map/all_to_all | solution.py:213
  120.4 1.6 fusion.2
  122.0 8.4 %convolution_convert_fusion.1 = bf16[2048,2048]{1,0:T(8,128)(2,1)} fusion(pred[512,2048]{0,1:T(32,128)(4,1)S(1)} %fusion.2, bf16[512,2048]{1,0:T(8,128)(2,1)} %all-gather.8.cloned.1.call-done), kind=kOutput, calls=%fused_computation.2 | convolution fusion | flops 4299161600 | bytes 11534336 | tf_op jit(solution)/shard_map/ts,td->sd/dot_general | solution.py:207
  130.4 5.2 %all-to-all-start.2 = ((bf16[32,64,2048]{2,1,0:T(8,128)(2,1)}), bf16[32,64,2048]{2,1,0:T(8,128)(2,1)}, u32[]{:S(2)}, u32[]{:S(2)}) async-start(bf16[32,64,2048]{2,1,0:T(8,128)(2,1)} %bitcast.133), calls=%async_computation.3 | async-start | bytes 16777216 | tf_op jit(solution)/shard_map/all_to_all | solution.py:220
  135.6 5.5 %slice_bitcast_fusion = (bf16[352,2048]{1,0:T(8,128)(2,1)}, bf16[352,2048]{1,0:T(8,128)(2,1)}, bf16[352,2048]{1,0:T(8,128)(2,1)}, bf16[352,2048]{1,0:T(8,128)(2,1)}) fusion(bf16[2,352,2048]{2,1,0:T(8,128)(2,1)} %param.29, bf16[2,352,2048]{2,1,0:T(8,128)(2,1)} %param.28), kind=kLoop, calls=%fused_computation.50 | loop fusion | bytes 11534336 | tf_op jit(solution)/shard_map/squeeze | solution.py:230
  141.2 56.8 %all-gather.6.cloned.1.call-done = bf16[128,16,2048]{2,1,0:T(8,128)(2,1)} async-done(((bf16[32,16,2048]{2,1,0:T(8,128)(2,1)}), bf16[128,16,2048]{2,1,0:T(8,128)(2,1)}) %all-gather.6.cloned.1.call-update) | async-done | bytes 8388624 | tf_op jit(solution)/shard_map/all_gather | solution.py:227
  197.9 9.6 %fusion.5 = f32[2048,704]{0,1:T(8,128)S(1)} fusion(bf16[2048,2048]{1,0:T(8,128)(2,1)} %bitcast.146, bf16[352,2048]{1,0:T(8,128)(2,1)} %get-tuple-element.18, bf16[352,2048]{1,0:T(8,128)(2,1)} %get-tuple-element.34), kind=kOutput, calls=%fused_computation.17 | convolution fusion | flops 5911347200 | bytes 17039360 | tf_op jit(solution)/shard_map/td,fd->tf/dot_general | solution.py:90
  207.5 7.0 %convolution_convert_fusion.2 = bf16[2048,2048]{1,0:T(8,128)(2,1)} fusion(f32[2048,704]{0,1:T(8,128)S(1)} %fusion.5, bf16[2,352,2048]{2,1,0:T(8,128)(2,1)S(1)} %copy-done.34), kind=kOutput, calls=%fused_computation.3 | convolution fusion | flops 2961309696 | bytes 15597568 | tf_op jit(solution)/shard_map/dot_general | solution.py:99
  214.6 26.9 %all-to-all-done.2 = bf16[32,64,2048]{2,1,0:T(8,128)(2,1)} async-done(((bf16[32,64,2048]{2,1,0:T(8,128)(2,1)}), bf16[32,64,2048]{2,1,0:T(8,128)(2,1)}, u32[]{:S(2)}, u32[]{:S(2)}) %all-to-all-start.2) | async-done | bytes 8388640 | tf_op jit(solution)/shard_map/all_to_all | solution.py:220
  241.5 9.7 %fusion.9 = f32[2048,704]{0,1:T(8,128)S(1)} fusion(bf16[2048,2048]{1,0:T(8,128)(2,1)} %bitcast.29, bf16[352,2048]{1,0:T(8,128)(2,1)} %get-tuple-element.17, bf16[352,2048]{1,0:T(8,128)(2,1)} %get-tuple-element.35), kind=kOutput, calls=%fused_computation.21 | convolution fusion | flops 5911347200 | bytes 17039360 | tf_op jit(solution)/shard_map/td,fd->tf/dot_general | solution.py:90
  251.2 7.1 %convolution_convert_fusion = bf16[2048,2048]{1,0:T(8,128)(2,1)} fusion(f32[2048,704]{0,1:T(8,128)S(1)} %fusion.9, bf16[2,352,2048]{2,1,0:T(8,128)(2,1)S(1)} %copy-done.35), kind=kOutput, calls=%fused_computation.1 | convolution fusion | flops 2961309696 | bytes 15597568 | tf_op jit(solution)/shard_map/dot_general | solution.py:99
  258.2 5.1 %all-to-all-start.3 = ((bf16[32,64,2048]{2,1,0:T(8,128)(2,1)}), bf16[32,64,2048]{2,1,0:T(8,128)(2,1)}, u32[]{:S(2)}, u32[]{:S(2)}) async-start(bf16[32,64,2048]{2,1,0:T(8,128)(2,1)} %bitcast.134), calls=%async_computation.4 | async-start | bytes 16777216 | tf_op jit(solution)/shard_map/all_to_all | solution.py:238
  263.8 4.1 fusion.13
  267.9 2.7 convolution_convert_fusion.3
  270.7 98.6 %all-to-all-done.3 = bf16[32,64,2048]{2,1,0:T(8,128)(2,1)} async-done(((bf16[32,64,2048]{2,1,0:T(8,128)(2,1)}), bf16[32,64,2048]{2,1,0:T(8,128)(2,1)}, u32[]{:S(2)}, u32[]{:S(2)}) %all-to-all-start.3) | async-done | bytes 8388640 | tf_op jit(solution)/shard_map/all_to_all | solution.py:238
  369.2 9.6 %fusion = bf16[512,2048]{1,0:T(8,128)(2,1)} fusion(bf16[512,2048]{1,0:T(8,128)(2,1)} %convolution_convert_fusion.3, bf16[32,64,2048]{2,1,0:T(8,128)(2,1)} %all-to-all-done.3, bf16[512,32]{0,1:T(8,128)(2,1)S(1)} %select_reduce_fusion, s32[512,32]{0,1:T(8,128)S(1)} %copy-done.16, pred[512,32]{0,1:T(8,128)(4,1)S(1)} %copy-done.12), kind=kOutput, calls=%fused_computation.5 | convolution fusion | flops 4301258752 | bytes 12697600 | tf_op jit(solution)/shard_map/dot_general | solution.py:250
  378.9 4.8 %all-to-all-start.1 = ((bf16[32,16,2048]{2,1,0:T(8,128)(2,1)}), bf16[32,16,2048]{2,1,0:T(8,128)(2,1)}, u32[]{:S(2)}, u32[]{:S(2)}) async-start(bf16[32,16,2048]{2,1,0:T(8,128)(2,1)} %bitcast.138), calls=%async_computation.2 | async-start | bytes 4194304 | tf_op jit(solution)/shard_map/all_to_all | solution.py:245
  383.7 21.0 %reduce-scatter.5.cloned.1.call-done = bf16[1,128,2048]{2,1,0:T(8,128)(2,1)} async-done(((bf16[4,128,2048]{2,1,0:T(8,128)(2,1)}), bf16[1,128,2048]{2,1,0:T(8,128)(2,1)}) %reduce-scatter.5.cloned.1.call-update) | async-done | bytes 524304 | tf_op jit(solution)/shard_map/reduce_scatter | solution.py:255
  404.7 9.0 %all-to-all-done.1 = bf16[32,16,2048]{2,1,0:T(8,128)(2,1)} async-done(((bf16[32,16,2048]{2,1,0:T(8,128)(2,1)}), bf16[32,16,2048]{2,1,0:T(8,128)(2,1)}, u32[]{:S(2)}, u32[]{:S(2)}) %all-to-all-start.1) | async-done | bytes 2097184 | tf_op jit(solution)/shard_map/all_to_all | solution.py:245
  413.7 3.0 fusion.21
  (130 shorter events, 13.9 us)
Async XLA Ops:
  6.5 261.4 %copy-start = (bf16[352,2048]{1,0:T(8,128)(2,1)S(1)}, bf16[352,2048]{1,0:T(8,128)(2,1)}, u32[]{:S(2)}) copy-start(bf16[352,2048]{1,0:T(8,128)(2,1)} %param.33) | copy-start | bytes 4325380
  6.5 16.5 %copy-start.4 = (bf16[128,2048]{1,0:T(8,128)(2,1)S(1)}, bf16[128,2048]{1,0:T(8,128)(2,1)}, u32[]{:S(2)}) copy-start(bf16[128,2048]{1,0:T(8,128)(2,1)} %param.19) | copy-start | bytes 1572868
  6.5 16.9 %copy-start.6 = (bf16[2,128,512]{2,1,0:T(8,128)(2,1)S(1)}, bf16[2,128,512]{2,1,0:T(8,128)(2,1)}, u32[]{:S(2)}) copy-start(bf16[2,128,512]{2,1,0:T(8,128)(2,1)} %param.20) | copy-start | bytes 786436
  6.5 17.0 %copy-start.36 = (s32[2,64]{1,0:T(2,128)S(1)}, s32[2,64]{1,0:T(2,128)}, u32[]{:S(2)}) copy-start(s32[2,64]{1,0:T(2,128)} %param.25) | copy-start | bytes 1540
  6.6 18.0 %copy-start.32 = (s32[2,4]{1,0:T(2,128)S(1)}, s32[2,4]{1,0:T(2,128)}, u32[]{:S(2)}) copy-start(s32[2,4]{1,0:T(2,128)} %param.23) | copy-start | bytes 100
  6.6 53.4 %all-gather.4.cloned.1.call-start = ((), (), s32[]{:S(2)}) async-start(), calls=%async_computation.6 | async-start | bytes 5242880 | tf_op jit(solution)/shard_map/all_gather | solution.py:145
  6.6 18.9 %copy-start.31 = (bf16[2048]{0:T(1024)(128)(2,1)S(1)}, bf16[2048]{0:T(1024)(128)(2,1)}, u32[]{:S(2)}) copy-start(bf16[2048]{0:T(1024)(128)(2,1)} %param.27) | copy-start | bytes 12292
  6.6 20.1 %copy-start.33 = (s32[2]{0:T(128)S(1)}, s32[2]{0:T(128)}, u32[]{:S(2)}) copy-start(s32[2]{0:T(128)} %param.24) | copy-start | bytes 28
  9.1 112.9 %all-gather.8.cloned.1.call-start = ((), (), s32[]{:S(2)}) async-start(), calls=%async_computation.9 | async-start | bytes 2621440 | tf_op jit(solution)/shard_map/all_gather | solution.py:172
  23.4 5.2 %copy-start.1 = (bf16[2,64,4,4,128]{4,3,2,1,0:T(4,128)(2,1)}, bf16[2,64,4,4,128]{4,3,2,1,0:T(4,128)(2,1)S(1)}, u32[]{:S(2)}) copy-start(bf16[2,64,4,4,128]{4,3,2,1,0:T(4,128)(2,1)S(1)} %reshape.106) | copy-start | bytes 1572868
  63.0 3.8 copy-start.2
  72.6 4.8 %copy-start.23 = (f32[2048]{0:T(1024)S(1)}, f32[2048]{0:T(1024)}, u32[]{:S(2)}) copy-start(f32[2048]{0:T(1024)} %convert_element_type.139) | copy-start | bytes 24580
  72.6 5.9 %copy-start.25 = (s32[128,6]{0,1:T(8,128)S(1)}, s32[128,6]{0,1:T(8,128)}, u32[]{:S(2)}) copy-start(s32[128,6]{0,1:T(8,128)} %param.34) | copy-start | bytes 9220
  72.6 6.5 %copy-start.19 = (s32[128,6]{0,1:T(8,128)S(1)}, s32[128,6]{0,1:T(8,128)}, u32[]{:S(2)}) copy-start(s32[128,6]{0,1:T(8,128)} %get-tuple-element.26) | copy-start | bytes 9220
  78.4 119.5 %all-gather.6.cloned.1.call-start = ((), (), s32[]{:S(2)}) async-start(), calls=%async_computation.7 | async-start | bytes 10485760 | tf_op jit(solution)/shard_map/all_gather | solution.py:227
  82.3 36.3 %copy-start.7 = (f32[512,12]{0,1:T(8,128)S(1)}, f32[512,12]{0,1:T(8,128)}, u32[]{:S(2)}) copy-start(f32[512,12]{0,1:T(8,128)} %all_gather.12) | copy-start | bytes 73732
  130.4 111.1 %all-to-all-start.2 = ((bf16[32,64,2048]{2,1,0:T(8,128)(2,1)}), bf16[32,64,2048]{2,1,0:T(8,128)(2,1)}, u32[]{:S(2)}, u32[]{:S(2)}) async-start(bf16[32,64,2048]{2,1,0:T(8,128)(2,1)} %bitcast.133), calls=%async_computation.3 | async-start | bytes 16777216 | tf_op jit(solution)/shard_map/all_to_all | solution.py:220
  135.6 243.3 %reduce-scatter.3.cloned.1.call-start = ((), (), s32[]{:S(2)}) async-start(), calls=%async_computation.8 | async-start | bytes 10485760 | tf_op jit(solution)/shard_map/reduce_scatter | solution.py:232
  197.9 9.6 %copy-start.34 = (bf16[2,352,2048]{2,1,0:T(8,128)(2,1)S(1)}, bf16[2,352,2048]{2,1,0:T(8,128)(2,1)}, u32[]{:S(2)}) copy-start(bf16[2,352,2048]{2,1,0:T(8,128)(2,1)} %param.30) | copy-start | bytes 8650756
  241.5 9.7 %copy-start.35 = (bf16[2,352,2048]{2,1,0:T(8,128)(2,1)S(1)}, bf16[2,352,2048]{2,1,0:T(8,128)(2,1)}, u32[]{:S(2)}) copy-start(bf16[2,352,2048]{2,1,0:T(8,128)(2,1)} %param.30) | copy-start | bytes 8650756
  258.2 5.4 %copy-start.8 = (f32[512,12]{0,1:T(8,128)S(1)}, f32[512,12]{0,1:T(8,128)}, u32[]{:S(2)}) copy-start(f32[512,12]{0,1:T(8,128)} %all_gather.12) | copy-start | bytes 73732
  258.2 5.4 %copy-start.22 = (pred[512,6]{0,1:T(8,128)(4,1)S(1)}, pred[512,6]{0,1:T(8,128)(4,1)}, u32[]{:S(2)}) copy-start(pred[512,6]{0,1:T(8,128)(4,1)} %copy-done.21) | copy-start | bytes 9220
  258.2 111.0 %all-to-all-start.3 = ((bf16[32,64,2048]{2,1,0:T(8,128)(2,1)}), bf16[32,64,2048]{2,1,0:T(8,128)(2,1)}, u32[]{:S(2)}, u32[]{:S(2)}) async-start(bf16[32,64,2048]{2,1,0:T(8,128)(2,1)} %bitcast.134), calls=%async_computation.4 | async-start | bytes 16777216 | tf_op jit(solution)/shard_map/all_to_all | solution.py:238
  263.4 141.4 %reduce-scatter.5.cloned.1.call-start = ((), (), s32[]{:S(2)}) async-start(), calls=%async_computation.10 | async-start | bytes 2621440 | tf_op jit(solution)/shard_map/reduce_scatter | solution.py:255
  267.9 101.3 %copy-start.12 = (pred[512,32]{0,1:T(8,128)(4,1)S(1)}, pred[512,32]{0,1:T(8,128)(4,1)}, u32[]{:S(2)}) copy-start(pred[512,32]{0,1:T(8,128)(4,1)} %copy-done.11) | copy-start | bytes 49156
  267.9 101.3 %copy-start.16 = (s32[512,32]{0,1:T(8,128)S(1)}, s32[512,32]{0,1:T(8,128)}, u32[]{:S(2)}) copy-start(s32[512,32]{0,1:T(8,128)} %copy-done.15) | copy-start | bytes 196612
  378.8 4.9 %copy-start.20 = (s32[128,6]{0,1:T(8,128)S(1)}, s32[128,6]{0,1:T(8,128)}, u32[]{:S(2)}) copy-start(s32[128,6]{0,1:T(8,128)} %get-tuple-element.26) | copy-start | bytes 9220
  378.8 4.9 %copy-start.27 = (f32[128,6]{0,1:T(8,128)S(1)}, f32[128,6]{0,1:T(8,128)}, u32[]{:S(2)}) copy-start(f32[128,6]{0,1:T(8,128)} %param.35) | copy-start | bytes 9220
  378.8 4.9 %copy-start.30 = (pred[128,6]{0,1:T(8,128)(4,1)S(1)}, pred[128,6]{0,1:T(8,128)(4,1)}, u32[]{:S(2)}) copy-start(pred[128,6]{0,1:T(8,128)(4,1)} %copy-done.29) | copy-start | bytes 2308
  378.8 34.9 %copy-start.14 = (s32[128,32]{0,1:T(8,128)S(1)}, s32[128,32]{0,1:T(8,128)}, u32[]{:S(2)}) copy-start(s32[128,32]{0,1:T(8,128)} %copy-done.13) | copy-start | bytes 49156
  378.8 34.9 %copy-start.18 = (pred[128,32]{0,1:T(8,128)(4,1)S(1)}, pred[128,32]{0,1:T(8,128)(4,1)}, u32[]{:S(2)}) copy-start(pred[128,32]{0,1:T(8,128)(4,1)} %copy-done.17) | copy-start | bytes 12292
  378.9 34.9 %all-to-all-start.1 = ((bf16[32,16,2048]{2,1,0:T(8,128)(2,1)}), bf16[32,16,2048]{2,1,0:T(8,128)(2,1)}, u32[]{:S(2)}, u32[]{:S(2)}) async-start(bf16[32,16,2048]{2,1,0:T(8,128)(2,1)} %bitcast.138), calls=%async_computation.2 | async-start | bytes 4194304 | tf_op jit(solution)/shard_map/all_to_all | solution.py:245
  (13 other events, 18.7 us)
Sparse Core Ops, SparseCore 0:
  9.3 50.6 all-gather.3
  78.5 31.1 all-gather.7
  118.0 79.8 all-gather.5
  214.7 81.4 reduce-scatter.2
  379.0 25.6 reduce-scatter.4

commit v8 on v7

--- a/solution.py
+++ b/solution.py
@@ -19,12 +19,13 @@
     node_index = jnp.arange(node_count, dtype=jnp.int32)
     linked = (parents[:, :, None] == node_index[None, None, :]).astype(jnp.float32)
     reached = jnp.minimum(linked + jnp.eye(node_count, dtype=jnp.float32)[None], 1.0)
-    for rounds in range(max(1, (node_count - 1).bit_length())):
+    def square(rounds, reached):
         flags = reached.astype(jnp.bfloat16)
-        reached = jnp.minimum(
+        return jnp.minimum(
             jnp.einsum("rij,rjk->rik", flags, flags, preferred_element_type=jnp.float32), 1.0
         )
-    return reached
+
+    return lax.fori_loop(0, max(1, (node_count - 1).bit_length()), square, reached)
 
 
 def score_block(query_heads, key_rows, live_mask):

time: 424 us -> 424 us (level)
  no operation moved by 1% of the time
where the time goes in v8:
time: 424 us; the launch traced here: 423 us
  waiting for transfers between devices  244 us (58%)
  matrix products  73.8 us (17%)
  blocking collectives  48.8 us (12%)
  local copies, waits for them, and re-layouts  18.5 us (4%)
  starting transfers between devices  15.5 us (4%)
  between operations  13.7 us (3%)
  other arithmetic  9.18 us (2%)
    all_to_all x1, waiting for transfers between devices, on_device(): lax.all_to_all(far_terms.astype(jnp.bfloat16).reshape(column_count, far_c...  98.6 us
    all_gather x1, waiting for transfers between devices, on_device(): lax.all_gather(near_arrived, 'dp', axis=0, tiled=True)  56.7 us
    all_to_all x1, blocking collectives, on_device(): lax.all_to_all(near_out.reshape(column_count, near_cap, model_width), 'ex...  35.6 us
    all_gather x1, waiting for transfers between devices, on_device(): lax.all_gather(jnp.stack([key_pool, value_pool]), 'dp', axis=1, tiled=True)  31.3 us
    all_to_all x1, waiting for transfers between devices, on_device(): lax.all_to_all(far_out.reshape(column_count, far_cap, model_width), 'exp'...  26.9 us
    dot_general x3, matrix products, shared_block(): jnp.einsum('td,fd->tf', tokens, jnp.concatenate([gate_rows, upper_rows],...  23.4 us
    reduce_scatter x1, waiting for transfers between devices, on_device(): lax.psum_scatter(far_part.astype(jnp.bfloat16).reshape(row_count, tok_row...  21 us
    dot_general x3, matrix products, shared_block(): return jnp.dot(inner, down_rows, preferred_element_type=jnp.float32)  16.8 us
  transfers between devices with their start and end apart: 8, of which 6 were waited for; matrix products, arithmetic and copies ran while one was open for 18% of the time, Pallas kernels for 0%

profile of v8, /device:TPU:0, one launch (start us, length us, event | category | flops | bytes accessed | tf_op | source)
XLA Modules:
  0.0 423.2 jit_solution(9869194093991938870)
XLA Ops:
  6.6 2.5 pad_maximum_fusion
  9.8 13.3 %all_gather.12 = f32[512,12]{0,1:T(8,128)} all-gather(f32[128,12]{0,1:T(8,128)S(1)} %pad_maximum_fusion.1), channel_id=1, replica_groups=mesh['dp'=4,'exp'=32] {'dp'}, dimensions={0}, use_global_device_ids=true | all-gather | bytes 30720 | tf_op jit(solution)/shard_map/all_gather | solution.py:124
  27.4 1.3 fusion.107
  28.7 31.3 %all-gather.4.cloned.1.call-done = bf16[2,32,64,512]{3,2,1,0:T(8,128)(2,1)} async-done(((bf16[2,8,64,512]{3,2,1,0:T(8,128)(2,1)}), bf16[2,32,64,512]{3,2,1,0:T(8,128)(2,1)}) %all-gather.4.cloned.1.call-update) | async-done | bytes 4194320 | tf_op jit(solution)/shard_map/all_gather | solution.py:146
  60.0 2.9 gather_fusion
  63.9 2.0 reshape_squeeze.14
  66.8 1.7 bitcast_reduce_fusion
  68.5 0.9 fusion.29
  70.6 1.2 fusion.45
  72.7 4.8 %multiply_reduce_fusion = (f32[128]{0:T(128)S(1)}, f32[128,2048]{1,0:T(8,128)S(1)}) fusion(bf16[128,2048]{1,0:T(8,128)(2,1)S(1)} %convert_element_type.113, bf16[2048,2048]{1,0:T(8,128)(2,1)} %param.28, bf16[128,2048]{1,0:T(8,128)(2,1)S(1)} %copy-done.3), kind=kOutput, calls=%fused_computation.75 | convolution fusion | flops 1075314560 | bytes 10486272 | tf_op jit(solution)/shard_map/dot_general | solution.py:161
  77.5 1.0 multiply_convert_fusion
  80.5 1.7 convolution_convert_fusion.4
  82.3 35.6 %all_to_all.20 = bf16[32,16,2048]{2,1,0:T(8,128)(2,1)} all-to-all(bf16[32,16,2048]{2,1,0:T(8,128)(2,1)S(1)} %bitcast.131), channel_id=1, replica_groups=mesh['dp'=4,'exp'=32] {'exp'}, dimensions={0} | all-to-all | bytes 4194304 | tf_op jit(solution)/shard_map/all_to_all | solution.py:214
  120.4 1.6 fusion.3
  122.0 8.4 %convolution_convert_fusion.1 = bf16[2048,2048]{1,0:T(8,128)(2,1)} fusion(pred[512,2048]{0,1:T(32,128)(4,1)S(1)} %fusion.3, bf16[512,2048]{1,0:T(8,128)(2,1)} %all-gather.8.cloned.1.call-done), kind=kOutput, calls=%fused_computation.4 | convolution fusion | flops 4299161600 | bytes 11534336 | tf_op jit(solution)/shard_map/ts,td->sd/dot_general | solution.py:208
  130.4 5.2 %all-to-all-start.2 = ((bf16[32,64,2048]{2,1,0:T(8,128)(2,1)}), bf16[32,64,2048]{2,1,0:T(8,128)(2,1)}, u32[]{:S(2)}, u32[]{:S(2)}) async-start(bf16[32,64,2048]{2,1,0:T(8,128)(2,1)} %bitcast.129), calls=%async_computation.3 | async-start | bytes 16777216 | tf_op jit(solution)/shard_map/all_to_all | solution.py:221
  135.6 5.5 %slice_bitcast_fusion = (bf16[352,2048]{1,0:T(8,128)(2,1)}, bf16[352,2048]{1,0:T(8,128)(2,1)}, bf16[352,2048]{1,0:T(8,128)(2,1)}, bf16[352,2048]{1,0:T(8,128)(2,1)}) fusion(bf16[2,352,2048]{2,1,0:T(8,128)(2,1)} %param.31, bf16[2,352,2048]{2,1,0:T(8,128)(2,1)} %param.30), kind=kLoop, calls=%fused_computation.52 | loop fusion | bytes 11534336 | tf_op jit(solution)/shard_map/squeeze | solution.py:231
  141.2 56.7 %all-gather.6.cloned.1.call-done = bf16[128,16,2048]{2,1,0:T(8,128)(2,1)} async-done(((bf16[32,16,2048]{2,1,0:T(8,128)(2,1)}), bf16[128,16,2048]{2,1,0:T(8,128)(2,1)}) %all-gather.6.cloned.1.call-update) | async-done | bytes 8388624 | tf_op jit(solution)/shard_map/all_gather | solution.py:228
  197.9 9.6 %fusion.6 = f32[2048,704]{0,1:T(8,128)S(1)} fusion(bf16[2048,2048]{1,0:T(8,128)(2,1)} %bitcast.142, bf16[352,2048]{1,0:T(8,128)(2,1)} %get-tuple-element.35, bf16[352,2048]{1,0:T(8,128)(2,1)} %get-tuple-element.51), kind=kOutput, calls=%fused_computation.19 | convolution fusion | flops 5911347200 | bytes 17039360 | tf_op jit(solution)/shard_map/td,fd->tf/dot_general | solution.py:91
  207.5 7.0 %convolution_convert_fusion.2 = bf16[2048,2048]{1,0:T(8,128)(2,1)} fusion(f32[2048,704]{0,1:T(8,128)S(1)} %fusion.6, bf16[2,352,2048]{2,1,0:T(8,128)(2,1)S(1)} %copy-done.35), kind=kOutput, calls=%fused_computation.5 | convolution fusion | flops 2961309696 | bytes 15597568 | tf_op jit(solution)/shard_map/dot_general | solution.py:100
  214.5 26.9 %all-to-all-done.2 = bf16[32,64,2048]{2,1,0:T(8,128)(2,1)} async-done(((bf16[32,64,2048]{2,1,0:T(8,128)(2,1)}), bf16[32,64,2048]{2,1,0:T(8,128)(2,1)}, u32[]{:S(2)}, u32[]{:S(2)}) %all-to-all-start.2) | async-done | bytes 8388640 | tf_op jit(solution)/shard_map/all_to_all | solution.py:221
  241.4 9.7 %fusion.10 = f32[2048,704]{0,1:T(8,128)S(1)} fusion(bf16[2048,2048]{1,0:T(8,128)(2,1)} %bitcast.29, bf16[352,2048]{1,0:T(8,128)(2,1)} %get-tuple-element.34, bf16[352,2048]{1,0:T(8,128)(2,1)} %get-tuple-element.52), kind=kOutput, calls=%fused_computation.23 | convolution fusion | flops 5911347200 | bytes 17039360 | tf_op jit(solution)/shard_map/td,fd->tf/dot_general | solution.py:91
  251.1 7.0 %convolution_convert_fusion = bf16[2048,2048]{1,0:T(8,128)(2,1)} fusion(f32[2048,704]{0,1:T(8,128)S(1)} %fusion.10, bf16[2,352,2048]{2,1,0:T(8,128)(2,1)S(1)} %copy-done.36), kind=kOutput, calls=%fused_computation.3 | convolution fusion | flops 2961309696 | bytes 15597568 | tf_op jit(solution)/shard_map/dot_general | solution.py:100
  258.2 5.1 %all-to-all-start.3 = ((bf16[32,64,2048]{2,1,0:T(8,128)(2,1)}), bf16[32,64,2048]{2,1,0:T(8,128)(2,1)}, u32[]{:S(2)}, u32[]{:S(2)}) async-start(bf16[32,64,2048]{2,1,0:T(8,128)(2,1)} %bitcast.130), calls=%async_computation.4 | async-start | bytes 16777216 | tf_op jit(solution)/shard_map/all_to_all | solution.py:239
  263.7 4.1 fusion.14
  267.9 2.7 convolution_convert_fusion.3
  270.6 98.6 %all-to-all-done.3 = bf16[32,64,2048]{2,1,0:T(8,128)(2,1)} async-done(((bf16[32,64,2048]{2,1,0:T(8,128)(2,1)}), bf16[32,64,2048]{2,1,0:T(8,128)(2,1)}, u32[]{:S(2)}, u32[]{:S(2)}) %all-to-all-start.3) | async-done | bytes 8388640 | tf_op jit(solution)/shard_map/all_to_all | solution.py:239
  369.2 9.6 %fusion.1 = bf16[512,2048]{1,0:T(8,128)(2,1)} fusion(bf16[512,2048]{1,0:T(8,128)(2,1)} %convolution_convert_fusion.3, bf16[32,64,2048]{2,1,0:T(8,128)(2,1)} %all-to-all-done.3, bf16[512,32]{0,1:T(8,128)(2,1)S(1)} %select_reduce_fusion, s32[512,32]{0,1:T(8,128)S(1)} %copy-done.16, pred[512,32]{0,1:T(8,128)(4,1)S(1)} %copy-done.12), kind=kOutput, calls=%fused_computation.7 | convolution fusion | flops 4301258752 | bytes 12697600 | tf_op jit(solution)/shard_map/dot_general | solution.py:251
  378.8 4.8 %all-to-all-start.1 = ((bf16[32,16,2048]{2,1,0:T(8,128)(2,1)}), bf16[32,16,2048]{2,1,0:T(8,128)(2,1)}, u32[]{:S(2)}, u32[]{:S(2)}) async-start(bf16[32,16,2048]{2,1,0:T(8,128)(2,1)} %bitcast.134), calls=%async_computation.2 | async-start | bytes 4194304 | tf_op jit(solution)/shard_map/all_to_all | solution.py:246
  383.7 21.0 %reduce-scatter.5.cloned.1.call-done = bf16[1,128,2048]{2,1,0:T(8,128)(2,1)} async-done(((bf16[4,128,2048]{2,1,0:T(8,128)(2,1)}), bf16[1,128,2048]{2,1,0:T(8,128)(2,1)}) %reduce-scatter.5.cloned.1.call-update) | async-done | bytes 524304 | tf_op jit(solution)/shard_map/reduce_scatter | solution.py:256
  404.7 9.0 %all-to-all-done.1 = bf16[32,16,2048]{2,1,0:T(8,128)(2,1)} async-done(((bf16[32,16,2048]{2,1,0:T(8,128)(2,1)}), bf16[32,16,2048]{2,1,0:T(8,128)(2,1)}, u32[]{:S(2)}, u32[]{:S(2)}) %all-to-all-start.1) | async-done | bytes 2097184 | tf_op jit(solution)/shard_map/all_to_all | solution.py:246
  413.7 3.0 fusion.22
  (142 shorter events, 14.7 us)
Async XLA Ops:
  6.5 261.3 %copy-start = (bf16[352,2048]{1,0:T(8,128)(2,1)S(1)}, bf16[352,2048]{1,0:T(8,128)(2,1)}, u32[]{:S(2)}) copy-start(bf16[352,2048]{1,0:T(8,128)(2,1)} %param.35) | copy-start | bytes 4325380
  6.5 16.5 %copy-start.4 = (bf16[128,2048]{1,0:T(8,128)(2,1)S(1)}, bf16[128,2048]{1,0:T(8,128)(2,1)}, u32[]{:S(2)}) copy-start(bf16[128,2048]{1,0:T(8,128)(2,1)} %param.21) | copy-start | bytes 1572868
  6.5 16.9 %copy-start.6 = (bf16[2,128,512]{2,1,0:T(8,128)(2,1)S(1)}, bf16[2,128,512]{2,1,0:T(8,128)(2,1)}, u32[]{:S(2)}) copy-start(bf16[2,128,512]{2,1,0:T(8,128)(2,1)} %param.22) | copy-start | bytes 786436
  6.5 17.0 %copy-start.32 = (s32[2,64]{1,0:T(2,128)S(1)}, s32[2,64]{1,0:T(2,128)}, u32[]{:S(2)}) copy-start(s32[2,64]{1,0:T(2,128)} %param.27) | copy-start | bytes 1540
  6.6 53.4 %all-gather.4.cloned.1.call-start = ((), (), s32[]{:S(2)}) async-start(), calls=%async_computation.6 | async-start | bytes 5242880 | tf_op jit(solution)/shard_map/all_gather | solution.py:146
  6.6 18.0 %copy-start.33 = (s32[2,4]{1,0:T(2,128)S(1)}, s32[2,4]{1,0:T(2,128)}, u32[]{:S(2)}) copy-start(s32[2,4]{1,0:T(2,128)} %param.25) | copy-start | bytes 100
  9.1 16.5 %copy-start.31 = (bf16[2048]{0:T(1024)(128)(2,1)S(1)}, bf16[2048]{0:T(1024)(128)(2,1)}, u32[]{:S(2)}) copy-start(bf16[2048]{0:T(1024)(128)(2,1)} %param.29) | copy-start | bytes 12292
  9.1 17.7 %copy-start.34 = (s32[2]{0:T(128)S(1)}, s32[2]{0:T(128)}, u32[]{:S(2)}) copy-start(s32[2]{0:T(128)} %param.26) | copy-start | bytes 28
  9.1 112.8 %all-gather.8.cloned.1.call-start = ((), (), s32[]{:S(2)}) async-start(), calls=%async_computation.9 | async-start | bytes 2621440 | tf_op jit(solution)/shard_map/all_gather | solution.py:173
  23.4 5.3 %copy-start.1 = (bf16[2,64,4,4,128]{4,3,2,1,0:T(4,128)(2,1)}, bf16[2,64,4,4,128]{4,3,2,1,0:T(4,128)(2,1)S(1)}, u32[]{:S(2)}) copy-start(bf16[2,64,4,4,128]{4,3,2,1,0:T(4,128)(2,1)S(1)} %reshape.106) | copy-start | bytes 1572868
  63.0 3.8 copy-start.2
  72.6 4.8 %copy-start.23 = (f32[2048]{0:T(1024)S(1)}, f32[2048]{0:T(1024)}, u32[]{:S(2)}) copy-start(f32[2048]{0:T(1024)} %convert_element_type.118) | copy-start | bytes 24580
  72.7 5.9 %copy-start.25 = (s32[128,6]{0,1:T(8,128)S(1)}, s32[128,6]{0,1:T(8,128)}, u32[]{:S(2)}) copy-start(s32[128,6]{0,1:T(8,128)} %param.36) | copy-start | bytes 9220
  72.7 6.5 %copy-start.19 = (s32[128,6]{0,1:T(8,128)S(1)}, s32[128,6]{0,1:T(8,128)}, u32[]{:S(2)}) copy-start(s32[128,6]{0,1:T(8,128)} %get-tuple-element.43) | copy-start | bytes 9220
  78.5 119.4 %all-gather.6.cloned.1.call-start = ((), (), s32[]{:S(2)}) async-start(), calls=%async_computation.7 | async-start | bytes 10485760 | tf_op jit(solution)/shard_map/all_gather | solution.py:228
  82.3 36.3 %copy-start.7 = (f32[512,12]{0,1:T(8,128)S(1)}, f32[512,12]{0,1:T(8,128)}, u32[]{:S(2)}) copy-start(f32[512,12]{0,1:T(8,128)} %all_gather.12) | copy-start | bytes 73732
  130.4 111.1 %all-to-all-start.2 = ((bf16[32,64,2048]{2,1,0:T(8,128)(2,1)}), bf16[32,64,2048]{2,1,0:T(8,128)(2,1)}, u32[]{:S(2)}, u32[]{:S(2)}) async-start(bf16[32,64,2048]{2,1,0:T(8,128)(2,1)} %bitcast.129), calls=%async_computation.3 | async-start | bytes 16777216 | tf_op jit(solution)/shard_map/all_to_all | solution.py:221
  135.6 243.3 %reduce-scatter.3.cloned.1.call-start = ((), (), s32[]{:S(2)}) async-start(), calls=%async_computation.8 | async-start | bytes 10485760 | tf_op jit(solution)/shard_map/reduce_scatter | solution.py:233
  197.9 9.6 %copy-start.35 = (bf16[2,352,2048]{2,1,0:T(8,128)(2,1)S(1)}, bf16[2,352,2048]{2,1,0:T(8,128)(2,1)}, u32[]{:S(2)}) copy-start(bf16[2,352,2048]{2,1,0:T(8,128)(2,1)} %param.32) | copy-start | bytes 8650756
  241.4 9.7 %copy-start.36 = (bf16[2,352,2048]{2,1,0:T(8,128)(2,1)S(1)}, bf16[2,352,2048]{2,1,0:T(8,128)(2,1)}, u32[]{:S(2)}) copy-start(bf16[2,352,2048]{2,1,0:T(8,128)(2,1)} %param.32) | copy-start | bytes 8650756
  258.2 5.4 %copy-start.8 = (f32[512,12]{0,1:T(8,128)S(1)}, f32[512,12]{0,1:T(8,128)}, u32[]{:S(2)}) copy-start(f32[512,12]{0,1:T(8,128)} %all_gather.12) | copy-start | bytes 73732
  258.2 5.4 %copy-start.22 = (pred[512,6]{0,1:T(8,128)(4,1)S(1)}, pred[512,6]{0,1:T(8,128)(4,1)}, u32[]{:S(2)}) copy-start(pred[512,6]{0,1:T(8,128)(4,1)} %copy-done.21) | copy-start | bytes 9220
  258.2 111.0 %all-to-all-start.3 = ((bf16[32,64,2048]{2,1,0:T(8,128)(2,1)}), bf16[32,64,2048]{2,1,0:T(8,128)(2,1)}, u32[]{:S(2)}, u32[]{:S(2)}) async-start(bf16[32,64,2048]{2,1,0:T(8,128)(2,1)} %bitcast.130), calls=%async_computation.4 | async-start | bytes 16777216 | tf_op jit(solution)/shard_map/all_to_all | solution.py:239
  263.3 141.4 %reduce-scatter.5.cloned.1.call-start = ((), (), s32[]{:S(2)}) async-start(), calls=%async_computation.10 | async-start | bytes 2621440 | tf_op jit(solution)/shard_map/reduce_scatter | solution.py:256
  267.9 101.3 %copy-start.12 = (pred[512,32]{0,1:T(8,128)(4,1)S(1)}, pred[512,32]{0,1:T(8,128)(4,1)}, u32[]{:S(2)}) copy-start(pred[512,32]{0,1:T(8,128)(4,1)} %copy-done.11) | copy-start | bytes 49156
  267.9 101.3 %copy-start.16 = (s32[512,32]{0,1:T(8,128)S(1)}, s32[512,32]{0,1:T(8,128)}, u32[]{:S(2)}) copy-start(s32[512,32]{0,1:T(8,128)} %copy-done.15) | copy-start | bytes 196612
  378.7 4.9 %copy-start.20 = (s32[128,6]{0,1:T(8,128)S(1)}, s32[128,6]{0,1:T(8,128)}, u32[]{:S(2)}) copy-start(s32[128,6]{0,1:T(8,128)} %get-tuple-element.43) | copy-start | bytes 9220
  378.7 4.9 %copy-start.27 = (f32[128,6]{0,1:T(8,128)S(1)}, f32[128,6]{0,1:T(8,128)}, u32[]{:S(2)}) copy-start(f32[128,6]{0,1:T(8,128)} %param.37) | copy-start | bytes 9220
  378.8 4.9 %copy-start.30 = (pred[128,6]{0,1:T(8,128)(4,1)S(1)}, pred[128,6]{0,1:T(8,128)(4,1)}, u32[]{:S(2)}) copy-start(pred[128,6]{0,1:T(8,128)(4,1)} %copy-done.29) | copy-start | bytes 2308
  378.8 34.9 %copy-start.14 = (s32[128,32]{0,1:T(8,128)S(1)}, s32[128,32]{0,1:T(8,128)}, u32[]{:S(2)}) copy-start(s32[128,32]{0,1:T(8,128)} %copy-done.13) | copy-start | bytes 49156
  378.8 34.9 %copy-start.18 = (pred[128,32]{0,1:T(8,128)(4,1)S(1)}, pred[128,32]{0,1:T(8,128)(4,1)}, u32[]{:S(2)}) copy-start(pred[128,32]{0,1:T(8,128)(4,1)} %copy-done.17) | copy-start | bytes 12292
  378.8 34.9 %all-to-all-start.1 = ((bf16[32,16,2048]{2,1,0:T(8,128)(2,1)}), bf16[32,16,2048]{2,1,0:T(8,128)(2,1)}, u32[]{:S(2)}, u32[]{:S(2)}) async-start(bf16[32,16,2048]{2,1,0:T(8,128)(2,1)} %bitcast.134), calls=%async_computation.2 | async-start | bytes 4194304 | tf_op jit(solution)/shard_map/all_to_all | solution.py:246
  (13 other events, 18.6 us)
Sparse Core Ops, SparseCore 0:
  9.2 50.6 all-gather.3
  78.6 31.1 all-gather.7
  118.0 79.8 all-gather.5
  214.6 81.4 reduce-scatter.2
  378.9 25.6 reduce-scatter.4
